TPU v7x, 512 devices: a whole 4x4x16 slice. The times are simulated.
512 devices in a mesh: tile: 128 (over x, z, core), epoch: 4 (over y).
Axes of the slice: x: 4, y: 4, z: 16, core: 2. Of those that a mesh axis runs over, the one named last changes fastest.
Arguments:
- psi: float32 [48, 4096, 512], P('epoch', 'tile'), may hold values from -6 to 6
- phi: float32 [48, 4096, 512], P('epoch', 'tile'), may hold values from 0.5 to 4
- shifts: int32 [8, 48, 2], replicated, may hold values from -16 to 16, as said below
Outputs:
- best_likelihood: float32 [4096, 512], P('tile', 'epoch')
Inputs may be any that keep to these rules, and one draw needn't show every extreme that they name: shifts[v, e, :] = floor(r_v * t_e / 64) for integer rates r_v of -16 to 16 per component and integer times t_e of 0 to 64; the first epoch has time 0 and the last 64; both extremes are reached.
All inputs are finite; a program needn't handle non-finite values.
Results may differ from a plain program's by a relative error of at most 0.0003.
Values sent between devices are 32-bit elements; how exact they have to be, the bound alone decides.
No kernel may reach another device: no remote copies, remote signals or barrier semaphores. Data moves between devices by JAX's collectives and lax.ppermute only.
A program may use at most 64 MiB of HBM per device.

v0:
```python
import jax
import jax.numpy as jnp
from jax import lax
from jax.sharding import PartitionSpec as P

HALO = 16


def padded_2(block, sides, width):
    for axis, dim in sides:
        count = lax.axis_size(axis)
        forward = [(i, i + 1) for i in range(count - 1)]
        backward = [(target, source) for source, target in forward]
        low = lax.ppermute(
            lax.slice_in_dim(block, block.shape[dim] - width, None, axis=dim), axis, forward
        )
        high = lax.ppermute(lax.slice_in_dim(block, 0, width, axis=dim), axis, backward)
        block = jnp.concatenate([low, block, high], axis=dim)
    return block


def make_windows(images, cols):
    width = min(128, cols)
    count = cols // width
    pieces = [images[..., j * width : j * width + width + 2 * HALO] for j in range(count)]
    return jnp.stack(pieces, axis=3)


def stack_epochs(windows, offsets, rows, cols):
    span = windows.shape[2]
    reach = windows.shape[4]
    width = reach - 2 * HALO
    row_target = (
        jnp.arange(rows, dtype=jnp.int32)[None, :, None] + HALO + offsets[:, 0][:, None, None]
    )
    row_select = (jnp.arange(span, dtype=jnp.int32)[None, None, :] == row_target).astype(
        jnp.float32
    )
    col_target = (
        jnp.arange(width, dtype=jnp.int32)[None, None, :] + HALO + offsets[:, 1][:, None, None]
    )
    col_select = (jnp.arange(reach, dtype=jnp.int32)[None, :, None] == col_target).astype(
        jnp.float32
    )
    moved = jnp.einsum("eyr,ekrjc->ekyjc", row_select, windows, precision=lax.Precision.HIGHEST)
    summed = jnp.einsum("ekyjc,ecx->kyjx", moved, col_select, precision=lax.Precision.HIGHEST)
    return summed.reshape(2, rows, cols)


def per_device(psi, phi, shifts):
    epochs = psi.shape[0]
    rows = psi.shape[1]
    cols = psi.shape[2]
    stacked = jnp.stack([psi, phi])
    padded = padded_2(stacked, (("tile", 2),), HALO)
    padded = jnp.pad(padded, ((0, 0), (0, 0), (0, 0), (HALO, HALO)))
    images = jnp.moveaxis(padded, 1, 0)
    windows = make_windows(images, cols)
    first = lax.axis_index("epoch") * epochs
    own_shifts = lax.dynamic_slice_in_dim(shifts, first, epochs, 1)
    partial_stacks = lax.map(lambda offsets: stack_epochs(windows, offsets, rows, cols), own_shifts)
    summed = lax.psum_scatter(partial_stacks, "epoch", scatter_dimension=3, tiled=True)
    ratio = summed[:, 0] / jnp.sqrt(summed[:, 1])
    return jnp.max(ratio, axis=0)


def solution(mesh):
    placed = (P("epoch", "tile", None), P("epoch", "tile", None), P())
    return jax.shard_map(
        per_device, mesh=mesh, in_specs=placed, out_specs=P("tile", "epoch"), check_vma=False
    )
```

profile of v0, /device:TPU:6, one launch (start us, length us, event | category | flops | bytes accessed | tf_op | source)
XLA Modules:
  0.0 156.6 jit_solution(9901653709663802275)
XLA Ops:
  6.5 1.5 fusion.15
  8.0 1.9 %collective-permute-start = (f32[2,12,16,512]{3,2,0,1:T(8,128)S(1)}, f32[2,12,16,512]{3,2,0,1:T(8,128)S(1)}, u32[]{:S(2)}, u32[]{:S(2)}) collective-permute-start(f32[2,12,16,512]{3,2,0,1:T(8,128)S(1)} %get-tuple-element.42), channel_id=1, source_target_pairs={{0,4},{4,8},{8,12},{12,16},{16,20},{20,24},{24,28},{28,32},{32,36}... | collective-permute-start | bytes 2359304 | tf_op jit(solution)/shard_map/ppermute | solution.py:14
  10.0 11.1 %collective-permute-start.1 = (f32[2,12,16,512]{3,2,0,1:T(8,128)S(1)}, f32[2,12,16,512]{3,2,0,1:T(8,128)S(1)}, u32[]{:S(2)}, u32[]{:S(2)}) collective-permute-start(f32[2,12,16,512]{3,2,0,1:T(8,128)S(1)} %get-tuple-element.43), channel_id=1, source_target_pairs={{4,0},{8,4},{12,8},{16,12},{20,16},{24,20},{28,24},{32,28},{36,32}... | collective-permute-start | bytes 2359304 | tf_op jit(solution)/shard_map/ppermute | solution.py:17
  21.2 7.6 %collective-permute-done = f32[2,12,16,512]{3,2,0,1:T(8,128)S(1)} collective-permute-done((f32[2,12,16,512]{3,2,0,1:T(8,128)S(1)}, f32[2,12,16,512]{3,2,0,1:T(8,128)S(1)}, u32[]{:S(2)}, u32[]{:S(2)}) %collective-permute-start) | collective-permute-done | bytes 786464 | tf_op jit(solution)/shard_map/ppermute | solution.py:14
  28.8 1.8 %collective-permute-done.1 = f32[2,12,16,512]{3,2,0,1:T(8,128)S(1)} collective-permute-done((f32[2,12,16,512]{3,2,0,1:T(8,128)S(1)}, f32[2,12,16,512]{3,2,0,1:T(8,128)S(1)}, u32[]{:S(2)}, u32[]{:S(2)}) %collective-permute-start.1) | collective-permute-done | bytes 786464 | tf_op jit(solution)/shard_map/ppermute | solution.py:17
  30.6 3.0 %fusion.13 = f32[12,2,64,544]{3,2,1,0:T(8,128)S(1)} fusion(f32[2,12,16,512]{3,2,0,1:T(8,128)S(1)} %collective-permute-done.1, f32[2,12,16,512]{3,2,0,1:T(8,128)S(1)} %collective-permute-done, f32[1,12,32,512]{3,2,0,1:T(8,128)} %bitcast.51, f32[1,12,32,512]{3,2,0,1:T(8,128)} %bitcast.49), kind=kLoop, calls=%fused_computation.23 | loop fusion | flops 8355840 | bytes 6488064 | tf_op jit(solution)/shard_map/transpose | solution.py:57
  33.6 0.7 slice_bitcast_fusion.4
  34.3 1.6 %copy.10 = f32[12,2,64,1,160]{4,3,2,1,0:T(1,128)S(1)} copy(f32[12,2,64,1,160]{4,2,1,0,3:T(8,128)S(1)} %get-tuple-element.40) | data formatting | bytes 1966080 | tf_op jit(solution)/shard_map/stack | solution.py:26
  35.9 1.6 %copy.8 = f32[12,2,64,1,160]{4,3,2,1,0:T(1,128)S(1)} copy(f32[12,2,64,1,160]{4,2,1,0,3:T(8,128)S(1)} %get-tuple-element.38) | data formatting | bytes 1966080 | tf_op jit(solution)/shard_map/stack | solution.py:26
  37.5 1.6 %copy.9 = f32[12,2,64,1,160]{4,3,2,1,0:T(1,128)S(1)} copy(f32[12,2,64,1,160]{4,2,1,0,3:T(8,128)S(1)} %get-tuple-element.41) | data formatting | bytes 1966080 | tf_op jit(solution)/shard_map/stack | solution.py:26
  39.2 1.2 stack.30
  40.4 8.0 %pad_maximum_fusion = f32[12,2,64,4,160]{4,3,2,1,0:T(4,128)} fusion(f32[12,2,64,1,160]{4,3,2,1,0:T(1,128)S(1)} %stack.30, f32[12,2,64,1,160]{4,3,2,1,0:T(1,128)S(1)} %copy.10, f32[12,2,64,1,160]{4,3,2,1,0:T(1,128)S(1)} %copy.9, f32[12,2,64,1,160]{4,3,2,1,0:T(1,128)S(1)} %copy.8), kind=kLoop, calls=%fused_computation.19 | loop fusion | flops 2949120 | bytes 7864320 | tf_op jit(solution)/shard_map/stack | solution.py:26
  48.4 69.7 %while.10 = (s32[]{:T(128)}, f32[8,2,32,512]{3,2,1,0:T(8,128)}, s32[8,12,2]{1,2,0:T(2,128)S(1)}, f32[12,2,64,4,160]{4,3,2,1,0:T(4,128)}, s32[]{:T(128)}) while((s32[]{:T(128)}, f32[8,2,32,512]{3,2,1,0:T(8,128)}, s32[8,12,2]{1,2,0:T(2,128)S(1)}, f32[12,2,64,4,160]{4,3,2,1,0:T(4,128)}, s32[]{:T(128)}) %tuple.25), condition=%wide.region_1.2_spmd, body=%wide.region_0.1_spmd.sunk | while | flops 1132734464 | bytes 8799521 | solution.py:61
  48.5 6.0 %fusion.28 = f32[12,32,2,4,160]{4,1,0,3,2:T(8,128)S(1)} fusion(f32[12,2,64,4,160]{4,3,2,1,0:T(4,128)} %get-tuple-element.86, s32[12,32]{1,0:T(8,128)S(1)} %broadcast_add_fusion.4), kind=kOutput, calls=%fused_computation.clone.1 | convolution fusion | flops 377511936 | bytes 5899776 | tf_op jit(solution)/shard_map/while/body/eval_jaxpr/eyr,ekrjc->ekyjc/dot_general | solution.py:45
  54.6 1.7 %fusion.29 = f32[2,32,4,128]{3,1,2,0:T(8,128)S(1)} fusion(f32[12,32,2,4,160]{4,1,0,3,2:T(8,128)S(1)} %fusion.28, s32[12,128]{1,0:T(8,128)S(1)} %broadcast_add_fusion.5), kind=kOutput, calls=%fused_computation.4.clone.1 | convolution fusion | flops 755220480 | bytes 2103296 | tf_op jit(solution)/shard_map/while/body/eval_jaxpr/ekyjc,ecx->kyjx/dot_general | solution.py:46
  57.2 6.0 %fusion.28 = f32[12,32,2,4,160]{4,1,0,3,2:T(8,128)S(1)} fusion(f32[12,2,64,4,160]{4,3,2,1,0:T(4,128)} %get-tuple-element.86, s32[12,32]{1,0:T(8,128)S(1)} %broadcast_add_fusion.4), kind=kOutput, calls=%fused_computation.clone.1 | convolution fusion | flops 377511936 | bytes 5899776 | tf_op jit(solution)/shard_map/while/body/eval_jaxpr/eyr,ekrjc->ekyjc/dot_general | solution.py:45
  63.3 1.7 %fusion.29 = f32[2,32,4,128]{3,1,2,0:T(8,128)S(1)} fusion(f32[12,32,2,4,160]{4,1,0,3,2:T(8,128)S(1)} %fusion.28, s32[12,128]{1,0:T(8,128)S(1)} %broadcast_add_fusion.5), kind=kOutput, calls=%fused_computation.4.clone.1 | convolution fusion | flops 755220480 | bytes 2103296 | tf_op jit(solution)/shard_map/while/body/eval_jaxpr/ekyjc,ecx->kyjx/dot_general | solution.py:46
  65.9 6.0 %fusion.28 = f32[12,32,2,4,160]{4,1,0,3,2:T(8,128)S(1)} fusion(f32[12,2,64,4,160]{4,3,2,1,0:T(4,128)} %get-tuple-element.86, s32[12,32]{1,0:T(8,128)S(1)} %broadcast_add_fusion.4), kind=kOutput, calls=%fused_computation.clone.1 | convolution fusion | flops 377511936 | bytes 5899776 | tf_op jit(solution)/shard_map/while/body/eval_jaxpr/eyr,ekrjc->ekyjc/dot_general | solution.py:45
  72.0 1.7 %fusion.29 = f32[2,32,4,128]{3,1,2,0:T(8,128)S(1)} fusion(f32[12,32,2,4,160]{4,1,0,3,2:T(8,128)S(1)} %fusion.28, s32[12,128]{1,0:T(8,128)S(1)} %broadcast_add_fusion.5), kind=kOutput, calls=%fused_computation.4.clone.1 | convolution fusion | flops 755220480 | bytes 2103296 | tf_op jit(solution)/shard_map/while/body/eval_jaxpr/ekyjc,ecx->kyjx/dot_general | solution.py:46
  73.9 0.7 constant_dynamic-update-slice_fusion.2
  74.6 6.0 %fusion.28 = f32[12,32,2,4,160]{4,1,0,3,2:T(8,128)S(1)} fusion(f32[12,2,64,4,160]{4,3,2,1,0:T(4,128)} %get-tuple-element.86, s32[12,32]{1,0:T(8,128)S(1)} %broadcast_add_fusion.4), kind=kOutput, calls=%fused_computation.clone.1 | convolution fusion | flops 377511936 | bytes 5899776 | tf_op jit(solution)/shard_map/while/body/eval_jaxpr/eyr,ekrjc->ekyjc/dot_general | solution.py:45
  80.7 1.7 %fusion.29 = f32[2,32,4,128]{3,1,2,0:T(8,128)S(1)} fusion(f32[12,32,2,4,160]{4,1,0,3,2:T(8,128)S(1)} %fusion.28, s32[12,128]{1,0:T(8,128)S(1)} %broadcast_add_fusion.5), kind=kOutput, calls=%fused_computation.4.clone.1 | convolution fusion | flops 755220480 | bytes 2103296 | tf_op jit(solution)/shard_map/while/body/eval_jaxpr/ekyjc,ecx->kyjx/dot_general | solution.py:46
  83.3 6.0 %fusion.28 = f32[12,32,2,4,160]{4,1,0,3,2:T(8,128)S(1)} fusion(f32[12,2,64,4,160]{4,3,2,1,0:T(4,128)} %get-tuple-element.86, s32[12,32]{1,0:T(8,128)S(1)} %broadcast_add_fusion.4), kind=kOutput, calls=%fused_computation.clone.1 | convolution fusion | flops 377511936 | bytes 5899776 | tf_op jit(solution)/shard_map/while/body/eval_jaxpr/eyr,ekrjc->ekyjc/dot_general | solution.py:45
  89.4 1.7 %fusion.29 = f32[2,32,4,128]{3,1,2,0:T(8,128)S(1)} fusion(f32[12,32,2,4,160]{4,1,0,3,2:T(8,128)S(1)} %fusion.28, s32[12,128]{1,0:T(8,128)S(1)} %broadcast_add_fusion.5), kind=kOutput, calls=%fused_computation.4.clone.1 | convolution fusion | flops 755220480 | bytes 2103296 | tf_op jit(solution)/shard_map/while/body/eval_jaxpr/ekyjc,ecx->kyjx/dot_general | solution.py:46
  92.0 6.0 %fusion.28 = f32[12,32,2,4,160]{4,1,0,3,2:T(8,128)S(1)} fusion(f32[12,2,64,4,160]{4,3,2,1,0:T(4,128)} %get-tuple-element.86, s32[12,32]{1,0:T(8,128)S(1)} %broadcast_add_fusion.4), kind=kOutput, calls=%fused_computation.clone.1 | convolution fusion | flops 377511936 | bytes 5899776 | tf_op jit(solution)/shard_map/while/body/eval_jaxpr/eyr,ekrjc->ekyjc/dot_general | solution.py:45
  98.1 1.7 %fusion.29 = f32[2,32,4,128]{3,1,2,0:T(8,128)S(1)} fusion(f32[12,32,2,4,160]{4,1,0,3,2:T(8,128)S(1)} %fusion.28, s32[12,128]{1,0:T(8,128)S(1)} %broadcast_add_fusion.5), kind=kOutput, calls=%fused_computation.4.clone.1 | convolution fusion | flops 755220480 | bytes 2103296 | tf_op jit(solution)/shard_map/while/body/eval_jaxpr/ekyjc,ecx->kyjx/dot_general | solution.py:46
  100.7 6.0 %fusion.28 = f32[12,32,2,4,160]{4,1,0,3,2:T(8,128)S(1)} fusion(f32[12,2,64,4,160]{4,3,2,1,0:T(4,128)} %get-tuple-element.86, s32[12,32]{1,0:T(8,128)S(1)} %broadcast_add_fusion.4), kind=kOutput, calls=%fused_computation.clone.1 | convolution fusion | flops 377511936 | bytes 5899776 | tf_op jit(solution)/shard_map/while/body/eval_jaxpr/eyr,ekrjc->ekyjc/dot_general | solution.py:45
  106.8 1.7 %fusion.29 = f32[2,32,4,128]{3,1,2,0:T(8,128)S(1)} fusion(f32[12,32,2,4,160]{4,1,0,3,2:T(8,128)S(1)} %fusion.28, s32[12,128]{1,0:T(8,128)S(1)} %broadcast_add_fusion.5), kind=kOutput, calls=%fused_computation.4.clone.1 | convolution fusion | flops 755220480 | bytes 2103296 | tf_op jit(solution)/shard_map/while/body/eval_jaxpr/ekyjc,ecx->kyjx/dot_general | solution.py:46
  109.4 6.0 %fusion.28 = f32[12,32,2,4,160]{4,1,0,3,2:T(8,128)S(1)} fusion(f32[12,2,64,4,160]{4,3,2,1,0:T(4,128)} %get-tuple-element.86, s32[12,32]{1,0:T(8,128)S(1)} %broadcast_add_fusion.4), kind=kOutput, calls=%fused_computation.clone.1 | convolution fusion | flops 377511936 | bytes 5899776 | tf_op jit(solution)/shard_map/while/body/eval_jaxpr/eyr,ekrjc->ekyjc/dot_general | solution.py:45
  115.5 1.7 %fusion.29 = f32[2,32,4,128]{3,1,2,0:T(8,128)S(1)} fusion(f32[12,32,2,4,160]{4,1,0,3,2:T(8,128)S(1)} %fusion.28, s32[12,128]{1,0:T(8,128)S(1)} %broadcast_add_fusion.5), kind=kOutput, calls=%fused_computation.4.clone.1 | convolution fusion | flops 755220480 | bytes 2103296 | tf_op jit(solution)/shard_map/while/body/eval_jaxpr/ekyjc,ecx->kyjx/dot_general | solution.py:46
  118.1 30.0 %reduce-scatter.2.cloned.1.call-done = f32[8,2,32,128]{3,2,1,0:T(8,128)} async-done(((f32[8,2,32,512]{3,2,1,0:T(8,128)}), f32[8,2,32,128]{3,2,1,0:T(8,128)}) %reduce-scatter.2.cloned.1.call-update) | async-done | bytes 262160 | tf_op jit(solution)/shard_map/reduce_scatter | solution.py:62
  148.1 1.6 %fusion.17 = f32[32,128]{1,0:T(8,128)} fusion(f32[8,2,32,128]{3,2,1,0:T(8,128)} %reduce-scatter.2.cloned.1.call-done), kind=kLoop, calls=%fused_computation.36 | loop fusion | flops 61440 | bytes 278528 | tf_op jit(solution)/shard_map/reduce_max | solution.py:64
  (77 shorter events, 7.2 us)
Async XLA Ops:
  6.5 14.6 %copy-start = (s32[8,48,2]{1,2,0:T(2,128)S(1)}, s32[8,48,2]{1,2,0:T(2,128)}, u32[]{:S(2)}) copy-start(s32[8,48,2]{1,2,0:T(2,128)} %param.7) | copy-start | bytes 9220
  6.5 141.6 %reduce-scatter.2.cloned.1.call-start = ((), (), s32[]{:S(2)}) async-start(), calls=%async_computation.1 | async-start | bytes 1310720 | tf_op jit(solution)/shard_map/reduce_scatter | solution.py:62
  8.0 20.8 %collective-permute-start = (f32[2,12,16,512]{3,2,0,1:T(8,128)S(1)}, f32[2,12,16,512]{3,2,0,1:T(8,128)S(1)}, u32[]{:S(2)}, u32[]{:S(2)}) collective-permute-start(f32[2,12,16,512]{3,2,0,1:T(8,128)S(1)} %get-tuple-element.42), channel_id=1, source_target_pairs={{0,4},{4,8},{8,12},{12,16},{16,20},{20,24},{24,28},{28,32},{32,36}... | collective-permute-start | bytes 2359304 | tf_op jit(solution)/shard_map/ppermute | solution.py:14
  10.0 20.6 %collective-permute-start.1 = (f32[2,12,16,512]{3,2,0,1:T(8,128)S(1)}, f32[2,12,16,512]{3,2,0,1:T(8,128)S(1)}, u32[]{:S(2)}, u32[]{:S(2)}) collective-permute-start(f32[2,12,16,512]{3,2,0,1:T(8,128)S(1)} %get-tuple-element.43), channel_id=1, source_target_pairs={{4,0},{8,4},{12,8},{16,12},{20,16},{24,20},{28,24},{32,28},{36,32}... | collective-permute-start | bytes 2359304 | tf_op jit(solution)/shard_map/ppermute | solution.py:17
Sparse Core Ops, SparseCore 0:
  118.2 29.8 reduce-scatter.1
where the time goes:
time: 157 us
  matrix products  61.6 us (39%)
  waiting for transfers between devices  39.4 us (25%)
  other arithmetic  15.3 us (10%)
  between operations  13.5 us (9%)
  local copies, waits for them, and re-layouts  13.4 us (9%)
  starting transfers between devices  13 us (8%)
    dot_general x8, matrix products, stack_epochs(): jnp.einsum('eyr,ekrjc->ekyjc', row_select, windows, precision=lax.Precisi...  48 us
    reduce_scatter x1, waiting for transfers between devices, per_device(): lax.psum_scatter(partial_stacks, 'epoch', scatter_dimension=3, tiled=True)  30 us
    dot_general x8, matrix products, stack_epochs(): jnp.einsum('ekyjc,ecx->kyjx', moved, col_select, precision=lax.Precision....  13.6 us
    ppermute x1, starting transfers between devices, padded_2(): lax.ppermute(lax.slice_in_dim(block, 0, width, axis=dim), axis, backward)  11.1 us
    another operation x1, other arithmetic, make_windows(): return jnp.stack(pieces, axis=3)  8.03 us
    ppermute x1, waiting for transfers between devices, padded_2(): lax.ppermute(lax.slice_in_dim(block, block.shape[dim] - width, None, axis...  7.63 us
    another operation x5, local copies, waits for them, and re-layouts, make_windows(): return jnp.stack(pieces, axis=3)  6.75 us
    dynamic_update_slice x8, local copies, waits for them, and re-layouts, per_device(): lax.map(lambda offsets: stack_epochs(windows, offsets, rows, cols), own_s...  5.35 us
  transfers between devices with their start and end apart: 3, of which 3 were waited for; matrix products, arithmetic and copies ran while one was open for 0% of the time, Pallas kernels for 0%

commit v1 on v0

v1 whole, which is shorter than its diff:
```python
import jax
import jax.numpy as jnp
from jax import lax
from jax.experimental import pallas as pl
from jax.experimental.pallas import tpu as pltpu
from jax.sharding import PartitionSpec as P

HALO = 16
LANES = 128
CHUNK = 8


def stack_kernel(sh_ref, x_ref, lo_ref, hi_ref, out_ref, pad_ref):
    epochs, rows, slots, lanes = x_ref.shape
    blocks = slots // 2
    vels = out_ref.shape[0]

    pad_ref[:, :HALO] = lo_ref[...]
    pad_ref[:, HALO : HALO + rows] = x_ref[...]
    pad_ref[:, HALO + rows :] = hi_ref[...]

    lane = lax.broadcasted_iota(jnp.int32, (slots, lanes), 1)
    block = lax.broadcasted_iota(jnp.int32, (slots, lanes), 0) % blocks
    for v in range(vels):

        def per_chunk(rc, carry, v=v):
            row0 = rc * CHUNK

            def body(e, acc):
                at = (v * epochs + e) * 2
                s_r = sh_ref[at]
                s_c = sh_ref[at + 1]
                win = pad_ref[e, pl.ds(row0 + HALO + s_r, CHUNK)]
                rolled = pltpu.roll(win, lax.rem(lanes - s_c, lanes), axis=2)
                later = pltpu.roll(rolled, slots - 1, axis=1)
                earlier = pltpu.roll(rolled, 1, axis=1)
                moved = lane + s_c
                inside = (moved >= 0) & (moved < lanes)
                forward = (jnp.zeros((slots, lanes), jnp.int32) + s_c) >= 0
                edge = jnp.where(s_c >= 0, blocks - 1, 0)
                edge_ok = (block != edge) & ~inside
                other = jnp.where(forward[None], later, earlier)
                picked = jnp.where(inside[None], rolled, jnp.where(edge_ok[None], other, 0.0))
                return acc + picked

            init = jnp.zeros((CHUNK, slots, lanes), jnp.float32)
            acc = lax.fori_loop(0, epochs, body, init, unroll=True)
            out_ref[v, pl.ds(row0, CHUNK)] = acc
            return carry

        lax.fori_loop(0, rows // CHUNK, per_chunk, 0)


def partial_stacks(own_shifts, x, lo, hi):
    epochs, rows, slots, lanes = x.shape
    vels = own_shifts.shape[0]
    vmem = pl.BlockSpec(memory_space=pltpu.VMEM)
    return pl.pallas_call(
        stack_kernel,
        out_shape=jax.ShapeDtypeStruct((vels, rows, slots, lanes), jnp.float32),
        in_specs=[pl.BlockSpec(memory_space=pltpu.SMEM)] + [vmem] * 3,
        out_specs=vmem,
        scratch_shapes=[pltpu.VMEM((epochs, rows + 2 * HALO, slots, lanes), jnp.float32)],
        cost_estimate=pl.CostEstimate(
            flops=2 * vels * epochs * rows * slots * lanes,
            bytes_accessed=4 * (epochs * (rows + 2 * HALO) + vels * rows) * slots * lanes,
            transcendentals=0,
        ),
    )(own_shifts.reshape(-1), x, lo, hi)


def per_device(psi, phi, shifts):
    epochs, rows, cols = psi.shape
    blocks = cols // LANES
    stacked = jnp.stack([psi, phi]).reshape(2, epochs, rows, blocks, LANES)
    x = stacked.transpose(1, 2, 0, 3, 4).reshape(epochs, rows, 2 * blocks, LANES)
    count = lax.axis_size("tile")
    forward = [(i, i + 1) for i in range(count - 1)]
    backward = [(i + 1, i) for i in range(count - 1)]
    lo = lax.ppermute(x[:, rows - HALO :], "tile", forward)
    hi = lax.ppermute(x[:, :HALO], "tile", backward)
    first = lax.axis_index("epoch") * epochs
    own_shifts = lax.dynamic_slice_in_dim(shifts, first, epochs, 1)
    part = partial_stacks(own_shifts, x, lo, hi)
    vels = part.shape[0]
    part = part.reshape(vels, rows, 2, blocks, LANES).transpose(3, 0, 2, 1, 4)
    summed = lax.psum_scatter(part, "epoch", scatter_dimension=0, tiled=True)
    groups = summed.shape[0]
    summed = jnp.moveaxis(summed, 0, 3).reshape(vels, 2, rows, groups * LANES)
    ratio = summed[:, 0] / jnp.sqrt(summed[:, 1])
    return jnp.max(ratio, axis=0)


def solution(mesh):
    placed = (P("epoch", "tile", None), P("epoch", "tile", None), P())
    return jax.shard_map(
        per_device, mesh=mesh, in_specs=placed, out_specs=P("tile", "epoch"), check_vma=False
    )
```

time: 157 us -> 82.8 us (0.53)
  matrix products: 61.6 us -> 0 us
  other arithmetic: 15.3 us -> 1.97 us
  Pallas kernels: 0 us -> 8.65 us
  local copies, waits for them, and re-layouts: 13.4 us -> 7.1 us
    dot_general x16 -> x0, matrix products: 61.6 us -> none  [the longest x8 48 us: stack_epochs(): jnp.einsum('eyr,ekrjc->ekyjc', row_select, windows, precision=lax.Precisi...]
    another operation x2 -> x1, other arithmetic: 9.53 us -> 0.36 us  [per_device(): stacked = jnp.stack([psi, phi]).reshape(2, epochs, rows, blocks, LANES)]
    pallas_call x0 -> x1, Pallas kernels: none -> 8.65 us  [partial_stacks(): pl.pallas_call(stack_kernel, out_shape=jax.ShapeDtypeStruct((vels, rows,...]
    dynamic_update_slice x8 -> x0, local copies, waits for them, and re-layouts: 5.35 us -> none  [per_device(): lax.map(lambda offsets: stack_epochs(windows, offsets, rows, cols), own_s...]
    another operation x5 -> x2, local copies, waits for them, and re-layouts: 6.75 us -> 1.73 us  [per_device(): stacked = jnp.stack([psi, phi]).reshape(2, epochs, rows, blocks, LANES)]
    reduce_scatter x1, waiting for transfers between devices: 30 us -> 25.7 us  [per_device(): summed = lax.psum_scatter(part, 'epoch', scatter_dimension=0, tiled=True)]
    ppermute x2, waiting for transfers between devices: 9.38 us -> 12.5 us  [the longest x1 6.62 us: per_device(): hi = lax.ppermute(x[:, :HALO], 'tile', backward)]
    reshape x0 -> x2, local copies, waits for them, and re-layouts: none -> 3.11 us  [the longest x1 2.4 us: per_device(): part = part.reshape(vels, rows, 2, blocks, LANES).transpose(3, 0, 2, 1, 4)]
  transfers between devices with their start and end apart: 3 -> 3, of which waited for: 3 -> 3; matrix products, arithmetic and copies ran while one was open for 0% -> 1% of each run, Pallas kernels for 0% -> 0%
where the time goes in v1:
time: 82.8 us; the launch traced here: 82.5 us
  waiting for transfers between devices  38.3 us (46%)
  between operations  13.5 us (16%)
  starting transfers between devices  13 us (16%)
  Pallas kernels  8.65 us (10%)
  local copies, waits for them, and re-layouts  7.1 us (9%)
  other arithmetic  1.97 us (2%)
    reduce_scatter x1, waiting for transfers between devices, per_device(): summed = lax.psum_scatter(part, 'epoch', scatter_dimension=0, tiled=True)  25.7 us
    ppermute x1, starting transfers between devices, per_device(): hi = lax.ppermute(x[:, :HALO], 'tile', backward)  11.1 us
    pallas_call x1, Pallas kernels, partial_stacks(): pl.pallas_call(stack_kernel, out_shape=jax.ShapeDtypeStruct((vels, rows,...  8.65 us
    ppermute x1, waiting for transfers between devices, per_device(): hi = lax.ppermute(x[:, :HALO], 'tile', backward)  6.62 us
    ppermute x1, waiting for transfers between devices, per_device(): lo = lax.ppermute(x[:, rows - HALO:], 'tile', forward)  5.93 us
    reshape x1, local copies, waits for them, and re-layouts, per_device(): part = part.reshape(vels, rows, 2, blocks, LANES).transpose(3, 0, 2, 1, 4)  2.4 us
    ppermute x1, starting transfers between devices, per_device(): lo = lax.ppermute(x[:, rows - HALO:], 'tile', forward)  1.92 us
    unnamed x10, local copies, waits for them, and re-layouts  1.89 us
  transfers between devices with their start and end apart: 3, of which 3 were waited for; matrix products, arithmetic and copies ran while one was open for 1% of the time, Pallas kernels for 0%

profile of v1, /device:TPU:6, one launch (start us, length us, event | category | flops | bytes accessed | tf_op | source)
XLA Modules:
  0.0 82.5 jit_solution(11723018115148054583)
XLA Ops:
  6.5 0.0 copy-start
  6.5 0.0 copy-start.4
  6.5 0.0 reduce-scatter.2.cloned.1.call-start
  6.5 1.5 %stack.9 = f32[1,12,32,4,128]{4,3,2,1,0:T(4,128)S(1)} reshape(f32[12,32,512]{2,1,0:T(8,128)} %param.3) | data formatting | bytes 1572864 | tf_op jit(solution)/shard_map/stack | solution.py:75
  8.0 0.0 copy-done.4
  8.0 0.3 stack.10
  8.3 0.4 pad_maximum_fusion
  8.7 0.0 copy-start.1
  8.7 0.1 fusion.2
  8.8 1.0 %copy-done.1 = f32[2,12,32,4,128]{4,3,0,2,1:T(4,128)} copy-done((f32[2,12,32,4,128]{4,3,0,2,1:T(4,128)}, f32[2,12,32,4,128]{4,3,0,2,1:T(4,128)S(1)}, u32[]{:S(2)}) %copy-start.1) | copy-done | bytes 1572888
  9.8 11.1 %collective-permute-start.1 = (f32[12,16,8,128]{3,2,1,0:T(8,128)S(1)}, f32[12,16,8,128]{3,2,1,0:T(8,128)S(1)}, u32[]{:S(2)}, u32[]{:S(2)}) collective-permute-start(f32[12,16,8,128]{3,2,1,0:T(8,128)S(1)} %get-tuple-element.5), channel_id=1, source_target_pairs={{4,0},{8,4},{12,8},{16,12},{20,16},{24,20},{28,24},{32,28},{36,32}... | collective-permute-start | bytes 2359304 | tf_op jit(solution)/shard_map/ppermute | solution.py:81
  20.9 1.9 %collective-permute-start = (f32[12,16,8,128]{3,2,1,0:T(8,128)S(1)}, f32[12,16,8,128]{3,2,1,0:T(8,128)S(1)}, u32[]{:S(2)}, u32[]{:S(2)}) collective-permute-start(f32[12,16,8,128]{3,2,1,0:T(8,128)S(1)} %get-tuple-element.6), channel_id=1, source_target_pairs={{0,4},{4,8},{8,12},{12,16},{16,20},{20,24},{24,28},{28,32},{32,36}... | collective-permute-start | bytes 2359304 | tf_op jit(solution)/shard_map/ppermute | solution.py:80
  22.9 0.0 copy-done
  22.9 0.1 constant_dynamic-slice_fusion
  22.9 0.1 copy.9
  23.1 0.7 reshape.16.sh_ref
  23.8 6.6 %collective-permute-done.1.hi_ref = f32[12,16,8,128]{3,2,1,0:T(8,128)S(1)} collective-permute-done((f32[12,16,8,128]{3,2,1,0:T(8,128)S(1)}, f32[12,16,8,128]{3,2,1,0:T(8,128)S(1)}, u32[]{:S(2)}, u32[]{:S(2)}) %collective-permute-start.1) | collective-permute-done | bytes 786464 | tf_op jit(solution)/shard_map/ppermute | solution.py:81
  30.4 0.0 copy-start.2
  30.4 5.9 %collective-permute-done.lo_ref = f32[12,16,8,128]{3,2,1,0:T(8,128)S(1)} collective-permute-done((f32[12,16,8,128]{3,2,1,0:T(8,128)S(1)}, f32[12,16,8,128]{3,2,1,0:T(8,128)S(1)}, u32[]{:S(2)}, u32[]{:S(2)}) %collective-permute-start) | collective-permute-done | bytes 786464 | tf_op jit(solution)/shard_map/ppermute | solution.py:80
  36.3 0.0 copy-done.2
  36.4 0.0 copy-start.3
  36.4 0.9 %copy-done.3 = f32[12,16,8,128]{3,2,1,0:T(8,128)} copy-done((f32[12,16,8,128]{3,2,1,0:T(8,128)}, f32[12,16,8,128]{3,2,1,0:T(8,128)S(1)}, u32[]{:S(2)}) %copy-start.3) | copy-done | bytes 786456
  37.2 8.6 %shard_map.37 = f32[8,32,8,128]{3,2,1,0:T(8,128)} custom-call(s32[192]{0:T(256)} %reshape.16.sh_ref, f32[12,32,8,128]{3,2,1,0:T(8,128)} %bitcast.11, f32[12,16,8,128]{3,2,1,0:T(8,128)} %copy-done.3, f32[12,16,8,128]{3,2,1,0:T(8,128)} %copy-done.2), custom_call_target="tpu_custom_call" | custom-call | flops 6291456 | bytes 4194304 | tf_op jit(solution)/shard_map/pallas_call | solution.py:58
  45.9 2.4 %copy.14 = f32[8,32,2,4,128]{4,1,2,0,3:T(8,128)} copy(f32[8,32,2,4,128]{4,3,2,1,0:T(4,128)} %bitcast.12) | data formatting | bytes 2097152 | tf_op jit(solution)/shard_map/reshape | solution.py:86
  48.3 0.0 reduce-scatter.2.cloned.1.call-update
  48.3 25.7 %reduce-scatter.2.cloned.1.call-done = f32[1,8,2,32,128]{4,3,2,1,0:T(8,128)} async-done(((f32[4,8,2,32,128]{4,3,2,1,0:T(8,128)}), f32[1,8,2,32,128]{4,3,2,1,0:T(8,128)}) %reduce-scatter.2.cloned.1.call-update) | async-done | bytes 262160 | tf_op jit(solution)/shard_map/reduce_scatter | solution.py:87
  74.0 1.6 %fusion.1 = f32[32,128]{1,0:T(8,128)} fusion(f32[8,2,32,128]{3,2,1,0:T(8,128)} %bitcast.16), kind=kLoop, calls=%fused_computation.4 | loop fusion | flops 61440 | bytes 278528 | tf_op jit(solution)/shard_map/reduce_max | solution.py:91
Async XLA Ops:
  6.5 16.3 %copy-start = (s32[8,48,2]{1,2,0:T(2,128)S(1)}, s32[8,48,2]{1,2,0:T(2,128)}, u32[]{:S(2)}) copy-start(s32[8,48,2]{1,2,0:T(2,128)} %param.5) | copy-start | bytes 9220
  6.5 1.5 %copy-start.4 = (f32[12,32,512]{2,1,0:T(8,128)S(1)}, f32[12,32,512]{2,1,0:T(8,128)}, u32[]{:S(2)}) copy-start(f32[12,32,512]{2,1,0:T(8,128)} %param.4) | copy-start | bytes 2359300
  6.5 67.5 %reduce-scatter.2.cloned.1.call-start = ((), (), s32[]{:S(2)}) async-start(), calls=%async_computation.1 | async-start | bytes 1310720 | tf_op jit(solution)/shard_map/reduce_scatter | solution.py:87
  8.7 1.2 %copy-start.1 = (f32[2,12,32,4,128]{4,3,0,2,1:T(4,128)}, f32[2,12,32,4,128]{4,3,0,2,1:T(4,128)S(1)}, u32[]{:S(2)}) copy-start(f32[2,12,32,4,128]{4,3,0,2,1:T(4,128)S(1)} %pad_maximum_fusion) | copy-start | bytes 4718596
  9.8 20.6 %collective-permute-start.1 = (f32[12,16,8,128]{3,2,1,0:T(8,128)S(1)}, f32[12,16,8,128]{3,2,1,0:T(8,128)S(1)}, u32[]{:S(2)}, u32[]{:S(2)}) collective-permute-start(f32[12,16,8,128]{3,2,1,0:T(8,128)S(1)} %get-tuple-element.5), channel_id=1, source_target_pairs={{4,0},{8,4},{12,8},{16,12},{20,16},{24,20},{28,24},{32,28},{36,32}... | collective-permute-start | bytes 2359304 | tf_op jit(solution)/shard_map/ppermute | solution.py:81
  20.9 15.4 %collective-permute-start = (f32[12,16,8,128]{3,2,1,0:T(8,128)S(1)}, f32[12,16,8,128]{3,2,1,0:T(8,128)S(1)}, u32[]{:S(2)}, u32[]{:S(2)}) collective-permute-start(f32[12,16,8,128]{3,2,1,0:T(8,128)S(1)} %get-tuple-element.6), channel_id=1, source_target_pairs={{0,4},{4,8},{8,12},{12,16},{16,20},{20,24},{24,28},{28,32},{32,36}... | collective-permute-start | bytes 2359304 | tf_op jit(solution)/shard_map/ppermute | solution.py:80
  30.4 5.9 %copy-start.2 = (f32[12,16,8,128]{3,2,1,0:T(8,128)}, f32[12,16,8,128]{3,2,1,0:T(8,128)S(1)}, u32[]{:S(2)}) copy-start(f32[12,16,8,128]{3,2,1,0:T(8,128)S(1)} %collective-permute-done.1.hi_ref) | copy-start | bytes 2359300
  36.4 0.9 %copy-start.3 = (f32[12,16,8,128]{3,2,1,0:T(8,128)}, f32[12,16,8,128]{3,2,1,0:T(8,128)S(1)}, u32[]{:S(2)}) copy-start(f32[12,16,8,128]{3,2,1,0:T(8,128)S(1)} %collective-permute-done.lo_ref) | copy-start | bytes 2359300
Sparse Core Ops, SparseCore 0:
  48.4 25.5 reduce-scatter.1

commit v2 on v1

--- a/solution.py
+++ b/solution.py
@@ -84,11 +84,29 @@
     part = partial_stacks(own_shifts, x, lo, hi)
     vels = part.shape[0]
     part = part.reshape(vels, rows, 2, blocks, LANES).transpose(3, 0, 2, 1, 4)
-    summed = lax.psum_scatter(part, "epoch", scatter_dimension=0, tiled=True)
-    groups = summed.shape[0]
-    summed = jnp.moveaxis(summed, 0, 3).reshape(vels, 2, rows, groups * LANES)
+    summed = ring_reduce_scatter(part, "epoch")
     ratio = summed[:, 0] / jnp.sqrt(summed[:, 1])
     return jnp.max(ratio, axis=0)
+
+
+def ring_reduce_scatter(part, axis):
+    n = lax.axis_size(axis)
+    g = lax.axis_index(axis)
+    half = part.shape[3] // 2
+    ahead = [(i, (i + 1) % n) for i in range(n)]
+    behind = [(i, (i - 1) % n) for i in range(n)]
+    upper = part[:, :, :, :half]
+    lower = part[:, :, :, half:]
+
+    def pick(x, b):
+        return lax.dynamic_index_in_dim(x, lax.rem(b + 2 * n, n), 0, keepdims=False)
+
+    up = pick(upper, g - 1)
+    down = pick(lower, g + 1)
+    for s in range(1, n):
+        up = lax.ppermute(up, axis, ahead) + pick(upper, g - 1 - s)
+        down = lax.ppermute(down, axis, behind) + pick(lower, g + 1 + s)
+    return jnp.concatenate([up, down], axis=2)
 
 
 def solution(mesh):

time: 82.8 us -> 70.2 us (0.85)
  starting transfers between devices: 13 us -> 34.9 us
  waiting for transfers between devices: 38.3 us -> 17.2 us
  between operations: 13.5 us -> 0.2 us
    reduce_scatter x1 -> x0, waiting for transfers between devices: 25.7 us -> none  [per_device(): summed = lax.psum_scatter(part, 'epoch', scatter_dimension=0, tiled=True)]
    ppermute x0 -> x6, starting transfers between devices: none -> 21.9 us  [the longest x3 16.1 us: ring_reduce_scatter(): down = lax.ppermute(down, axis, behind) + pick(lower, g + 1 + s)]
    ppermute x0 -> x6, waiting for transfers between devices: none -> 8.73 us  [the longest x3 5.74 us: ring_reduce_scatter(): up = lax.ppermute(up, axis, ahead) + pick(upper, g - 1 - s)]
    ppermute x1, waiting for transfers between devices: 6.62 us -> 1.75 us  [per_device(): hi = lax.ppermute(x[:, :HALO], 'tile', backward)]
    reshape x1 -> x0, local copies, waits for them, and re-layouts: 2.4 us -> none  [per_device(): part = part.reshape(vels, rows, 2, blocks, LANES).transpose(3, 0, 2, 1, 4)]
    slice x0 -> x1, local copies, waits for them, and re-layouts: none -> 1.38 us  [ring_reduce_scatter(): upper = part[:, :, :, :half]]
    dynamic_slice x0 -> x1, local copies, waits for them, and re-layouts: none -> 1.15 us  [pick(): return lax.dynamic_index_in_dim(x, lax.rem(b + 2 * n, n), 0, keepdims=False)]
  transfers between devices with their start and end apart: 3 -> 8, of which waited for: 3 -> 7; matrix products, arithmetic and copies ran while one was open for 1% -> 2% of each run, Pallas kernels for 0% -> 0%
where the time goes in v2:
time: 70.2 us; the launch traced here: 69.9 us
  starting transfers between devices  34.9 us (50%)
  waiting for transfers between devices  17.2 us (25%)
  Pallas kernels  8.66 us (12%)
  local copies, waits for them, and re-layouts  7.23 us (10%)
  other arithmetic  1.67 us (2%)
    ppermute x3, starting transfers between devices, ring_reduce_scatter(): down = lax.ppermute(down, axis, behind) + pick(lower, g + 1 + s)  16.1 us
    ppermute x1, starting transfers between devices, per_device(): hi = lax.ppermute(x[:, :HALO], 'tile', backward)  11.1 us
    pallas_call x1, Pallas kernels, partial_stacks(): pl.pallas_call(stack_kernel, out_shape=jax.ShapeDtypeStruct((vels, rows,...  8.66 us
    ppermute x1, waiting for transfers between devices, per_device(): lo = lax.ppermute(x[:, rows - HALO:], 'tile', forward)  6.76 us
    ppermute x3, starting transfers between devices, ring_reduce_scatter(): up = lax.ppermute(up, axis, ahead) + pick(upper, g - 1 - s)  5.76 us
    ppermute x3, waiting for transfers between devices, ring_reduce_scatter(): up = lax.ppermute(up, axis, ahead) + pick(upper, g - 1 - s)  5.74 us
    ppermute x3, waiting for transfers between devices, ring_reduce_scatter(): down = lax.ppermute(down, axis, behind) + pick(lower, g + 1 + s)  2.99 us
    ppermute x1, starting transfers between devices, per_device(): lo = lax.ppermute(x[:, rows - HALO:], 'tile', forward)  1.91 us
  transfers between devices with their start and end apart: 8, of which 7 were waited for; matrix products, arithmetic and copies ran while one was open for 2% of the time, Pallas kernels for 0%

profile of v2, /device:TPU:6, one launch (start us, length us, event | category | flops | bytes accessed | tf_op | source)
XLA Modules:
  0.0 69.9 jit_solution(16492570254320359150)
XLA Ops:
  0.0 1.5 %stack.10 = f32[1,12,32,4,128]{4,3,2,1,0:T(4,128)S(1)} reshape(f32[12,32,512]{2,1,0:T(8,128)} %param.4) | data formatting | bytes 1572864 | tf_op jit(solution)/shard_map/stack | solution.py:75
  1.5 0.3 stack.9
  1.8 0.4 pad_maximum_fusion
  2.1 0.1 fusion.4
  2.3 1.0 %copy-done.1 = f32[2,12,32,4,128]{4,3,0,2,1:T(4,128)} copy-done((f32[2,12,32,4,128]{4,3,0,2,1:T(4,128)}, f32[2,12,32,4,128]{4,3,0,2,1:T(4,128)S(1)}, u32[]{:S(2)}) %copy-start.1) | copy-done | bytes 1572888
  3.3 1.9 %collective-permute-start = (f32[12,16,8,128]{3,2,1,0:T(8,128)S(1)}, f32[12,16,8,128]{3,2,1,0:T(8,128)S(1)}, u32[]{:S(2)}, u32[]{:S(2)}) collective-permute-start(f32[12,16,8,128]{3,2,1,0:T(8,128)S(1)} %get-tuple-element.6), channel_id=1, source_target_pairs={{0,4},{4,8},{8,12},{12,16},{16,20},{20,24},{24,28},{28,32},{32,36}... | collective-permute-start | bytes 2359304 | tf_op jit(solution)/shard_map/ppermute | solution.py:80
  5.2 11.1 %collective-permute-start.1 = (f32[12,16,8,128]{3,2,1,0:T(8,128)S(1)}, f32[12,16,8,128]{3,2,1,0:T(8,128)S(1)}, u32[]{:S(2)}, u32[]{:S(2)}) collective-permute-start(f32[12,16,8,128]{3,2,1,0:T(8,128)S(1)} %get-tuple-element.5), channel_id=1, source_target_pairs={{4,0},{8,4},{12,8},{16,12},{20,16},{24,20},{28,24},{32,28},{36,32}... | collective-permute-start | bytes 2359304 | tf_op jit(solution)/shard_map/ppermute | solution.py:81
  16.4 0.1 constant_dynamic-slice_fusion.8
  16.4 0.1 copy.6
  16.6 0.7 %reshape.16.sh_ref = s32[192]{0:T(256)} reshape(s32[8,12,2]{2,1,0:T(8,128)S(1)} %copy.6) | data formatting | bytes 1536 | tf_op jit(solution)/shard_map/reshape | solution.py:69
  17.3 6.8 %collective-permute-done.lo_ref = f32[12,16,8,128]{3,2,1,0:T(8,128)S(1)} collective-permute-done((f32[12,16,8,128]{3,2,1,0:T(8,128)S(1)}, f32[12,16,8,128]{3,2,1,0:T(8,128)S(1)}, u32[]{:S(2)}, u32[]{:S(2)}) %collective-permute-start) | collective-permute-done | bytes 786464 | tf_op jit(solution)/shard_map/ppermute | solution.py:80
  24.1 1.8 %collective-permute-done.1.hi_ref = f32[12,16,8,128]{3,2,1,0:T(8,128)S(1)} collective-permute-done((f32[12,16,8,128]{3,2,1,0:T(8,128)S(1)}, f32[12,16,8,128]{3,2,1,0:T(8,128)S(1)}, u32[]{:S(2)}, u32[]{:S(2)}) %collective-permute-start.1) | collective-permute-done | bytes 786464 | tf_op jit(solution)/shard_map/ppermute | solution.py:81
  25.8 0.9 %copy-done.3 = f32[12,16,8,128]{3,2,1,0:T(8,128)} copy-done((f32[12,16,8,128]{3,2,1,0:T(8,128)}, f32[12,16,8,128]{3,2,1,0:T(8,128)S(1)}, u32[]{:S(2)}) %copy-start.3) | copy-done | bytes 786456
  26.7 8.7 %shard_map.37 = f32[8,32,8,128]{3,2,1,0:T(8,128)} custom-call(s32[192]{0:T(256)} %reshape.16.sh_ref, f32[12,32,8,128]{3,2,1,0:T(8,128)} %bitcast.17, f32[12,16,8,128]{3,2,1,0:T(8,128)} %copy-done.2, f32[12,16,8,128]{3,2,1,0:T(8,128)} %copy-done.3), custom_call_target="tpu_custom_call" | custom-call | flops 6291456 | bytes 4194304 | tf_op jit(solution)/shard_map/pallas_call | solution.py:58
  35.4 1.4 %fusion.5 = (f32[4,8,2,16,128]{4,0,2,3,1:T(4,128)S(1)}, f32[4,8,2,16,128]{4,0,2,3,1:T(4,128)S(1)}) fusion(f32[4,8,2,32,128]{4,0,2,3,1:T(4,128)} %bitcast.18), kind=kLoop, calls=%fused_computation.18 | loop fusion | bytes 2097152 | tf_op jit(solution)/shard_map/slice | solution.py:98
  36.7 1.2 %constant_dynamic-slice_fusion = (f32[1,8,2,16,128]{4,0,2,3,1:T(1,128)S(1)}, f32[1,8,2,16,128]{4,0,2,3,1:T(1,128)S(1)}, f32[1,8,2,16,128]{4,0,2,3,1:T(1,128)S(1)...) fusion(f32[4,8,2,16,128]{4,0,2,3,1:T(4,128)S(1)} %get-tuple-ele, ...), kind=kLoop, calls=%fused_computation.8 | loop fusion | bytes 2097184 | tf_op jit(solution)/shard_map/jit(dynamic_index_in_dim)/dynamic_slice | solution.py:102
  37.9 4.9 %collective-permute-start.5 = (f32[8,2,16,128]{3,1,2,0:T(2,128)S(1)}, f32[8,2,16,128]{3,1,2,0:T(2,128)S(1)}, u32[]{:S(2)}, u32[]{:S(2)}) collective-permute-start(f32[8,2,16,128]{3,1,2,0:T(2,128)S(1)} %bitcast.28), channel_id=1, source_target_pairs={{0,3},{1,0},{2,1},{3,2},{4,7},{5,4},{6,5},{7,6},{8,11},{9,8},{10,9... | collective-permute-start | bytes 393224 | tf_op jit(solution)/shard_map/ppermute | solution.py:108
  42.8 1.9 %collective-permute-start.2 = (f32[8,2,16,128]{3,1,2,0:T(2,128)S(1)}, f32[8,2,16,128]{3,1,2,0:T(2,128)S(1)}, u32[]{:S(2)}, u32[]{:S(2)}) collective-permute-start(f32[8,2,16,128]{3,1,2,0:T(2,128)S(1)} %bitcast.27), channel_id=1, source_target_pairs={{0,1},{1,2},{2,3},{3,0},{4,5},{5,6},{6,7},{7,4},{8,9},{9,10},{10,1... | collective-permute-start | bytes 393224 | tf_op jit(solution)/shard_map/ppermute | solution.py:107
  44.8 0.9 %collective-permute-done.5 = f32[8,2,16,128]{3,1,2,0:T(2,128)S(1)} collective-permute-done((f32[8,2,16,128]{3,1,2,0:T(2,128)S(1)}, f32[8,2,16,128]{3,1,2,0:T(2,128)S(1)}, u32[]{:S(2)}, u32[]{:S(2)}) %collective-permute-start.5) | collective-permute-done | bytes 131104 | tf_op jit(solution)/shard_map/ppermute | solution.py:108
  45.7 5.6 %collective-permute-start.6 = (f32[8,2,16,128]{3,1,2,0:T(2,128)S(1)}, f32[8,2,16,128]{3,1,2,0:T(2,128)S(1)}, u32[]{:S(2)}, u32[]{:S(2)}) collective-permute-start(f32[8,2,16,128]{3,1,2,0:T(2,128)S(1)} %add.125), channel_id=1, source_target_pairs={{0,3},{1,0},{2,1},{3,2},{4,7},{5,4},{6,5},{7,6},{8,11},{9,8},{10,9... | collective-permute-start | bytes 393224 | tf_op jit(solution)/shard_map/ppermute | solution.py:108
  51.3 0.1 collective-permute-done.2
  51.5 0.1 add.114
  51.5 1.9 %collective-permute-start.3 = (f32[8,2,16,128]{3,1,2,0:T(2,128)S(1)}, f32[8,2,16,128]{3,1,2,0:T(2,128)S(1)}, u32[]{:S(2)}, u32[]{:S(2)}) collective-permute-start(f32[8,2,16,128]{3,1,2,0:T(2,128)S(1)} %add.114), channel_id=1, source_target_pairs={{0,1},{1,2},{2,3},{3,0},{4,5},{5,6},{6,7},{7,4},{8,9},{9,10},{10,1... | collective-permute-start | bytes 393224 | tf_op jit(solution)/shard_map/ppermute | solution.py:107
  53.5 1.6 %collective-permute-done.6 = f32[8,2,16,128]{3,1,2,0:T(2,128)S(1)} collective-permute-done((f32[8,2,16,128]{3,1,2,0:T(2,128)S(1)}, f32[8,2,16,128]{3,1,2,0:T(2,128)S(1)}, u32[]{:S(2)}, u32[]{:S(2)}) %collective-permute-start.6) | collective-permute-done | bytes 131104 | tf_op jit(solution)/shard_map/ppermute | solution.py:108
  55.2 5.6 %collective-permute-start.7 = (f32[8,2,16,128]{3,1,2,0:T(2,128)S(1)}, f32[8,2,16,128]{3,1,2,0:T(2,128)S(1)}, u32[]{:S(2)}, u32[]{:S(2)}) collective-permute-start(f32[8,2,16,128]{3,1,2,0:T(2,128)S(1)} %add.128), channel_id=1, source_target_pairs={{0,3},{1,0},{2,1},{3,2},{4,7},{5,4},{6,5},{7,6},{8,11},{9,8},{10,9... | collective-permute-start | bytes 393224 | tf_op jit(solution)/shard_map/ppermute | solution.py:108
  60.8 0.1 add.117
  60.9 1.9 %collective-permute-start.4 = (f32[8,2,16,128]{3,1,2,0:T(2,128)S(1)}, f32[8,2,16,128]{3,1,2,0:T(2,128)S(1)}, u32[]{:S(2)}, u32[]{:S(2)}) collective-permute-start(f32[8,2,16,128]{3,1,2,0:T(2,128)S(1)} %add.117), channel_id=1, source_target_pairs={{0,1},{1,2},{2,3},{3,0},{4,5},{5,6},{6,7},{7,4},{8,9},{9,10},{10,1... | collective-permute-start | bytes 393224 | tf_op jit(solution)/shard_map/ppermute | solution.py:107
  62.8 0.5 collective-permute-done.7
  63.3 0.1 add.131
  63.4 5.6 %collective-permute-done.4 = f32[8,2,16,128]{3,1,2,0:T(2,128)S(1)} collective-permute-done((f32[8,2,16,128]{3,1,2,0:T(2,128)S(1)}, f32[8,2,16,128]{3,1,2,0:T(2,128)S(1)}, u32[]{:S(2)}, u32[]{:S(2)}) %collective-permute-start.4) | collective-permute-done | bytes 131104 | tf_op jit(solution)/shard_map/ppermute | solution.py:107
  69.0 0.1 add.120
  69.0 0.9 %fusion.3 = f32[32,128]{1,0:T(8,128)} fusion(f32[8,2,16,128]{3,1,2,0:T(2,128)S(1)} %add.131, f32[8,2,16,128]{3,1,2,0:T(2,128)S(1)} %add.120), kind=kLoop, calls=%fused_computation.7 | loop fusion | flops 126976 | bytes 278528 | tf_op jit(solution)/shard_map/reduce_max | solution.py:89
  (11 shorter events, 0.2 us)
Async XLA Ops:
  0.0 16.4 %copy-start = (s32[8,48,2]{1,2,0:T(2,128)S(1)}, s32[8,48,2]{1,2,0:T(2,128)}, u32[]{:S(2)}) copy-start(s32[8,48,2]{1,2,0:T(2,128)} %param.5) | copy-start | bytes 9220
  0.0 1.5 %copy-start.4 = (f32[12,32,512]{2,1,0:T(8,128)S(1)}, f32[12,32,512]{2,1,0:T(8,128)}, u32[]{:S(2)}) copy-start(f32[12,32,512]{2,1,0:T(8,128)} %param.3) | copy-start | bytes 2359300
  2.1 1.2 %copy-start.1 = (f32[2,12,32,4,128]{4,3,0,2,1:T(4,128)}, f32[2,12,32,4,128]{4,3,0,2,1:T(4,128)S(1)}, u32[]{:S(2)}) copy-start(f32[2,12,32,4,128]{4,3,0,2,1:T(4,128)S(1)} %pad_maximum_fusion) | copy-start | bytes 4718596
  3.3 20.8 %collective-permute-start = (f32[12,16,8,128]{3,2,1,0:T(8,128)S(1)}, f32[12,16,8,128]{3,2,1,0:T(8,128)S(1)}, u32[]{:S(2)}, u32[]{:S(2)}) collective-permute-start(f32[12,16,8,128]{3,2,1,0:T(8,128)S(1)} %get-tuple-element.6), channel_id=1, source_target_pairs={{0,4},{4,8},{8,12},{12,16},{16,20},{20,24},{24,28},{28,32},{32,36}... | collective-permute-start | bytes 2359304 | tf_op jit(solution)/shard_map/ppermute | solution.py:80
  5.2 20.6 %collective-permute-start.1 = (f32[12,16,8,128]{3,2,1,0:T(8,128)S(1)}, f32[12,16,8,128]{3,2,1,0:T(8,128)S(1)}, u32[]{:S(2)}, u32[]{:S(2)}) collective-permute-start(f32[12,16,8,128]{3,2,1,0:T(8,128)S(1)} %get-tuple-element.5), channel_id=1, source_target_pairs={{4,0},{8,4},{12,8},{16,12},{20,16},{24,20},{28,24},{32,28},{36,32}... | collective-permute-start | bytes 2359304 | tf_op jit(solution)/shard_map/ppermute | solution.py:81
  24.1 1.8 %copy-start.2 = (f32[12,16,8,128]{3,2,1,0:T(8,128)}, f32[12,16,8,128]{3,2,1,0:T(8,128)S(1)}, u32[]{:S(2)}) copy-start(f32[12,16,8,128]{3,2,1,0:T(8,128)S(1)} %collective-permute-done.lo_ref) | copy-start | bytes 2359300
  25.8 0.9 %copy-start.3 = (f32[12,16,8,128]{3,2,1,0:T(8,128)}, f32[12,16,8,128]{3,2,1,0:T(8,128)S(1)}, u32[]{:S(2)}) copy-start(f32[12,16,8,128]{3,2,1,0:T(8,128)S(1)} %collective-permute-done.1.hi_ref) | copy-start | bytes 2359300
  37.9 7.7 %collective-permute-start.5 = (f32[8,2,16,128]{3,1,2,0:T(2,128)S(1)}, f32[8,2,16,128]{3,1,2,0:T(2,128)S(1)}, u32[]{:S(2)}, u32[]{:S(2)}) collective-permute-start(f32[8,2,16,128]{3,1,2,0:T(2,128)S(1)} %bitcast.28), channel_id=1, source_target_pairs={{0,3},{1,0},{2,1},{3,2},{4,7},{5,4},{6,5},{7,6},{8,11},{9,8},{10,9... | collective-permute-start | bytes 393224 | tf_op jit(solution)/shard_map/ppermute | solution.py:108
  42.8 8.6 %collective-permute-start.2 = (f32[8,2,16,128]{3,1,2,0:T(2,128)S(1)}, f32[8,2,16,128]{3,1,2,0:T(2,128)S(1)}, u32[]{:S(2)}, u32[]{:S(2)}) collective-permute-start(f32[8,2,16,128]{3,1,2,0:T(2,128)S(1)} %bitcast.27), channel_id=1, source_target_pairs={{0,1},{1,2},{2,3},{3,0},{4,5},{5,6},{6,7},{7,4},{8,9},{9,10},{10,1... | collective-permute-start | bytes 393224 | tf_op jit(solution)/shard_map/ppermute | solution.py:107
  45.7 9.4 %collective-permute-start.6 = (f32[8,2,16,128]{3,1,2,0:T(2,128)S(1)}, f32[8,2,16,128]{3,1,2,0:T(2,128)S(1)}, u32[]{:S(2)}, u32[]{:S(2)}) collective-permute-start(f32[8,2,16,128]{3,1,2,0:T(2,128)S(1)} %add.125), channel_id=1, source_target_pairs={{0,3},{1,0},{2,1},{3,2},{4,7},{5,4},{6,5},{7,6},{8,11},{9,8},{10,9... | collective-permute-start | bytes 393224 | tf_op jit(solution)/shard_map/ppermute | solution.py:108
  51.5 9.2 %collective-permute-start.3 = (f32[8,2,16,128]{3,1,2,0:T(2,128)S(1)}, f32[8,2,16,128]{3,1,2,0:T(2,128)S(1)}, u32[]{:S(2)}, u32[]{:S(2)}) collective-permute-start(f32[8,2,16,128]{3,1,2,0:T(2,128)S(1)} %add.114), channel_id=1, source_target_pairs={{0,1},{1,2},{2,3},{3,0},{4,5},{5,6},{6,7},{7,4},{8,9},{9,10},{10,1... | collective-permute-start | bytes 393224 | tf_op jit(solution)/shard_map/ppermute | solution.py:107
  55.2 8.1 %collective-permute-start.7 = (f32[8,2,16,128]{3,1,2,0:T(2,128)S(1)}, f32[8,2,16,128]{3,1,2,0:T(2,128)S(1)}, u32[]{:S(2)}, u32[]{:S(2)}) collective-permute-start(f32[8,2,16,128]{3,1,2,0:T(2,128)S(1)} %add.128), channel_id=1, source_target_pairs={{0,3},{1,0},{2,1},{3,2},{4,7},{5,4},{6,5},{7,6},{8,11},{9,8},{10,9... | collective-permute-start | bytes 393224 | tf_op jit(solution)/shard_map/ppermute | solution.py:108
  60.9 8.1 %collective-permute-start.4 = (f32[8,2,16,128]{3,1,2,0:T(2,128)S(1)}, f32[8,2,16,128]{3,1,2,0:T(2,128)S(1)}, u32[]{:S(2)}, u32[]{:S(2)}) collective-permute-start(f32[8,2,16,128]{3,1,2,0:T(2,128)S(1)} %add.117), channel_id=1, source_target_pairs={{0,1},{1,2},{2,3},{3,0},{4,5},{5,6},{6,7},{7,4},{8,9},{9,10},{10,1... | collective-permute-start | bytes 393224 | tf_op jit(solution)/shard_map/ppermute | solution.py:107

commit v3 on v2

--- a/solution.py
+++ b/solution.py
@@ -84,7 +84,7 @@
     part = partial_stacks(own_shifts, x, lo, hi)
     vels = part.shape[0]
     part = part.reshape(vels, rows, 2, blocks, LANES).transpose(3, 0, 2, 1, 4)
-    summed = ring_reduce_scatter(part, "epoch")
+    summed = jnp.sum(lax.all_to_all(part, "epoch", 0, 0, tiled=True), axis=0)
     ratio = summed[:, 0] / jnp.sqrt(summed[:, 1])
     return jnp.max(ratio, axis=0)
 

time: 70.2 us -> 58 us (0.83)
  starting transfers between devices: 34.9 us -> 13 us
  blocking collectives: 0 us -> 15.2 us
  waiting for transfers between devices: 17.2 us -> 12.5 us
  local copies, waits for them, and re-layouts: 7.23 us -> 6.47 us
    ppermute x6 -> x0, starting transfers between devices: 21.9 us -> none  [the longest x3 16.1 us: ring_reduce_scatter(): down = lax.ppermute(down, axis, behind) + pick(lower, g + 1 + s)]
    all_to_all x0 -> x1, blocking collectives: none -> 15.2 us  [per_device(): summed = jnp.sum(lax.all_to_all(part, 'epoch', 0, 0, tiled=True), axis=0)]
    ppermute x6 -> x0, waiting for transfers between devices: 8.73 us -> none  [the longest x3 5.74 us: ring_reduce_scatter(): up = lax.ppermute(up, axis, ahead) + pick(upper, g - 1 - s)]
    ppermute x1, waiting for transfers between devices: 1.75 us -> 6.62 us  [per_device(): hi = lax.ppermute(x[:, :HALO], 'tile', backward)]
    reshape x0 -> x1, local copies, waits for them, and re-layouts: none -> 1.76 us  [per_device(): part = part.reshape(vels, rows, 2, blocks, LANES).transpose(3, 0, 2, 1, 4)]
    slice x1 -> x0, local copies, waits for them, and re-layouts: 1.38 us -> none  [ring_reduce_scatter(): upper = part[:, :, :, :half]]
    dynamic_slice x1 -> x0, local copies, waits for them, and re-layouts: 1.15 us -> none  [pick(): return lax.dynamic_index_in_dim(x, lax.rem(b + 2 * n, n), 0, keepdims=False)]
    ppermute x1, waiting for transfers between devices: 6.76 us -> 5.93 us  [per_device(): lo = lax.ppermute(x[:, rows - HALO:], 'tile', forward)]
  transfers between devices with their start and end apart: 8 -> 2, of which waited for: 7 -> 2; matrix products, arithmetic and copies ran while one was open for 2% -> 2% of each run, Pallas kernels for 0% -> 0%
where the time goes in v3:
time: 58 us; the launch traced here: 57.8 us
  blocking collectives  15.2 us (26%)
  starting transfers between devices  13 us (22%)
  waiting for transfers between devices  12.5 us (22%)
  Pallas kernels  8.65 us (15%)
  local copies, waits for them, and re-layouts  6.47 us (11%)
  other arithmetic  1.88 us (3%)
    all_to_all x1, blocking collectives, per_device(): summed = jnp.sum(lax.all_to_all(part, 'epoch', 0, 0, tiled=True), axis=0)  15.2 us
    ppermute x1, starting transfers between devices, per_device(): hi = lax.ppermute(x[:, :HALO], 'tile', backward)  11.1 us
    pallas_call x1, Pallas kernels, partial_stacks(): pl.pallas_call(stack_kernel, out_shape=jax.ShapeDtypeStruct((vels, rows,...  8.65 us
    ppermute x1, waiting for transfers between devices, per_device(): hi = lax.ppermute(x[:, :HALO], 'tile', backward)  6.62 us
    ppermute x1, waiting for transfers between devices, per_device(): lo = lax.ppermute(x[:, rows - HALO:], 'tile', forward)  5.93 us
    ppermute x1, starting transfers between devices, per_device(): lo = lax.ppermute(x[:, rows - HALO:], 'tile', forward)  1.92 us
    unnamed x10, local copies, waits for them, and re-layouts  1.9 us
    reshape x1, local copies, waits for them, and re-layouts, per_device(): part = part.reshape(vels, rows, 2, blocks, LANES).transpose(3, 0, 2, 1, 4)  1.76 us
  transfers between devices with their start and end apart: 2, of which 2 were waited for; matrix products, arithmetic and copies ran while one was open for 2% of the time, Pallas kernels for 0%

profile of v3, /device:TPU:6, one launch (start us, length us, event | category | flops | bytes accessed | tf_op | source)
XLA Modules:
  0.0 57.8 jit_solution(8043619025896193476)
XLA Ops:
  0.0 0.0 copy-start
  0.0 0.0 copy-start.4
  0.0 1.5 %stack.9 = f32[1,12,32,4,128]{4,3,2,1,0:T(4,128)S(1)} reshape(f32[12,32,512]{2,1,0:T(8,128)} %param.3) | data formatting | bytes 1572864 | tf_op jit(solution)/shard_map/stack | solution.py:75
  1.5 0.0 copy-done.4
  1.5 0.3 stack.10
  1.8 0.4 pad_maximum_fusion
  2.1 0.0 copy-start.1
  2.1 0.1 fusion.2
  2.3 1.0 %copy-done.1 = f32[2,12,32,4,128]{4,3,0,2,1:T(4,128)} copy-done((f32[2,12,32,4,128]{4,3,0,2,1:T(4,128)}, f32[2,12,32,4,128]{4,3,0,2,1:T(4,128)S(1)}, u32[]{:S(2)}) %copy-start.1) | copy-done | bytes 1572888
  3.3 11.1 %collective-permute-start.1 = (f32[12,16,8,128]{3,2,1,0:T(8,128)S(1)}, f32[12,16,8,128]{3,2,1,0:T(8,128)S(1)}, u32[]{:S(2)}, u32[]{:S(2)}) collective-permute-start(f32[12,16,8,128]{3,2,1,0:T(8,128)S(1)} %get-tuple-element.5), channel_id=1, source_target_pairs={{4,0},{8,4},{12,8},{16,12},{20,16},{24,20},{28,24},{32,28},{36,32}... | collective-permute-start | bytes 2359304 | tf_op jit(solution)/shard_map/ppermute | solution.py:81
  14.4 1.9 %collective-permute-start = (f32[12,16,8,128]{3,2,1,0:T(8,128)S(1)}, f32[12,16,8,128]{3,2,1,0:T(8,128)S(1)}, u32[]{:S(2)}, u32[]{:S(2)}) collective-permute-start(f32[12,16,8,128]{3,2,1,0:T(8,128)S(1)} %get-tuple-element.6), channel_id=1, source_target_pairs={{0,4},{4,8},{8,12},{12,16},{16,20},{20,24},{24,28},{28,32},{32,36}... | collective-permute-start | bytes 2359304 | tf_op jit(solution)/shard_map/ppermute | solution.py:80
  16.3 0.0 copy-done
  16.4 0.1 constant_dynamic-slice_fusion
  16.4 0.1 copy.9
  16.6 0.7 %reshape.16.sh_ref = s32[192]{0:T(256)} reshape(s32[8,12,2]{2,1,0:T(8,128)S(1)} %copy.9) | data formatting | bytes 1536 | tf_op jit(solution)/shard_map/reshape | solution.py:69
  17.3 6.6 %collective-permute-done.1.hi_ref = f32[12,16,8,128]{3,2,1,0:T(8,128)S(1)} collective-permute-done((f32[12,16,8,128]{3,2,1,0:T(8,128)S(1)}, f32[12,16,8,128]{3,2,1,0:T(8,128)S(1)}, u32[]{:S(2)}, u32[]{:S(2)}) %collective-permute-start.1) | collective-permute-done | bytes 786464 | tf_op jit(solution)/shard_map/ppermute | solution.py:81
  23.9 0.0 copy-start.2
  23.9 5.9 %collective-permute-done.lo_ref = f32[12,16,8,128]{3,2,1,0:T(8,128)S(1)} collective-permute-done((f32[12,16,8,128]{3,2,1,0:T(8,128)S(1)}, f32[12,16,8,128]{3,2,1,0:T(8,128)S(1)}, u32[]{:S(2)}, u32[]{:S(2)}) %collective-permute-start) | collective-permute-done | bytes 786464 | tf_op jit(solution)/shard_map/ppermute | solution.py:80
  29.8 0.0 copy-done.2
  29.8 0.0 copy-start.3
  29.8 0.9 %copy-done.3 = f32[12,16,8,128]{3,2,1,0:T(8,128)} copy-done((f32[12,16,8,128]{3,2,1,0:T(8,128)}, f32[12,16,8,128]{3,2,1,0:T(8,128)S(1)}, u32[]{:S(2)}) %copy-start.3) | copy-done | bytes 786456
  30.7 8.6 %shard_map.37 = f32[8,32,8,128]{3,2,1,0:T(8,128)} custom-call(s32[192]{0:T(256)} %reshape.16.sh_ref, f32[12,32,8,128]{3,2,1,0:T(8,128)} %bitcast.10, f32[12,16,8,128]{3,2,1,0:T(8,128)} %copy-done.3, f32[12,16,8,128]{3,2,1,0:T(8,128)} %copy-done.2), custom_call_target="tpu_custom_call" | custom-call | flops 6291456 | bytes 4194304 | tf_op jit(solution)/shard_map/pallas_call | solution.py:58
  39.4 1.8 %copy.18 = f32[8,32,2,4,128]{4,2,1,0,3:T(2,128)S(1)} copy(f32[8,32,2,4,128]{4,3,2,1,0:T(4,128)} %bitcast.11) | data formatting | bytes 2097152 | tf_op jit(solution)/shard_map/reshape | solution.py:86
  41.1 15.2 %all_to_all.5 = f32[4,8,2,32,128]{4,2,3,1,0:T(2,128)S(1)} all-to-all(f32[4,8,2,32,128]{4,2,3,1,0:T(2,128)S(1)} %bitcast.12), channel_id=1, replica_groups=mesh['tile'=128,'epoch'=4] {'epoch'}, dimensions={0} | all-to-all | bytes 2097152 | tf_op jit(solution)/shard_map/all_to_all | solution.py:87
  56.3 0.7 %reduce_sum.9 = f32[8,2,32,128]{3,1,2,0:T(2,128)S(1)} reduce(f32[4,8,2,32,128]{4,2,3,1,0:T(2,128)S(1)} %all_to_all.5, f32[]{:T(128)} %constant.4.clone.1), dimensions={0}, to_apply=%region_0.0 | reduce | flops 196608 | bytes 1310724 | tf_op jit(solution)/shard_map/reduce_sum | solution.py:87
  57.0 0.8 %fusion.1 = f32[32,128]{1,0:T(8,128)} fusion(f32[8,2,32,128]{3,1,2,0:T(2,128)S(1)} %reduce_sum.9), kind=kLoop, calls=%fused_computation.4 | loop fusion | flops 61440 | bytes 278528 | tf_op jit(solution)/shard_map/reduce_max | solution.py:89
Async XLA Ops:
  0.0 16.3 %copy-start = (s32[8,48,2]{1,2,0:T(2,128)S(1)}, s32[8,48,2]{1,2,0:T(2,128)}, u32[]{:S(2)}) copy-start(s32[8,48,2]{1,2,0:T(2,128)} %param.5) | copy-start | bytes 9220
  0.0 1.5 %copy-start.4 = (f32[12,32,512]{2,1,0:T(8,128)S(1)}, f32[12,32,512]{2,1,0:T(8,128)}, u32[]{:S(2)}) copy-start(f32[12,32,512]{2,1,0:T(8,128)} %param.4) | copy-start | bytes 2359300
  2.1 1.2 %copy-start.1 = (f32[2,12,32,4,128]{4,3,0,2,1:T(4,128)}, f32[2,12,32,4,128]{4,3,0,2,1:T(4,128)S(1)}, u32[]{:S(2)}) copy-start(f32[2,12,32,4,128]{4,3,0,2,1:T(4,128)S(1)} %pad_maximum_fusion) | copy-start | bytes 4718596
  3.3 20.6 %collective-permute-start.1 = (f32[12,16,8,128]{3,2,1,0:T(8,128)S(1)}, f32[12,16,8,128]{3,2,1,0:T(8,128)S(1)}, u32[]{:S(2)}, u32[]{:S(2)}) collective-permute-start(f32[12,16,8,128]{3,2,1,0:T(8,128)S(1)} %get-tuple-element.5), channel_id=1, source_target_pairs={{4,0},{8,4},{12,8},{16,12},{20,16},{24,20},{28,24},{32,28},{36,32}... | collective-permute-start | bytes 2359304 | tf_op jit(solution)/shard_map/ppermute | solution.py:81
  14.4 15.4 %collective-permute-start = (f32[12,16,8,128]{3,2,1,0:T(8,128)S(1)}, f32[12,16,8,128]{3,2,1,0:T(8,128)S(1)}, u32[]{:S(2)}, u32[]{:S(2)}) collective-permute-start(f32[12,16,8,128]{3,2,1,0:T(8,128)S(1)} %get-tuple-element.6), channel_id=1, source_target_pairs={{0,4},{4,8},{8,12},{12,16},{16,20},{20,24},{24,28},{28,32},{32,36}... | collective-permute-start | bytes 2359304 | tf_op jit(solution)/shard_map/ppermute | solution.py:80
  23.9 5.9 %copy-start.2 = (f32[12,16,8,128]{3,2,1,0:T(8,128)}, f32[12,16,8,128]{3,2,1,0:T(8,128)S(1)}, u32[]{:S(2)}) copy-start(f32[12,16,8,128]{3,2,1,0:T(8,128)S(1)} %collective-permute-done.1.hi_ref) | copy-start | bytes 2359300
  29.8 0.9 %copy-start.3 = (f32[12,16,8,128]{3,2,1,0:T(8,128)}, f32[12,16,8,128]{3,2,1,0:T(8,128)S(1)}, u32[]{:S(2)}) copy-start(f32[12,16,8,128]{3,2,1,0:T(8,128)S(1)} %collective-permute-done.lo_ref) | copy-start | bytes 2359300

commit v4 on v1

v4 whole, which is shorter than its diff:
```python
import jax
import jax.numpy as jnp
from jax import lax
from jax.experimental import pallas as pl
from jax.experimental.pallas import tpu as pltpu
from jax.sharding import PartitionSpec as P

HALO = 16
LANES = 128
CHUNK = 8


def stack_kernel(sh_ref, x_ref, out_ref):
    epochs, rows, slots, lanes = x_ref.shape
    blocks = slots // 2
    vels = out_ref.shape[0]

    out_ref[...] = jnp.zeros(out_ref.shape, jnp.float32)
    lane = lax.broadcasted_iota(jnp.int32, (slots, lanes), 1)
    block = lax.broadcasted_iota(jnp.int32, (slots, lanes), 0) % blocks
    for v in range(vels):

        def body(e, carry, v=v):
            at = (v * epochs + e) * 2
            s_r = sh_ref[at]
            s_c = sh_ref[at + 1]
            amount = lax.rem(lanes - s_c, lanes)
            moved = lane + s_c
            inside = (moved >= 0) & (moved < lanes)
            forward = (jnp.zeros((slots, lanes), jnp.int32) + s_c) >= 0
            edge = jnp.where(s_c >= 0, blocks - 1, 0)
            edge_ok = (block != edge) & ~inside
            for rc in range(rows // CHUNK):
                win = x_ref[e, rc * CHUNK : (rc + 1) * CHUNK]
                rolled = pltpu.roll(win, amount, axis=2)
                later = pltpu.roll(rolled, slots - 1, axis=1)
                earlier = pltpu.roll(rolled, 1, axis=1)
                other = jnp.where(forward[None], later, earlier)
                picked = jnp.where(inside[None], rolled, jnp.where(edge_ok[None], other, 0.0))
                dest = out_ref.at[v, pl.ds(HALO - s_r + rc * CHUNK, CHUNK)]
                dest[...] = dest[...] + picked
            return carry

        lax.fori_loop(0, epochs, body, 0)


def partial_stacks(own_shifts, x):
    epochs, rows, slots, lanes = x.shape
    vels = own_shifts.shape[0]
    vmem = pl.BlockSpec(memory_space=pltpu.VMEM)
    return pl.pallas_call(
        stack_kernel,
        out_shape=jax.ShapeDtypeStruct((vels, rows + 2 * HALO, slots, lanes), jnp.float32),
        in_specs=[pl.BlockSpec(memory_space=pltpu.SMEM), vmem],
        out_specs=vmem,
        cost_estimate=pl.CostEstimate(
            flops=2 * vels * epochs * rows * slots * lanes,
            bytes_accessed=4 * (epochs * rows + vels * (rows + 2 * HALO)) * slots * lanes,
            transcendentals=0,
        ),
    )(own_shifts.reshape(-1), x)


def per_device(psi, phi, shifts):
    epochs, rows, cols = psi.shape
    blocks = cols // LANES
    stacked = jnp.stack([psi, phi]).reshape(2, epochs, rows, blocks, LANES)
    x = stacked.transpose(1, 2, 0, 3, 4).reshape(epochs, rows, 2 * blocks, LANES)
    first = lax.axis_index("epoch") * epochs
    own_shifts = lax.dynamic_slice_in_dim(shifts, first, epochs, 1)
    part = partial_stacks(own_shifts, x)
    count = lax.axis_size("tile")
    forward = [(i, i + 1) for i in range(count - 1)]
    backward = [(i + 1, i) for i in range(count - 1)]
    from_above = lax.ppermute(part[:, rows + HALO :], "tile", forward)
    from_below = lax.ppermute(part[:, :HALO], "tile", backward)
    vels = part.shape[0]
    middle = jnp.zeros((vels, rows - 2 * HALO) + part.shape[2:], jnp.float32)
    part = part[:, HALO : HALO + rows] + jnp.concatenate([from_above, middle, from_below], axis=1)
    part = part.reshape(vels, rows, 2, blocks, LANES).transpose(3, 0, 2, 1, 4)
    summed = jnp.sum(lax.all_to_all(part, "epoch", 0, 0, tiled=True), axis=0)
    ratio = summed[:, 0] / jnp.sqrt(summed[:, 1])
    return jnp.max(ratio, axis=0)


def solution(mesh):
    placed = (P("epoch", "tile", None), P("epoch", "tile", None), P())
    return jax.shard_map(
        per_device, mesh=mesh, in_specs=placed, out_specs=P("tile", "epoch"), check_vma=False
    )
```

time: 82.8 us -> 57.2 us (0.69)
  waiting for transfers between devices: 38.3 us -> 6.68 us
  blocking collectives: 0 us -> 15.2 us
  between operations: 13.5 us -> 0.07 us
  Pallas kernels: 8.65 us -> 13.7 us
  local copies, waits for them, and re-layouts: 7.1 us -> 5.25 us
  other arithmetic: 1.97 us -> 3.15 us
    reduce_scatter x1 -> x0, waiting for transfers between devices: 25.7 us -> none  [per_device(): summed = lax.psum_scatter(part, 'epoch', scatter_dimension=0, tiled=True)]
    all_to_all x0 -> x1, blocking collectives: none -> 15.2 us  [per_device(): summed = jnp.sum(lax.all_to_all(part, 'epoch', 0, 0, tiled=True), axis=0)]
    ppermute x2, waiting for transfers between devices: 12.5 us -> 6.68 us  [the longest x1 4.92 us: per_device(): from_above = lax.ppermute(part[:, rows + HALO:], 'tile', forward)]
    pallas_call x1, Pallas kernels: 8.65 us -> 13.7 us  [partial_stacks(): pl.pallas_call(stack_kernel, out_shape=jax.ShapeDtypeStruct((vels, rows +...]
    reshape x1, local copies, waits for them, and re-layouts: 2.4 us -> 0.54 us  [per_device(): part = part.reshape(vels, rows, 2, blocks, LANES).transpose(3, 0, 2, 1, 4)]
    slice x1, local copies, waits for them, and re-layouts: 0.15 us -> 1.43 us  [per_device(): from_above = lax.ppermute(part[:, rows + HALO:], 'tile', forward)]
    unnamed x10 -> x6, local copies, waits for them, and re-layouts: 1.89 us -> 0.7 us
    another operation x1, other arithmetic: 0.36 us -> 1.52 us  [per_device(): stacked = jnp.stack([psi, phi]).reshape(2, epochs, rows, blocks, LANES)]
  transfers between devices with their start and end apart: 3 -> 2, of which waited for: 3 -> 2; matrix products, arithmetic and copies ran while one was open for 1% -> 0% of each run, Pallas kernels for 0% -> 0%
where the time goes in v4:
time: 57.2 us; the launch traced here: 57 us
  blocking collectives  15.2 us (27%)
  Pallas kernels  13.7 us (24%)
  starting transfers between devices  13 us (23%)
  waiting for transfers between devices  6.68 us (12%)
  local copies, waits for them, and re-layouts  5.25 us (9%)
  other arithmetic  3.15 us (6%)
    all_to_all x1, blocking collectives, per_device(): summed = jnp.sum(lax.all_to_all(part, 'epoch', 0, 0, tiled=True), axis=0)  15.2 us
    pallas_call x1, Pallas kernels, partial_stacks(): pl.pallas_call(stack_kernel, out_shape=jax.ShapeDtypeStruct((vels, rows +...  13.7 us
    ppermute x1, starting transfers between devices, per_device(): from_below = lax.ppermute(part[:, :HALO], 'tile', backward)  11.1 us
    ppermute x1, waiting for transfers between devices, per_device(): from_above = lax.ppermute(part[:, rows + HALO:], 'tile', forward)  4.92 us
    ppermute x1, starting transfers between devices, per_device(): from_above = lax.ppermute(part[:, rows + HALO:], 'tile', forward)  1.92 us
    ppermute x1, waiting for transfers between devices, per_device(): from_below = lax.ppermute(part[:, :HALO], 'tile', backward)  1.76 us
    another operation x2, local copies, waits for them, and re-layouts, per_device(): stacked = jnp.stack([psi, phi]).reshape(2, epochs, rows, blocks, LANES)  1.66 us
    another operation x1, other arithmetic, per_device(): stacked = jnp.stack([psi, phi]).reshape(2, epochs, rows, blocks, LANES)  1.52 us
  transfers between devices with their start and end apart: 2, of which 2 were waited for; matrix products, arithmetic and copies ran while one was open for 0% of the time, Pallas kernels for 0%

profile of v4, /device:TPU:6, one launch (start us, length us, event | category | flops | bytes accessed | tf_op | source)
XLA Modules:
  0.0 57.0 jit_solution(14423673497438902589)
XLA Ops:
  0.0 0.0 copy-start
  0.0 0.0 copy-start.2
  0.0 0.7 %copy-done = s32[8,48,2]{1,2,0:T(2,128)S(1)} copy-done((s32[8,48,2]{1,2,0:T(2,128)S(1)}, s32[8,48,2]{1,2,0:T(2,128)}, u32[]{:S(2)}) %copy-start) | copy-done | bytes 3096
  0.7 0.1 constant_dynamic-slice_fusion
  0.8 0.1 copy.9
  0.9 0.7 %reshape.16.sh_ref = s32[192]{0:T(256)} reshape(s32[8,12,2]{2,1,0:T(8,128)S(1)} %copy.9) | data formatting | bytes 1536 | tf_op jit(solution)/shard_map/reshape | solution.py:61
  1.6 1.4 %stack.9 = f32[1,12,32,4,128]{4,3,2,1,0:T(4,128)S(1)} reshape(f32[12,32,512]{2,1,0:T(8,128)} %param.3) | data formatting | bytes 1572864 | tf_op jit(solution)/shard_map/stack | solution.py:67
  3.0 0.0 copy-done.2
  3.0 0.3 stack.10
  3.3 1.5 %pad_maximum_fusion = f32[2,12,32,4,128]{4,3,0,2,1:T(4,128)} fusion(f32[1,12,32,4,128]{4,3,0,2,1:T(4,128)S(1)} %bitcast.13, f32[1,12,32,4,128]{4,3,0,2,1:T(4,128)S(1)} %bitcast.12), kind=kLoop, calls=%fused_computation | loop fusion | flops 393216 | bytes 3145728 | tf_op jit(solution)/shard_map/stack | solution.py:67
  4.8 13.7 %shard_map.37 = f32[8,64,8,128]{3,2,1,0:T(8,128)} custom-call(s32[192]{0:T(256)} %reshape.16.sh_ref, f32[12,32,8,128]{3,2,1,0:T(8,128)} %bitcast.9), custom_call_target="tpu_custom_call" | custom-call | flops 6291456 | bytes 3670016 | tf_op jit(solution)/shard_map/pallas_call | solution.py:51
  18.5 0.0 copy-start.1
  18.5 1.4 %fusion.2 = (f32[8,16,8,128]{3,2,1,0:T(8,128)S(1)}, f32[8,16,8,128]{3,2,1,0:T(8,128)S(1)}) fusion(f32[8,64,8,128]{3,2,1,0:T(8,128)} %shard_map.37), kind=kLoop, calls=%fused_computation.7 | loop fusion | bytes 2097152 | tf_op jit(solution)/shard_map/slice | solution.py:75
  19.9 1.9 %collective-permute-start = (f32[8,16,8,128]{3,2,1,0:T(8,128)S(1)}, f32[8,16,8,128]{3,2,1,0:T(8,128)S(1)}, u32[]{:S(2)}, u32[]{:S(2)}) collective-permute-start(f32[8,16,8,128]{3,2,1,0:T(8,128)S(1)} %get-tuple-element.5), channel_id=1, source_target_pairs={{0,4},{4,8},{8,12},{12,16},{16,20},{20,24},{24,28},{28,32},{32,36}... | collective-permute-start | bytes 1572872 | tf_op jit(solution)/shard_map/ppermute | solution.py:75
  21.8 11.1 %collective-permute-start.1 = (f32[8,16,8,128]{3,2,1,0:T(8,128)S(1)}, f32[8,16,8,128]{3,2,1,0:T(8,128)S(1)}, u32[]{:S(2)}, u32[]{:S(2)}) collective-permute-start(f32[8,16,8,128]{3,2,1,0:T(8,128)S(1)} %get-tuple-element.6), channel_id=1, source_target_pairs={{4,0},{8,4},{12,8},{16,12},{20,16},{24,20},{28,24},{32,28},{36,32}... | collective-permute-start | bytes 1572872 | tf_op jit(solution)/shard_map/ppermute | solution.py:76
  33.0 4.9 %collective-permute-done = f32[8,16,8,128]{3,2,1,0:T(8,128)S(1)} collective-permute-done((f32[8,16,8,128]{3,2,1,0:T(8,128)S(1)}, f32[8,16,8,128]{3,2,1,0:T(8,128)S(1)}, u32[]{:S(2)}, u32[]{:S(2)}) %collective-permute-start) | collective-permute-done | bytes 524320 | tf_op jit(solution)/shard_map/ppermute | solution.py:75
  37.9 1.8 %collective-permute-done.1 = f32[8,16,8,128]{3,2,1,0:T(8,128)S(1)} collective-permute-done((f32[8,16,8,128]{3,2,1,0:T(8,128)S(1)}, f32[8,16,8,128]{3,2,1,0:T(8,128)S(1)}, u32[]{:S(2)}, u32[]{:S(2)}) %collective-permute-start.1) | collective-permute-done | bytes 524320 | tf_op jit(solution)/shard_map/ppermute | solution.py:76
  39.6 0.0 copy-done.1
  39.6 0.1 slice_add_fusion
  39.7 0.5 copy.18
  40.3 15.2 %all_to_all.5 = f32[4,8,2,32,128]{4,2,3,1,0:T(2,128)S(1)} all-to-all(f32[4,8,2,32,128]{4,2,3,1,0:T(2,128)S(1)} %bitcast.11), channel_id=1, replica_groups=mesh['tile'=128,'epoch'=4] {'epoch'}, dimensions={0} | all-to-all | bytes 2097152 | tf_op jit(solution)/shard_map/all_to_all | solution.py:81
  55.5 0.7 %reduce_sum.9 = f32[8,2,32,128]{3,1,2,0:T(2,128)S(1)} reduce(f32[4,8,2,32,128]{4,2,3,1,0:T(2,128)S(1)} %all_to_all.5, f32[]{:T(128)} %constant.4.clone.1), dimensions={0}, to_apply=%region_0.0 | reduce | flops 196608 | bytes 1310724 | tf_op jit(solution)/shard_map/reduce_sum | solution.py:81
  56.1 0.8 %fusion.1 = f32[32,128]{1,0:T(8,128)} fusion(f32[8,2,32,128]{3,1,2,0:T(2,128)S(1)} %reduce_sum.9), kind=kLoop, calls=%fused_computation.5 | loop fusion | flops 61440 | bytes 278528 | tf_op jit(solution)/shard_map/reduce_max | solution.py:83
Async XLA Ops:
  0.0 0.7 %copy-start = (s32[8,48,2]{1,2,0:T(2,128)S(1)}, s32[8,48,2]{1,2,0:T(2,128)}, u32[]{:S(2)}) copy-start(s32[8,48,2]{1,2,0:T(2,128)} %param.5) | copy-start | bytes 9220
  0.0 3.0 %copy-start.2 = (f32[12,32,512]{2,1,0:T(8,128)S(1)}, f32[12,32,512]{2,1,0:T(8,128)}, u32[]{:S(2)}) copy-start(f32[12,32,512]{2,1,0:T(8,128)} %param.4) | copy-start | bytes 2359300
  18.5 21.2 %copy-start.1 = (f32[8,64,8,128]{3,2,1,0:T(8,128)S(1)}, f32[8,64,8,128]{3,2,1,0:T(8,128)}, u32[]{:S(2)}) copy-start(f32[8,64,8,128]{3,2,1,0:T(8,128)} %shard_map.37) | copy-start | bytes 6291460
  19.9 18.0 %collective-permute-start = (f32[8,16,8,128]{3,2,1,0:T(8,128)S(1)}, f32[8,16,8,128]{3,2,1,0:T(8,128)S(1)}, u32[]{:S(2)}, u32[]{:S(2)}) collective-permute-start(f32[8,16,8,128]{3,2,1,0:T(8,128)S(1)} %get-tuple-element.5), channel_id=1, source_target_pairs={{0,4},{4,8},{8,12},{12,16},{16,20},{20,24},{24,28},{28,32},{32,36}... | collective-permute-start | bytes 1572872 | tf_op jit(solution)/shard_map/ppermute | solution.py:75
  21.8 17.8 %collective-permute-start.1 = (f32[8,16,8,128]{3,2,1,0:T(8,128)S(1)}, f32[8,16,8,128]{3,2,1,0:T(8,128)S(1)}, u32[]{:S(2)}, u32[]{:S(2)}) collective-permute-start(f32[8,16,8,128]{3,2,1,0:T(8,128)S(1)} %get-tuple-element.6), channel_id=1, source_target_pairs={{4,0},{8,4},{12,8},{16,12},{20,16},{24,20},{28,24},{32,28},{36,32}... | collective-permute-start | bytes 1572872 | tf_op jit(solution)/shard_map/ppermute | solution.py:76

commit v5 on v4

--- a/solution.py
+++ b/solution.py
@@ -27,15 +27,13 @@
             amount = lax.rem(lanes - s_c, lanes)
             moved = lane + s_c
             inside = (moved >= 0) & (moved < lanes)
-            forward = (jnp.zeros((slots, lanes), jnp.int32) + s_c) >= 0
+            step = jnp.where(s_c >= 0, slots - 1, 1)
             edge = jnp.where(s_c >= 0, blocks - 1, 0)
             edge_ok = (block != edge) & ~inside
             for rc in range(rows // CHUNK):
                 win = x_ref[e, rc * CHUNK : (rc + 1) * CHUNK]
                 rolled = pltpu.roll(win, amount, axis=2)
-                later = pltpu.roll(rolled, slots - 1, axis=1)
-                earlier = pltpu.roll(rolled, 1, axis=1)
-                other = jnp.where(forward[None], later, earlier)
+                other = pltpu.roll(rolled, step, axis=1)
                 picked = jnp.where(inside[None], rolled, jnp.where(edge_ok[None], other, 0.0))
                 dest = out_ref.at[v, pl.ds(HALO - s_r + rc * CHUNK, CHUNK)]
                 dest[...] = dest[...] + picked

time: 57.2 us -> 57.1 us (level)
  no operation moved by 1% of the time
where the time goes in v5:
time: 57.1 us; the launch traced here: 56.9 us
  blocking collectives  15.2 us (27%)
  Pallas kernels  13.6 us (24%)
  starting transfers between devices  13 us (23%)
  waiting for transfers between devices  6.68 us (12%)
  local copies, waits for them, and re-layouts  5.25 us (9%)
  other arithmetic  3.15 us (6%)
    all_to_all x1, blocking collectives, per_device(): summed = jnp.sum(lax.all_to_all(part, 'epoch', 0, 0, tiled=True), axis=0)  15.2 us
    pallas_call x1, Pallas kernels, partial_stacks(): pl.pallas_call(stack_kernel, out_shape=jax.ShapeDtypeStruct((vels, rows +...  13.6 us
    ppermute x1, starting transfers between devices, per_device(): from_below = lax.ppermute(part[:, :HALO], 'tile', backward)  11.1 us
    ppermute x1, waiting for transfers between devices, per_device(): from_above = lax.ppermute(part[:, rows + HALO:], 'tile', forward)  4.92 us
    ppermute x1, starting transfers between devices, per_device(): from_above = lax.ppermute(part[:, rows + HALO:], 'tile', forward)  1.92 us
    ppermute x1, waiting for transfers between devices, per_device(): from_below = lax.ppermute(part[:, :HALO], 'tile', backward)  1.76 us
    another operation x2, local copies, waits for them, and re-layouts, per_device(): stacked = jnp.stack([psi, phi]).reshape(2, epochs, rows, blocks, LANES)  1.66 us
    another operation x1, other arithmetic, per_device(): stacked = jnp.stack([psi, phi]).reshape(2, epochs, rows, blocks, LANES)  1.52 us
  transfers between devices with their start and end apart: 2, of which 2 were waited for; matrix products, arithmetic and copies ran while one was open for 0% of the time, Pallas kernels for 0%

profile of v5, /device:TPU:6, one launch (start us, length us, event | category | flops | bytes accessed | tf_op | source)
XLA Modules:
  0.0 56.9 jit_solution(3055800560385814233)
XLA Ops:
  0.0 0.0 copy-start
  0.0 0.0 copy-start.2
  0.0 0.7 %copy-done = s32[8,48,2]{1,2,0:T(2,128)S(1)} copy-done((s32[8,48,2]{1,2,0:T(2,128)S(1)}, s32[8,48,2]{1,2,0:T(2,128)}, u32[]{:S(2)}) %copy-start) | copy-done | bytes 3096
  0.7 0.1 constant_dynamic-slice_fusion
  0.8 0.1 copy.9
  0.9 0.7 %reshape.16.sh_ref = s32[192]{0:T(256)} reshape(s32[8,12,2]{2,1,0:T(8,128)S(1)} %copy.9) | data formatting | bytes 1536 | tf_op jit(solution)/shard_map/reshape | solution.py:59
  1.6 1.4 %stack.9 = f32[1,12,32,4,128]{4,3,2,1,0:T(4,128)S(1)} reshape(f32[12,32,512]{2,1,0:T(8,128)} %param.3) | data formatting | bytes 1572864 | tf_op jit(solution)/shard_map/stack | solution.py:65
  3.0 0.0 copy-done.2
  3.0 0.3 stack.10
  3.3 1.5 %pad_maximum_fusion = f32[2,12,32,4,128]{4,3,0,2,1:T(4,128)} fusion(f32[1,12,32,4,128]{4,3,0,2,1:T(4,128)S(1)} %bitcast.13, f32[1,12,32,4,128]{4,3,0,2,1:T(4,128)S(1)} %bitcast.12), kind=kLoop, calls=%fused_computation | loop fusion | flops 393216 | bytes 3145728 | tf_op jit(solution)/shard_map/stack | solution.py:65
  4.8 13.6 %shard_map.37 = f32[8,64,8,128]{3,2,1,0:T(8,128)} custom-call(s32[192]{0:T(256)} %reshape.16.sh_ref, f32[12,32,8,128]{3,2,1,0:T(8,128)} %bitcast.9), custom_call_target="tpu_custom_call" | custom-call | flops 6291456 | bytes 3670016 | tf_op jit(solution)/shard_map/pallas_call | solution.py:49
  18.4 0.0 copy-start.1
  18.4 1.4 %fusion.2 = (f32[8,16,8,128]{3,2,1,0:T(8,128)S(1)}, f32[8,16,8,128]{3,2,1,0:T(8,128)S(1)}) fusion(f32[8,64,8,128]{3,2,1,0:T(8,128)} %shard_map.37), kind=kLoop, calls=%fused_computation.7 | loop fusion | bytes 2097152 | tf_op jit(solution)/shard_map/slice | solution.py:73
  19.8 1.9 %collective-permute-start = (f32[8,16,8,128]{3,2,1,0:T(8,128)S(1)}, f32[8,16,8,128]{3,2,1,0:T(8,128)S(1)}, u32[]{:S(2)}, u32[]{:S(2)}) collective-permute-start(f32[8,16,8,128]{3,2,1,0:T(8,128)S(1)} %get-tuple-element.5), channel_id=1, source_target_pairs={{0,4},{4,8},{8,12},{12,16},{16,20},{20,24},{24,28},{28,32},{32,36}... | collective-permute-start | bytes 1572872 | tf_op jit(solution)/shard_map/ppermute | solution.py:73
  21.7 11.1 %collective-permute-start.1 = (f32[8,16,8,128]{3,2,1,0:T(8,128)S(1)}, f32[8,16,8,128]{3,2,1,0:T(8,128)S(1)}, u32[]{:S(2)}, u32[]{:S(2)}) collective-permute-start(f32[8,16,8,128]{3,2,1,0:T(8,128)S(1)} %get-tuple-element.6), channel_id=1, source_target_pairs={{4,0},{8,4},{12,8},{16,12},{20,16},{24,20},{28,24},{32,28},{36,32}... | collective-permute-start | bytes 1572872 | tf_op jit(solution)/shard_map/ppermute | solution.py:74
  32.9 4.9 %collective-permute-done = f32[8,16,8,128]{3,2,1,0:T(8,128)S(1)} collective-permute-done((f32[8,16,8,128]{3,2,1,0:T(8,128)S(1)}, f32[8,16,8,128]{3,2,1,0:T(8,128)S(1)}, u32[]{:S(2)}, u32[]{:S(2)}) %collective-permute-start) | collective-permute-done | bytes 524320 | tf_op jit(solution)/shard_map/ppermute | solution.py:73
  37.8 1.8 %collective-permute-done.1 = f32[8,16,8,128]{3,2,1,0:T(8,128)S(1)} collective-permute-done((f32[8,16,8,128]{3,2,1,0:T(8,128)S(1)}, f32[8,16,8,128]{3,2,1,0:T(8,128)S(1)}, u32[]{:S(2)}, u32[]{:S(2)}) %collective-permute-start.1) | collective-permute-done | bytes 524320 | tf_op jit(solution)/shard_map/ppermute | solution.py:74
  39.5 0.0 copy-done.1
  39.5 0.1 slice_add_fusion
  39.6 0.5 copy.18
  40.2 15.2 %all_to_all.5 = f32[4,8,2,32,128]{4,2,3,1,0:T(2,128)S(1)} all-to-all(f32[4,8,2,32,128]{4,2,3,1,0:T(2,128)S(1)} %bitcast.11), channel_id=1, replica_groups=mesh['tile'=128,'epoch'=4] {'epoch'}, dimensions={0} | all-to-all | bytes 2097152 | tf_op jit(solution)/shard_map/all_to_all | solution.py:79
  55.3 0.7 %reduce_sum.9 = f32[8,2,32,128]{3,1,2,0:T(2,128)S(1)} reduce(f32[4,8,2,32,128]{4,2,3,1,0:T(2,128)S(1)} %all_to_all.5, f32[]{:T(128)} %constant.4.clone.1), dimensions={0}, to_apply=%region_0.0 | reduce | flops 196608 | bytes 1310724 | tf_op jit(solution)/shard_map/reduce_sum | solution.py:79
  56.0 0.8 %fusion.1 = f32[32,128]{1,0:T(8,128)} fusion(f32[8,2,32,128]{3,1,2,0:T(2,128)S(1)} %reduce_sum.9), kind=kLoop, calls=%fused_computation.5 | loop fusion | flops 61440 | bytes 278528 | tf_op jit(solution)/shard_map/reduce_max | solution.py:81
Async XLA Ops:
  0.0 0.7 %copy-start = (s32[8,48,2]{1,2,0:T(2,128)S(1)}, s32[8,48,2]{1,2,0:T(2,128)}, u32[]{:S(2)}) copy-start(s32[8,48,2]{1,2,0:T(2,128)} %param.5) | copy-start | bytes 9220
  0.0 3.0 %copy-start.2 = (f32[12,32,512]{2,1,0:T(8,128)S(1)}, f32[12,32,512]{2,1,0:T(8,128)}, u32[]{:S(2)}) copy-start(f32[12,32,512]{2,1,0:T(8,128)} %param.4) | copy-start | bytes 2359300
  18.4 21.2 %copy-start.1 = (f32[8,64,8,128]{3,2,1,0:T(8,128)S(1)}, f32[8,64,8,128]{3,2,1,0:T(8,128)}, u32[]{:S(2)}) copy-start(f32[8,64,8,128]{3,2,1,0:T(8,128)} %shard_map.37) | copy-start | bytes 6291460
  19.8 18.0 %collective-permute-start = (f32[8,16,8,128]{3,2,1,0:T(8,128)S(1)}, f32[8,16,8,128]{3,2,1,0:T(8,128)S(1)}, u32[]{:S(2)}, u32[]{:S(2)}) collective-permute-start(f32[8,16,8,128]{3,2,1,0:T(8,128)S(1)} %get-tuple-element.5), channel_id=1, source_target_pairs={{0,4},{4,8},{8,12},{12,16},{16,20},{20,24},{24,28},{28,32},{32,36}... | collective-permute-start | bytes 1572872 | tf_op jit(solution)/shard_map/ppermute | solution.py:73
  21.7 17.8 %collective-permute-start.1 = (f32[8,16,8,128]{3,2,1,0:T(8,128)S(1)}, f32[8,16,8,128]{3,2,1,0:T(8,128)S(1)}, u32[]{:S(2)}, u32[]{:S(2)}) collective-permute-start(f32[8,16,8,128]{3,2,1,0:T(8,128)S(1)} %get-tuple-element.6), channel_id=1, source_target_pairs={{4,0},{8,4},{12,8},{16,12},{20,16},{24,20},{28,24},{32,28},{36,32}... | collective-permute-start | bytes 1572872 | tf_op jit(solution)/shard_map/ppermute | solution.py:74

commit v6 on v5

--- a/solution.py
+++ b/solution.py
@@ -10,17 +10,23 @@
 CHUNK = 8
 
 
-def stack_kernel(sh_ref, x_ref, out_ref):
+def stack_kernel(sh_ref, x_ref, out_ref, odd_ref):
     epochs, rows, slots, lanes = x_ref.shape
     blocks = slots // 2
     vels = out_ref.shape[0]
 
     out_ref[...] = jnp.zeros(out_ref.shape, jnp.float32)
+    odd_ref[...] = jnp.zeros(odd_ref.shape, jnp.float32)
     lane = lax.broadcasted_iota(jnp.int32, (slots, lanes), 1)
     block = lax.broadcasted_iota(jnp.int32, (slots, lanes), 0) % blocks
     for v in range(vels):
 
-        def body(e, carry, v=v):
+        def body(i, carry, v=v):
+            for parity, acc_ref in ((0, out_ref), (1, odd_ref)):
+                add_epoch(v, 2 * i + parity, acc_ref)
+            return carry
+
+        def add_epoch(v, e, acc_ref):
             at = (v * epochs + e) * 2
             s_r = sh_ref[at]
             s_c = sh_ref[at + 1]
@@ -35,11 +41,11 @@
                 rolled = pltpu.roll(win, amount, axis=2)
                 other = pltpu.roll(rolled, step, axis=1)
                 picked = jnp.where(inside[None], rolled, jnp.where(edge_ok[None], other, 0.0))
-                dest = out_ref.at[v, pl.ds(HALO - s_r + rc * CHUNK, CHUNK)]
+                dest = acc_ref.at[v, pl.ds(HALO - s_r + rc * CHUNK, CHUNK)]
                 dest[...] = dest[...] + picked
-            return carry
 
-        lax.fori_loop(0, epochs, body, 0)
+        lax.fori_loop(0, epochs // 2, body, 0)
+        out_ref[v] = out_ref[v] + odd_ref[v]
 
 
 def partial_stacks(own_shifts, x):
@@ -51,6 +57,7 @@
         out_shape=jax.ShapeDtypeStruct((vels, rows + 2 * HALO, slots, lanes), jnp.float32),
         in_specs=[pl.BlockSpec(memory_space=pltpu.SMEM), vmem],
         out_specs=vmem,
+        scratch_shapes=[pltpu.VMEM((vels, rows + 2 * HALO, slots, lanes), jnp.float32)],
         cost_estimate=pl.CostEstimate(
             flops=2 * vels * epochs * rows * slots * lanes,
             bytes_accessed=4 * (epochs * rows + vels * (rows + 2 * HALO)) * slots * lanes,

time: 57.1 us -> 53.7 us (0.940)
  Pallas kernels: 13.6 us -> 10.1 us
    pallas_call x1, Pallas kernels: 13.6 us -> 10.1 us  [partial_stacks(): pl.pallas_call(stack_kernel, out_shape=jax.ShapeDtypeStruct((vels, rows +...]
where the time goes in v6:
time: 53.7 us; the launch traced here: 53.4 us
  blocking collectives  15.2 us (28%)
  starting transfers between devices  13 us (24%)
  Pallas kernels  10.1 us (19%)
  waiting for transfers between devices  6.68 us (12%)
  local copies, waits for them, and re-layouts  5.25 us (10%)
  other arithmetic  3.15 us (6%)
    all_to_all x1, blocking collectives, per_device(): summed = jnp.sum(lax.all_to_all(part, 'epoch', 0, 0, tiled=True), axis=0)  15.2 us
    ppermute x1, starting transfers between devices, per_device(): from_below = lax.ppermute(part[:, :HALO], 'tile', backward)  11.1 us
    pallas_call x1, Pallas kernels, partial_stacks(): pl.pallas_call(stack_kernel, out_shape=jax.ShapeDtypeStruct((vels, rows +...  10.1 us
    ppermute x1, waiting for transfers between devices, per_device(): from_above = lax.ppermute(part[:, rows + HALO:], 'tile', forward)  4.92 us
    ppermute x1, starting transfers between devices, per_device(): from_above = lax.ppermute(part[:, rows + HALO:], 'tile', forward)  1.92 us
    ppermute x1, waiting for transfers between devices, per_device(): from_below = lax.ppermute(part[:, :HALO], 'tile', backward)  1.76 us
    another operation x2, local copies, waits for them, and re-layouts, per_device(): stacked = jnp.stack([psi, phi]).reshape(2, epochs, rows, blocks, LANES)  1.66 us
    another operation x1, other arithmetic, per_device(): stacked = jnp.stack([psi, phi]).reshape(2, epochs, rows, blocks, LANES)  1.52 us
  transfers between devices with their start and end apart: 2, of which 2 were waited for; matrix products, arithmetic and copies ran while one was open for 0% of the time, Pallas kernels for 0%

profile of v6, /device:TPU:6, one launch (start us, length us, event | category | flops | bytes accessed | tf_op | source)
XLA Modules:
  0.0 53.4 jit_solution(7388643401851916129)
XLA Ops:
  0.0 0.0 copy-start
  0.0 0.0 copy-start.2
  0.0 0.7 %copy-done = s32[8,48,2]{1,2,0:T(2,128)S(1)} copy-done((s32[8,48,2]{1,2,0:T(2,128)S(1)}, s32[8,48,2]{1,2,0:T(2,128)}, u32[]{:S(2)}) %copy-start) | copy-done | bytes 3096
  0.7 0.1 constant_dynamic-slice_fusion
  0.8 0.1 copy.9
  0.9 0.7 %reshape.16.sh_ref = s32[192]{0:T(256)} reshape(s32[8,12,2]{2,1,0:T(8,128)S(1)} %copy.9) | data formatting | bytes 1536 | tf_op jit(solution)/shard_map/reshape | solution.py:66
  1.6 1.4 %stack.9 = f32[1,12,32,4,128]{4,3,2,1,0:T(4,128)S(1)} reshape(f32[12,32,512]{2,1,0:T(8,128)} %param.3) | data formatting | bytes 1572864 | tf_op jit(solution)/shard_map/stack | solution.py:72
  3.0 0.0 copy-done.2
  3.0 0.3 stack.10
  3.3 1.5 %pad_maximum_fusion = f32[2,12,32,4,128]{4,3,0,2,1:T(4,128)} fusion(f32[1,12,32,4,128]{4,3,0,2,1:T(4,128)S(1)} %bitcast.13, f32[1,12,32,4,128]{4,3,0,2,1:T(4,128)S(1)} %bitcast.12), kind=kLoop, calls=%fused_computation | loop fusion | flops 393216 | bytes 3145728 | tf_op jit(solution)/shard_map/stack | solution.py:72
  4.8 10.1 %shard_map.37 = f32[8,64,8,128]{3,2,1,0:T(8,128)} custom-call(s32[192]{0:T(256)} %reshape.16.sh_ref, f32[12,32,8,128]{3,2,1,0:T(8,128)} %bitcast.9), custom_call_target="tpu_custom_call" | custom-call | flops 6291456 | bytes 3670016 | tf_op jit(solution)/shard_map/pallas_call | solution.py:55
  14.9 0.0 copy-start.1
  14.9 1.4 %fusion.2 = (f32[8,16,8,128]{3,2,1,0:T(8,128)S(1)}, f32[8,16,8,128]{3,2,1,0:T(8,128)S(1)}) fusion(f32[8,64,8,128]{3,2,1,0:T(8,128)} %shard_map.37), kind=kLoop, calls=%fused_computation.7 | loop fusion | bytes 2097152 | tf_op jit(solution)/shard_map/slice | solution.py:80
  16.4 1.9 %collective-permute-start = (f32[8,16,8,128]{3,2,1,0:T(8,128)S(1)}, f32[8,16,8,128]{3,2,1,0:T(8,128)S(1)}, u32[]{:S(2)}, u32[]{:S(2)}) collective-permute-start(f32[8,16,8,128]{3,2,1,0:T(8,128)S(1)} %get-tuple-element.5), channel_id=1, source_target_pairs={{0,4},{4,8},{8,12},{12,16},{16,20},{20,24},{24,28},{28,32},{32,36}... | collective-permute-start | bytes 1572872 | tf_op jit(solution)/shard_map/ppermute | solution.py:80
  18.3 11.1 %collective-permute-start.1 = (f32[8,16,8,128]{3,2,1,0:T(8,128)S(1)}, f32[8,16,8,128]{3,2,1,0:T(8,128)S(1)}, u32[]{:S(2)}, u32[]{:S(2)}) collective-permute-start(f32[8,16,8,128]{3,2,1,0:T(8,128)S(1)} %get-tuple-element.6), channel_id=1, source_target_pairs={{4,0},{8,4},{12,8},{16,12},{20,16},{24,20},{28,24},{32,28},{36,32}... | collective-permute-start | bytes 1572872 | tf_op jit(solution)/shard_map/ppermute | solution.py:81
  29.4 4.9 %collective-permute-done = f32[8,16,8,128]{3,2,1,0:T(8,128)S(1)} collective-permute-done((f32[8,16,8,128]{3,2,1,0:T(8,128)S(1)}, f32[8,16,8,128]{3,2,1,0:T(8,128)S(1)}, u32[]{:S(2)}, u32[]{:S(2)}) %collective-permute-start) | collective-permute-done | bytes 524320 | tf_op jit(solution)/shard_map/ppermute | solution.py:80
  34.3 1.8 %collective-permute-done.1 = f32[8,16,8,128]{3,2,1,0:T(8,128)S(1)} collective-permute-done((f32[8,16,8,128]{3,2,1,0:T(8,128)S(1)}, f32[8,16,8,128]{3,2,1,0:T(8,128)S(1)}, u32[]{:S(2)}, u32[]{:S(2)}) %collective-permute-start.1) | collective-permute-done | bytes 524320 | tf_op jit(solution)/shard_map/ppermute | solution.py:81
  36.1 0.0 copy-done.1
  36.1 0.1 slice_add_fusion
  36.2 0.5 %copy.18 = f32[8,32,2,4,128]{4,2,1,0,3:T(2,128)S(1)} copy(f32[8,32,2,4,128]{4,3,2,1,0:T(4,128)S(1)} %bitcast.10) | data formatting | bytes 2097152 | tf_op jit(solution)/shard_map/reshape | solution.py:85
  36.7 15.2 %all_to_all.5 = f32[4,8,2,32,128]{4,2,3,1,0:T(2,128)S(1)} all-to-all(f32[4,8,2,32,128]{4,2,3,1,0:T(2,128)S(1)} %bitcast.11), channel_id=1, replica_groups=mesh['tile'=128,'epoch'=4] {'epoch'}, dimensions={0} | all-to-all | bytes 2097152 | tf_op jit(solution)/shard_map/all_to_all | solution.py:86
  51.9 0.7 %reduce_sum.9 = f32[8,2,32,128]{3,1,2,0:T(2,128)S(1)} reduce(f32[4,8,2,32,128]{4,2,3,1,0:T(2,128)S(1)} %all_to_all.5, f32[]{:T(128)} %constant.4.clone.1), dimensions={0}, to_apply=%region_0.0 | reduce | flops 196608 | bytes 1310724 | tf_op jit(solution)/shard_map/reduce_sum | solution.py:86
  52.6 0.8 %fusion.1 = f32[32,128]{1,0:T(8,128)} fusion(f32[8,2,32,128]{3,1,2,0:T(2,128)S(1)} %reduce_sum.9), kind=kLoop, calls=%fused_computation.5 | loop fusion | flops 61440 | bytes 278528 | tf_op jit(solution)/shard_map/reduce_max | solution.py:88
Async XLA Ops:
  0.0 0.7 %copy-start = (s32[8,48,2]{1,2,0:T(2,128)S(1)}, s32[8,48,2]{1,2,0:T(2,128)}, u32[]{:S(2)}) copy-start(s32[8,48,2]{1,2,0:T(2,128)} %param.5) | copy-start | bytes 9220
  0.0 3.0 %copy-start.2 = (f32[12,32,512]{2,1,0:T(8,128)S(1)}, f32[12,32,512]{2,1,0:T(8,128)}, u32[]{:S(2)}) copy-start(f32[12,32,512]{2,1,0:T(8,128)} %param.4) | copy-start | bytes 2359300
  14.9 21.2 %copy-start.1 = (f32[8,64,8,128]{3,2,1,0:T(8,128)S(1)}, f32[8,64,8,128]{3,2,1,0:T(8,128)}, u32[]{:S(2)}) copy-start(f32[8,64,8,128]{3,2,1,0:T(8,128)} %shard_map.37) | copy-start | bytes 6291460
  16.4 18.0 %collective-permute-start = (f32[8,16,8,128]{3,2,1,0:T(8,128)S(1)}, f32[8,16,8,128]{3,2,1,0:T(8,128)S(1)}, u32[]{:S(2)}, u32[]{:S(2)}) collective-permute-start(f32[8,16,8,128]{3,2,1,0:T(8,128)S(1)} %get-tuple-element.5), channel_id=1, source_target_pairs={{0,4},{4,8},{8,12},{12,16},{16,20},{20,24},{24,28},{28,32},{32,36}... | collective-permute-start | bytes 1572872 | tf_op jit(solution)/shard_map/ppermute | solution.py:80
  18.3 17.8 %collective-permute-start.1 = (f32[8,16,8,128]{3,2,1,0:T(8,128)S(1)}, f32[8,16,8,128]{3,2,1,0:T(8,128)S(1)}, u32[]{:S(2)}, u32[]{:S(2)}) collective-permute-start(f32[8,16,8,128]{3,2,1,0:T(8,128)S(1)} %get-tuple-element.6), channel_id=1, source_target_pairs={{4,0},{8,4},{12,8},{16,12},{20,16},{24,20},{28,24},{32,28},{36,32}... | collective-permute-start | bytes 1572872 | tf_op jit(solution)/shard_map/ppermute | solution.py:81

commit v7 on v5

v7 whole, which is shorter than its diff:
```python
import jax
import jax.numpy as jnp
from jax import lax
from jax.experimental import pallas as pl
from jax.experimental.pallas import tpu as pltpu
from jax.sharding import PartitionSpec as P

HALO = 16
LANES = 128
CHUNK = 8


def stack_kernel(sh_ref, x_ref, own_ref, top_ref, bottom_ref, acc_ref):
    epochs, rows, slots, lanes = x_ref.shape
    blocks = slots // 2
    chains = acc_ref.shape[0]
    vels = acc_ref.shape[1]
    total = sh_ref.shape[0] // (2 * vels)
    first = lax.axis_index("epoch") * epochs

    acc_ref[...] = jnp.zeros(acc_ref.shape, jnp.float32)
    lane = lax.broadcasted_iota(jnp.int32, (slots, lanes), 1)
    block = lax.broadcasted_iota(jnp.int32, (slots, lanes), 0) % blocks
    for v in range(vels):

        def add_epoch(v, e, into):
            at = (v * total + first + e) * 2
            s_r = sh_ref[at]
            s_c = sh_ref[at + 1]
            amount = lax.rem(lanes - s_c, lanes)
            moved = lane + s_c
            inside = (moved >= 0) & (moved < lanes)
            step = jnp.where(s_c >= 0, slots - 1, 1)
            edge = jnp.where(s_c >= 0, blocks - 1, 0)
            edge_ok = (block != edge) & ~inside
            for rc in range(rows // CHUNK):
                win = x_ref[e, rc * CHUNK : (rc + 1) * CHUNK]
                rolled = pltpu.roll(win, amount, axis=2)
                other = pltpu.roll(rolled, step, axis=1)
                picked = jnp.where(inside[None], rolled, jnp.where(edge_ok[None], other, 0.0))
                dest = acc_ref.at[into, v, pl.ds(HALO - s_r + rc * CHUNK, CHUNK)]
                dest[...] = dest[...] + picked

        def body(i, carry, v=v):
            for chain in range(chains):
                add_epoch(v, chains * i + chain, chain)
            return carry

        lax.fori_loop(0, epochs // chains, body, 0)
        total_v = acc_ref[0, v]
        for chain in range(1, chains):
            total_v = total_v + acc_ref[chain, v]
        top_ref[v] = total_v[:HALO]
        own_ref[v] = total_v[HALO : HALO + rows]
        bottom_ref[v] = total_v[HALO + rows :]


def partial_stacks(shifts, x):
    epochs, rows, slots, lanes = x.shape
    vels = shifts.shape[0]
    chains = 4 if epochs % 4 == 0 else (2 if epochs % 2 == 0 else 1)
    vmem = pl.BlockSpec(memory_space=pltpu.VMEM)
    spill = jax.ShapeDtypeStruct((vels, HALO, slots, lanes), jnp.float32)
    return pl.pallas_call(
        stack_kernel,
        out_shape=(jax.ShapeDtypeStruct((vels, rows, slots, lanes), jnp.float32), spill, spill),
        in_specs=[pl.BlockSpec(memory_space=pltpu.SMEM), vmem],
        out_specs=(vmem, vmem, vmem),
        scratch_shapes=[pltpu.VMEM((chains, vels, rows + 2 * HALO, slots, lanes), jnp.float32)],
        cost_estimate=pl.CostEstimate(
            flops=2 * vels * epochs * rows * slots * lanes,
            bytes_accessed=4 * (epochs * rows + vels * (rows + 2 * HALO)) * slots * lanes,
            transcendentals=0,
        ),
    )(shifts.reshape(-1), x)


def per_device(psi, phi, shifts):
    epochs, rows, cols = psi.shape
    blocks = cols // LANES
    stacked = jnp.stack([psi, phi]).reshape(2, epochs, rows, blocks, LANES)
    x = stacked.transpose(1, 2, 0, 3, 4).reshape(epochs, rows, 2 * blocks, LANES)
    own, top, bottom = partial_stacks(shifts, x)
    count = lax.axis_size("tile")
    forward = [(i, i + 1) for i in range(count - 1)]
    backward = [(i + 1, i) for i in range(count - 1)]
    from_above = lax.ppermute(bottom, "tile", forward)
    from_below = lax.ppermute(top, "tile", backward)
    vels = own.shape[0]
    middle = jnp.zeros((vels, rows - 2 * HALO) + own.shape[2:], jnp.float32)
    part = own + jnp.concatenate([from_above, middle, from_below], axis=1)
    part = part.reshape(vels, rows, 2, blocks, LANES).transpose(3, 0, 2, 1, 4)
    summed = jnp.sum(lax.all_to_all(part, "epoch", 0, 0, tiled=True), axis=0)
    ratio = summed[:, 0] / jnp.sqrt(summed[:, 1])
    return jnp.max(ratio, axis=0)


def solution(mesh):
    placed = (P("epoch", "tile", None), P("epoch", "tile", None), P())
    return jax.shard_map(
        per_device, mesh=mesh, in_specs=placed, out_specs=P("tile", "epoch"), check_vma=False
    )
```

time: 57.1 us -> 52.4 us (0.918)
  Pallas kernels: 13.6 us -> 8.71 us
  local copies, waits for them, and re-layouts: 5.25 us -> 3.84 us
  other arithmetic: 3.15 us -> 4.37 us
    pallas_call x1, Pallas kernels: 13.6 us -> 8.71 us  [partial_stacks(): pl.pallas_call(stack_kernel, out_shape=(jax.ShapeDtypeStruct((vels, rows,...]
    slice x1 -> x0, local copies, waits for them, and re-layouts: 1.43 us -> none  [per_device(): from_above = lax.ppermute(part[:, rows + HALO:], 'tile', forward)]
    add x1, other arithmetic: 0.11 us -> 1.39 us  [per_device(): part = own + jnp.concatenate([from_above, middle, from_below], axis=1)]
where the time goes in v7:
time: 52.4 us; the launch traced here: 52.2 us
  blocking collectives  15.2 us (29%)
  starting transfers between devices  13 us (25%)
  Pallas kernels  8.71 us (17%)
  waiting for transfers between devices  6.99 us (13%)
  other arithmetic  4.37 us (8%)
  local copies, waits for them, and re-layouts  3.84 us (7%)
    all_to_all x1, blocking collectives, per_device(): summed = jnp.sum(lax.all_to_all(part, 'epoch', 0, 0, tiled=True), axis=0)  15.2 us
    ppermute x1, starting transfers between devices, per_device(): from_below = lax.ppermute(top, 'tile', backward)  11.1 us
    pallas_call x1, Pallas kernels, partial_stacks(): pl.pallas_call(stack_kernel, out_shape=(jax.ShapeDtypeStruct((vels, rows,...  8.71 us
    ppermute x1, waiting for transfers between devices, per_device(): from_above = lax.ppermute(bottom, 'tile', forward)  5.13 us
    ppermute x1, starting transfers between devices, per_device(): from_above = lax.ppermute(bottom, 'tile', forward)  1.91 us
    ppermute x1, waiting for transfers between devices, per_device(): from_below = lax.ppermute(top, 'tile', backward)  1.86 us
    another operation x2, local copies, waits for them, and re-layouts, per_device(): stacked = jnp.stack([psi, phi]).reshape(2, epochs, rows, blocks, LANES)  1.66 us
    another operation x1, other arithmetic, per_device(): stacked = jnp.stack([psi, phi]).reshape(2, epochs, rows, blocks, LANES)  1.52 us
  transfers between devices with their start and end apart: 2, of which 2 were waited for; matrix products, arithmetic and copies ran while one was open for 0% of the time, Pallas kernels for 0%

profile of v7, /device:TPU:6, one launch (start us, length us, event | category | flops | bytes accessed | tf_op | source)
XLA Modules:
  0.0 52.2 jit_solution(301211701382094938)
XLA Ops:
  0.0 0.0 copy-start
  0.0 0.9 %copy.9 = s32[8,48,2]{2,1,0:T(8,128)S(1)} copy(s32[8,48,2]{1,2,0:T(2,128)} %param.5) | data formatting | bytes 6144 | tf_op args[2]
  0.9 0.7 %reshape.16.sh_ref = s32[768]{0:T(1024)} reshape(s32[8,48,2]{2,1,0:T(8,128)S(1)} %copy.9) | data formatting | bytes 6144 | tf_op jit(solution)/shard_map/reshape | solution.py:75
  1.6 1.4 %stack.9 = f32[1,12,32,4,128]{4,3,2,1,0:T(4,128)S(1)} reshape(f32[12,32,512]{2,1,0:T(8,128)} %param.3) | data formatting | bytes 1572864 | tf_op jit(solution)/shard_map/stack | solution.py:81
  3.0 0.0 copy-done
  3.0 0.3 stack.10
  3.3 1.5 %pad_maximum_fusion = f32[2,12,32,4,128]{4,3,0,2,1:T(4,128)} fusion(f32[1,12,32,4,128]{4,3,0,2,1:T(4,128)S(1)} %bitcast.13, f32[1,12,32,4,128]{4,3,0,2,1:T(4,128)S(1)} %bitcast.12), kind=kLoop, calls=%fused_computation | loop fusion | flops 393216 | bytes 3145728 | tf_op jit(solution)/shard_map/stack | solution.py:81
  4.9 8.7 %shard_map.37 = (f32[8,32,8,128]{3,2,1,0:T(8,128)}, f32[8,16,8,128]{3,2,1,0:T(8,128)}, f32[8,16,8,128]{3,2,1,0:T(8,128)}) custom-call(s32[768]{0:T(1024)} %reshape.16.sh_ref, f32[12,32,8,128]{3,2,1,0:T(8,128)} %bitcast.9), custom_call_target="tpu_custom_call" | custom-call | flops 6291456 | bytes 3670016 | tf_op jit(solution)/shard_map/pallas_call | solution.py:64
  13.6 1.9 %collective-permute-start = (f32[8,16,8,128]{3,2,1,0:T(8,128)}, f32[8,16,8,128]{3,2,1,0:T(8,128)S(1)}, u32[]{:S(2)}, u32[]{:S(2)}) collective-permute-start(f32[8,16,8,128]{3,2,1,0:T(8,128)} %get-tuple-element.9), channel_id=1, source_target_pairs={{0,4},{4,8},{8,12},{12,16},{16,20},{20,24},{24,28},{28,32},{32,36}... | collective-permute-start | bytes 1572872 | tf_op jit(solution)/shard_map/ppermute | solution.py:87
  15.5 11.1 %collective-permute-start.1 = (f32[8,16,8,128]{3,2,1,0:T(8,128)}, f32[8,16,8,128]{3,2,1,0:T(8,128)S(1)}, u32[]{:S(2)}, u32[]{:S(2)}) collective-permute-start(f32[8,16,8,128]{3,2,1,0:T(8,128)} %get-tuple-element.10), channel_id=1, source_target_pairs={{4,0},{8,4},{12,8},{16,12},{20,16},{24,20},{28,24},{32,28},{36,32}... | collective-permute-start | bytes 1572872 | tf_op jit(solution)/shard_map/ppermute | solution.py:88
  26.6 5.1 %collective-permute-done = f32[8,16,8,128]{3,2,1,0:T(8,128)S(1)} collective-permute-done((f32[8,16,8,128]{3,2,1,0:T(8,128)}, f32[8,16,8,128]{3,2,1,0:T(8,128)S(1)}, u32[]{:S(2)}, u32[]{:S(2)}) %collective-permute-start) | collective-permute-done | bytes 524320 | tf_op jit(solution)/shard_map/ppermute | solution.py:87
  31.7 1.9 %collective-permute-done.1 = f32[8,16,8,128]{3,2,1,0:T(8,128)S(1)} collective-permute-done((f32[8,16,8,128]{3,2,1,0:T(8,128)}, f32[8,16,8,128]{3,2,1,0:T(8,128)S(1)}, u32[]{:S(2)}, u32[]{:S(2)}) %collective-permute-start.1) | collective-permute-done | bytes 524320 | tf_op jit(solution)/shard_map/ppermute | solution.py:88
  33.6 1.4 %maximum_add_fusion = f32[8,32,8,128]{3,2,1,0:T(8,128)S(1)} fusion(f32[8,32,8,128]{3,2,1,0:T(8,128)} %get-tuple-element.8, f32[8,16,8,128]{3,2,1,0:T(8,128)S(1)} %collective-permute-done.1, f32[8,16,8,128]{3,2,1,0:T(8,128)S(1)} %collective-permute-done), kind=kLoop, calls=%fused_computation.1 | loop fusion | flops 524288 | bytes 3145728 | tf_op jit(solution)/shard_map/add | solution.py:91
  35.0 0.5 %copy.18 = f32[8,32,2,4,128]{4,2,1,0,3:T(2,128)S(1)} copy(f32[8,32,2,4,128]{4,3,2,1,0:T(4,128)S(1)} %bitcast.10) | data formatting | bytes 2097152 | tf_op jit(solution)/shard_map/reshape | solution.py:92
  35.5 15.2 %all_to_all.5 = f32[4,8,2,32,128]{4,2,3,1,0:T(2,128)S(1)} all-to-all(f32[4,8,2,32,128]{4,2,3,1,0:T(2,128)S(1)} %bitcast.11), channel_id=1, replica_groups=mesh['tile'=128,'epoch'=4] {'epoch'}, dimensions={0} | all-to-all | bytes 2097152 | tf_op jit(solution)/shard_map/all_to_all | solution.py:93
  50.7 0.6 %reduce_sum.9 = f32[8,2,32,128]{3,1,2,0:T(2,128)S(1)} reduce(f32[4,8,2,32,128]{4,2,3,1,0:T(2,128)S(1)} %all_to_all.5, f32[]{:T(128)} %constant.0.clone.1), dimensions={0}, to_apply=%region_0.0 | reduce | flops 196608 | bytes 1310724 | tf_op jit(solution)/shard_map/reduce_sum | solution.py:93
  51.3 0.8 %fusion.1 = f32[32,128]{1,0:T(8,128)} fusion(f32[8,2,32,128]{3,1,2,0:T(2,128)S(1)} %reduce_sum.9), kind=kLoop, calls=%fused_computation.5 | loop fusion | flops 61440 | bytes 278528 | tf_op jit(solution)/shard_map/reduce_max | solution.py:95
Async XLA Ops:
  0.0 3.0 %copy-start = (f32[12,32,512]{2,1,0:T(8,128)S(1)}, f32[12,32,512]{2,1,0:T(8,128)}, u32[]{:S(2)}) copy-start(f32[12,32,512]{2,1,0:T(8,128)} %param.4) | copy-start | bytes 2359300
  13.6 18.2 %collective-permute-start = (f32[8,16,8,128]{3,2,1,0:T(8,128)}, f32[8,16,8,128]{3,2,1,0:T(8,128)S(1)}, u32[]{:S(2)}, u32[]{:S(2)}) collective-permute-start(f32[8,16,8,128]{3,2,1,0:T(8,128)} %get-tuple-element.9), channel_id=1, source_target_pairs={{0,4},{4,8},{8,12},{12,16},{16,20},{20,24},{24,28},{28,32},{32,36}... | collective-permute-start | bytes 1572872 | tf_op jit(solution)/shard_map/ppermute | solution.py:87
  15.5 18.1 %collective-permute-start.1 = (f32[8,16,8,128]{3,2,1,0:T(8,128)}, f32[8,16,8,128]{3,2,1,0:T(8,128)S(1)}, u32[]{:S(2)}, u32[]{:S(2)}) collective-permute-start(f32[8,16,8,128]{3,2,1,0:T(8,128)} %get-tuple-element.10), channel_id=1, source_target_pairs={{4,0},{8,4},{12,8},{16,12},{20,16},{24,20},{28,24},{32,28},{36,32}... | collective-permute-start | bytes 1572872 | tf_op jit(solution)/shard_map/ppermute | solution.py:88

commit v8 on v7

v8 whole, which is shorter than its diff:
```python
import jax
import jax.numpy as jnp
from jax import lax
from jax.experimental import pallas as pl
from jax.experimental.pallas import tpu as pltpu
from jax.sharding import PartitionSpec as P

HALO = 16
LANES = 128
CHUNK = 8


def stack_kernel(sh_ref, x_ref, own_ref, top_ref, bottom_ref, acc_ref):
    epochs, rows, slots, lanes = x_ref.shape
    blocks = slots // 2
    vels = acc_ref.shape[0]
    first = lax.axis_index("epoch") * epochs

    acc_ref[...] = jnp.zeros(acc_ref.shape, jnp.float32)
    lane = lax.broadcasted_iota(jnp.int32, (slots, lanes), 1)
    block = lax.broadcasted_iota(jnp.int32, (slots, lanes), 0) % blocks

    def add_epoch(v, e):
        s_r = sh_ref[v, first + e, 0]
        s_c = sh_ref[v, first + e, 1]
        amount = lax.rem(lanes - s_c, lanes)
        moved = lane + s_c
        inside = (moved >= 0) & (moved < lanes)
        step = jnp.where(s_c >= 0, slots - 1, 1)
        edge = jnp.where(s_c >= 0, blocks - 1, 0)
        edge_ok = (block != edge) & ~inside
        for rc in range(rows // CHUNK):
            win = x_ref[e, rc * CHUNK : (rc + 1) * CHUNK]
            rolled = pltpu.roll(win, amount, axis=2)
            other = pltpu.roll(rolled, step, axis=1)
            picked = jnp.where(inside[None], rolled, jnp.where(edge_ok[None], other, 0.0))
            dest = acc_ref.at[v, pl.ds(HALO - s_r + rc * CHUNK, CHUNK)]
            dest[...] = dest[...] + picked

    def body(e, carry):
        for v in range(vels):
            add_epoch(v, e)
        return carry

    lax.fori_loop(0, epochs, body, 0)
    for v in range(vels):
        top_ref[v] = acc_ref[v, :HALO]
        own_ref[v] = acc_ref[v, HALO : HALO + rows]
        bottom_ref[v] = acc_ref[v, HALO + rows :]


def partial_stacks(shifts, x):
    epochs, rows, slots, lanes = x.shape
    vels = shifts.shape[0]
    vmem = pl.BlockSpec(memory_space=pltpu.VMEM)
    spill = jax.ShapeDtypeStruct((vels, HALO, slots, lanes), jnp.float32)
    return pl.pallas_call(
        stack_kernel,
        out_shape=(jax.ShapeDtypeStruct((vels, rows, slots, lanes), jnp.float32), spill, spill),
        in_specs=[pl.BlockSpec(memory_space=pltpu.SMEM), vmem],
        out_specs=(vmem, vmem, vmem),
        scratch_shapes=[pltpu.VMEM((vels, rows + 2 * HALO, slots, lanes), jnp.float32)],
        cost_estimate=pl.CostEstimate(
            flops=2 * vels * epochs * rows * slots * lanes,
            bytes_accessed=4 * (epochs * rows + vels * (rows + 2 * HALO)) * slots * lanes,
            transcendentals=0,
        ),
    )(shifts, x)


def per_device(psi, phi, shifts):
    epochs, rows, cols = psi.shape
    blocks = cols // LANES
    stacked = jnp.stack([psi, phi]).reshape(2, epochs, rows, blocks, LANES)
    x = stacked.transpose(1, 2, 0, 3, 4).reshape(epochs, rows, 2 * blocks, LANES)
    own, top, bottom = partial_stacks(shifts, x)
    count = lax.axis_size("tile")
    forward = [(i, i + 1) for i in range(count - 1)]
    backward = [(i + 1, i) for i in range(count - 1)]
    from_above = lax.ppermute(bottom, "tile", forward)
    from_below = lax.ppermute(top, "tile", backward)
    vels = own.shape[0]
    middle = jnp.zeros((vels, rows - 2 * HALO) + own.shape[2:], jnp.float32)
    part = own + jnp.concatenate([from_above, middle, from_below], axis=1)
    part = part.reshape(vels, rows, 2, blocks, LANES).transpose(3, 0, 2, 1, 4)
    summed = jnp.sum(lax.all_to_all(part, "epoch", 0, 0, tiled=True), axis=0)
    ratio = summed[:, 0] / jnp.sqrt(summed[:, 1])
    return jnp.max(ratio, axis=0)


def solution(mesh):
    placed = (P("epoch", "tile", None), P("epoch", "tile", None), P())
    return jax.shard_map(
        per_device, mesh=mesh, in_specs=placed, out_specs=P("tile", "epoch"), check_vma=False
    )
```

time: 52.4 us -> 53.2 us (1.015)
  Pallas kernels: 8.71 us -> 9.53 us
    pallas_call x1, Pallas kernels: 8.71 us -> 9.53 us  [partial_stacks(): pl.pallas_call(stack_kernel, out_shape=(jax.ShapeDtypeStruct((vels, rows,...]
    reshape x1 -> x0, local copies, waits for them, and re-layouts: 0.74 us -> none  [partial_stacks(): shifts.reshape(-1)]
    unnamed x3, local copies, waits for them, and re-layouts: 0.9 us -> 1.6 us
where the time goes in v8:
time: 53.2 us; the launch traced here: 52.9 us
  blocking collectives  15.2 us (29%)
  starting transfers between devices  13 us (24%)
  Pallas kernels  9.53 us (18%)
  waiting for transfers between devices  6.99 us (13%)
  other arithmetic  4.37 us (8%)
  local copies, waits for them, and re-layouts  3.8 us (7%)
    all_to_all x1, blocking collectives, per_device(): summed = jnp.sum(lax.all_to_all(part, 'epoch', 0, 0, tiled=True), axis=0)  15.2 us
    ppermute x1, starting transfers between devices, per_device(): from_below = lax.ppermute(top, 'tile', backward)  11.1 us
    pallas_call x1, Pallas kernels, partial_stacks(): pl.pallas_call(stack_kernel, out_shape=(jax.ShapeDtypeStruct((vels, rows,...  9.53 us
    ppermute x1, waiting for transfers between devices, per_device(): from_above = lax.ppermute(bottom, 'tile', forward)  5.13 us
    ppermute x1, starting transfers between devices, per_device(): from_above = lax.ppermute(bottom, 'tile', forward)  1.91 us
    ppermute x1, waiting for transfers between devices, per_device(): from_below = lax.ppermute(top, 'tile', backward)  1.86 us
    another operation x2, local copies, waits for them, and re-layouts, per_device(): stacked = jnp.stack([psi, phi]).reshape(2, epochs, rows, blocks, LANES)  1.66 us
    unnamed x3, local copies, waits for them, and re-layouts  1.6 us
  transfers between devices with their start and end apart: 2, of which 2 were waited for; matrix products, arithmetic and copies ran while one was open for 0% of the time, Pallas kernels for 0%

profile of v8, /device:TPU:6, one launch (start us, length us, event | category | flops | bytes accessed | tf_op | source)
XLA Modules:
  0.0 52.9 jit_solution(6511461595108444736)
XLA Ops:
  0.0 0.0 copy-start
  0.0 1.6 %copy.9.sh_ref = s32[8,48,2]{2,1,0:T(8,128)} copy(s32[8,48,2]{1,2,0:T(2,128)} %param.5) | data formatting | bytes 6144 | tf_op args[2]
  1.6 1.4 %stack.9 = f32[1,12,32,4,128]{4,3,2,1,0:T(4,128)S(1)} reshape(f32[12,32,512]{2,1,0:T(8,128)} %param.3) | data formatting | bytes 1572864 | tf_op jit(solution)/shard_map/stack | solution.py:74
  3.0 0.0 copy-done
  3.0 0.3 stack.10
  3.3 1.5 %pad_maximum_fusion = f32[2,12,32,4,128]{4,3,0,2,1:T(4,128)} fusion(f32[1,12,32,4,128]{4,3,0,2,1:T(4,128)S(1)} %bitcast.13, f32[1,12,32,4,128]{4,3,0,2,1:T(4,128)S(1)} %bitcast.12), kind=kLoop, calls=%fused_computation | loop fusion | flops 393216 | bytes 3145728 | tf_op jit(solution)/shard_map/stack | solution.py:74
  4.8 9.5 %shard_map.37 = (f32[8,32,8,128]{3,2,1,0:T(8,128)}, f32[8,16,8,128]{3,2,1,0:T(8,128)}, f32[8,16,8,128]{3,2,1,0:T(8,128)}) custom-call(s32[8,48,2]{2,1,0:T(8,128)} %copy.9.sh_ref, f32[12,32,8,128]{3,2,1,0:T(8,128)} %bitcast.9), custom_call_target="tpu_custom_call" | custom-call | flops 6291456 | bytes 3670016 | tf_op jit(solution)/shard_map/pallas_call | solution.py:57
  14.3 1.9 %collective-permute-start = (f32[8,16,8,128]{3,2,1,0:T(8,128)}, f32[8,16,8,128]{3,2,1,0:T(8,128)S(1)}, u32[]{:S(2)}, u32[]{:S(2)}) collective-permute-start(f32[8,16,8,128]{3,2,1,0:T(8,128)} %get-tuple-element.9), channel_id=1, source_target_pairs={{0,4},{4,8},{8,12},{12,16},{16,20},{20,24},{24,28},{28,32},{32,36}... | collective-permute-start | bytes 1572872 | tf_op jit(solution)/shard_map/ppermute | solution.py:80
  16.3 11.1 %collective-permute-start.1 = (f32[8,16,8,128]{3,2,1,0:T(8,128)}, f32[8,16,8,128]{3,2,1,0:T(8,128)S(1)}, u32[]{:S(2)}, u32[]{:S(2)}) collective-permute-start(f32[8,16,8,128]{3,2,1,0:T(8,128)} %get-tuple-element.10), channel_id=1, source_target_pairs={{4,0},{8,4},{12,8},{16,12},{20,16},{24,20},{28,24},{32,28},{36,32}... | collective-permute-start | bytes 1572872 | tf_op jit(solution)/shard_map/ppermute | solution.py:81
  27.4 5.1 %collective-permute-done = f32[8,16,8,128]{3,2,1,0:T(8,128)S(1)} collective-permute-done((f32[8,16,8,128]{3,2,1,0:T(8,128)}, f32[8,16,8,128]{3,2,1,0:T(8,128)S(1)}, u32[]{:S(2)}, u32[]{:S(2)}) %collective-permute-start) | collective-permute-done | bytes 524320 | tf_op jit(solution)/shard_map/ppermute | solution.py:80
  32.5 1.9 %collective-permute-done.1 = f32[8,16,8,128]{3,2,1,0:T(8,128)S(1)} collective-permute-done((f32[8,16,8,128]{3,2,1,0:T(8,128)}, f32[8,16,8,128]{3,2,1,0:T(8,128)S(1)}, u32[]{:S(2)}, u32[]{:S(2)}) %collective-permute-start.1) | collective-permute-done | bytes 524320 | tf_op jit(solution)/shard_map/ppermute | solution.py:81
  34.4 1.4 %maximum_add_fusion = f32[8,32,8,128]{3,2,1,0:T(8,128)S(1)} fusion(f32[8,32,8,128]{3,2,1,0:T(8,128)} %get-tuple-element.8, f32[8,16,8,128]{3,2,1,0:T(8,128)S(1)} %collective-permute-done.1, f32[8,16,8,128]{3,2,1,0:T(8,128)S(1)} %collective-permute-done), kind=kLoop, calls=%fused_computation.1 | loop fusion | flops 524288 | bytes 3145728 | tf_op jit(solution)/shard_map/add | solution.py:84
  35.8 0.5 %copy.16 = f32[8,32,2,4,128]{4,2,1,0,3:T(2,128)S(1)} copy(f32[8,32,2,4,128]{4,3,2,1,0:T(4,128)S(1)} %bitcast.10) | data formatting | bytes 2097152 | tf_op jit(solution)/shard_map/reshape | solution.py:85
  36.3 15.2 %all_to_all.5 = f32[4,8,2,32,128]{4,2,3,1,0:T(2,128)S(1)} all-to-all(f32[4,8,2,32,128]{4,2,3,1,0:T(2,128)S(1)} %bitcast.11), channel_id=1, replica_groups=mesh['tile'=128,'epoch'=4] {'epoch'}, dimensions={0} | all-to-all | bytes 2097152 | tf_op jit(solution)/shard_map/all_to_all | solution.py:86
  51.5 0.6 %reduce_sum.9 = f32[8,2,32,128]{3,1,2,0:T(2,128)S(1)} reduce(f32[4,8,2,32,128]{4,2,3,1,0:T(2,128)S(1)} %all_to_all.5, f32[]{:T(128)} %constant.0.clone.1), dimensions={0}, to_apply=%region_0.0 | reduce | flops 196608 | bytes 1310724 | tf_op jit(solution)/shard_map/reduce_sum | solution.py:86
  52.1 0.8 %fusion.1 = f32[32,128]{1,0:T(8,128)} fusion(f32[8,2,32,128]{3,1,2,0:T(2,128)S(1)} %reduce_sum.9), kind=kLoop, calls=%fused_computation.5 | loop fusion | flops 61440 | bytes 278528 | tf_op jit(solution)/shard_map/reduce_max | solution.py:88
Async XLA Ops:
  0.0 3.0 %copy-start = (f32[12,32,512]{2,1,0:T(8,128)S(1)}, f32[12,32,512]{2,1,0:T(8,128)}, u32[]{:S(2)}) copy-start(f32[12,32,512]{2,1,0:T(8,128)} %param.4) | copy-start | bytes 2359300
  14.3 18.2 %collective-permute-start = (f32[8,16,8,128]{3,2,1,0:T(8,128)}, f32[8,16,8,128]{3,2,1,0:T(8,128)S(1)}, u32[]{:S(2)}, u32[]{:S(2)}) collective-permute-start(f32[8,16,8,128]{3,2,1,0:T(8,128)} %get-tuple-element.9), channel_id=1, source_target_pairs={{0,4},{4,8},{8,12},{12,16},{16,20},{20,24},{24,28},{28,32},{32,36}... | collective-permute-start | bytes 1572872 | tf_op jit(solution)/shard_map/ppermute | solution.py:80
  16.3 18.1 %collective-permute-start.1 = (f32[8,16,8,128]{3,2,1,0:T(8,128)}, f32[8,16,8,128]{3,2,1,0:T(8,128)S(1)}, u32[]{:S(2)}, u32[]{:S(2)}) collective-permute-start(f32[8,16,8,128]{3,2,1,0:T(8,128)} %get-tuple-element.10), channel_id=1, source_target_pairs={{4,0},{8,4},{12,8},{16,12},{20,16},{24,20},{28,24},{32,28},{36,32}... | collective-permute-start | bytes 1572872 | tf_op jit(solution)/shard_map/ppermute | solution.py:81

commit v9 on v7

--- a/solution.py
+++ b/solution.py
@@ -15,7 +15,6 @@
     blocks = slots // 2
     chains = acc_ref.shape[0]
     vels = acc_ref.shape[1]
-    total = sh_ref.shape[0] // (2 * vels)
     first = lax.axis_index("epoch") * epochs
 
     acc_ref[...] = jnp.zeros(acc_ref.shape, jnp.float32)
@@ -24,9 +23,8 @@
     for v in range(vels):
 
         def add_epoch(v, e, into):
-            at = (v * total + first + e) * 2
-            s_r = sh_ref[at]
-            s_c = sh_ref[at + 1]
+            s_r = sh_ref[v, first + e, 0]
+            s_c = sh_ref[v, first + e, 1]
             amount = lax.rem(lanes - s_c, lanes)
             moved = lane + s_c
             inside = (moved >= 0) & (moved < lanes)
@@ -72,7 +70,7 @@
             bytes_accessed=4 * (epochs * rows + vels * (rows + 2 * HALO)) * slots * lanes,
             transcendentals=0,
         ),
-    )(shifts.reshape(-1), x)
+    )(shifts, x)
 
 
 def per_device(psi, phi, shifts):

time: 52.4 us -> 54.9 us (1.048)
  Pallas kernels: 8.71 us -> 11.2 us
    pallas_call x1, Pallas kernels: 8.71 us -> 11.2 us  [partial_stacks(): pl.pallas_call(stack_kernel, out_shape=(jax.ShapeDtypeStruct((vels, rows,...]
    reshape x1 -> x0, local copies, waits for them, and re-layouts: 0.74 us -> none  [partial_stacks(): shifts.reshape(-1)]
    unnamed x3, local copies, waits for them, and re-layouts: 0.9 us -> 1.6 us
where the time goes in v9:
time: 54.9 us; the launch traced here: 54.6 us
  blocking collectives  15.2 us (28%)
  starting transfers between devices  13 us (24%)
  Pallas kernels  11.2 us (20%)
  waiting for transfers between devices  6.99 us (13%)
  other arithmetic  4.37 us (8%)
  local copies, waits for them, and re-layouts  3.8 us (7%)
    all_to_all x1, blocking collectives, per_device(): summed = jnp.sum(lax.all_to_all(part, 'epoch', 0, 0, tiled=True), axis=0)  15.2 us
    pallas_call x1, Pallas kernels, partial_stacks(): pl.pallas_call(stack_kernel, out_shape=(jax.ShapeDtypeStruct((vels, rows,...  11.2 us
    ppermute x1, starting transfers between devices, per_device(): from_below = lax.ppermute(top, 'tile', backward)  11.1 us
    ppermute x1, waiting for transfers between devices, per_device(): from_above = lax.ppermute(bottom, 'tile', forward)  5.13 us
    ppermute x1, starting transfers between devices, per_device(): from_above = lax.ppermute(bottom, 'tile', forward)  1.91 us
    ppermute x1, waiting for transfers between devices, per_device(): from_below = lax.ppermute(top, 'tile', backward)  1.86 us
    another operation x2, local copies, waits for them, and re-layouts, per_device(): stacked = jnp.stack([psi, phi]).reshape(2, epochs, rows, blocks, LANES)  1.66 us
    unnamed x3, local copies, waits for them, and re-layouts  1.6 us
  transfers between devices with their start and end apart: 2, of which 2 were waited for; matrix products, arithmetic and copies ran while one was open for 0% of the time, Pallas kernels for 0%

profile of v9, /device:TPU:6, one launch (start us, length us, event | category | flops | bytes accessed | tf_op | source)
XLA Modules:
  0.0 54.6 jit_solution(4734363824917819297)
XLA Ops:
  0.0 0.0 copy-start
  0.0 1.6 %copy.9.sh_ref = s32[8,48,2]{2,1,0:T(8,128)} copy(s32[8,48,2]{1,2,0:T(2,128)} %param.5) | data formatting | bytes 6144 | tf_op args[2]
  1.6 1.4 %stack.9 = f32[1,12,32,4,128]{4,3,2,1,0:T(4,128)S(1)} reshape(f32[12,32,512]{2,1,0:T(8,128)} %param.3) | data formatting | bytes 1572864 | tf_op jit(solution)/shard_map/stack | solution.py:79
  3.0 0.0 copy-done
  3.0 0.3 stack.10
  3.3 1.5 %pad_maximum_fusion = f32[2,12,32,4,128]{4,3,0,2,1:T(4,128)} fusion(f32[1,12,32,4,128]{4,3,0,2,1:T(4,128)S(1)} %bitcast.13, f32[1,12,32,4,128]{4,3,0,2,1:T(4,128)S(1)} %bitcast.12), kind=kLoop, calls=%fused_computation | loop fusion | flops 393216 | bytes 3145728 | tf_op jit(solution)/shard_map/stack | solution.py:79
  4.8 11.2 %shard_map.37 = (f32[8,32,8,128]{3,2,1,0:T(8,128)}, f32[8,16,8,128]{3,2,1,0:T(8,128)}, f32[8,16,8,128]{3,2,1,0:T(8,128)}) custom-call(s32[8,48,2]{2,1,0:T(8,128)} %copy.9.sh_ref, f32[12,32,8,128]{3,2,1,0:T(8,128)} %bitcast.9), custom_call_target="tpu_custom_call" | custom-call | flops 6291456 | bytes 3670016 | tf_op jit(solution)/shard_map/pallas_call | solution.py:62
  16.0 1.9 %collective-permute-start = (f32[8,16,8,128]{3,2,1,0:T(8,128)}, f32[8,16,8,128]{3,2,1,0:T(8,128)S(1)}, u32[]{:S(2)}, u32[]{:S(2)}) collective-permute-start(f32[8,16,8,128]{3,2,1,0:T(8,128)} %get-tuple-element.9), channel_id=1, source_target_pairs={{0,4},{4,8},{8,12},{12,16},{16,20},{20,24},{24,28},{28,32},{32,36}... | collective-permute-start | bytes 1572872 | tf_op jit(solution)/shard_map/ppermute | solution.py:85
  17.9 11.1 %collective-permute-start.1 = (f32[8,16,8,128]{3,2,1,0:T(8,128)}, f32[8,16,8,128]{3,2,1,0:T(8,128)S(1)}, u32[]{:S(2)}, u32[]{:S(2)}) collective-permute-start(f32[8,16,8,128]{3,2,1,0:T(8,128)} %get-tuple-element.10), channel_id=1, source_target_pairs={{4,0},{8,4},{12,8},{16,12},{20,16},{24,20},{28,24},{32,28},{36,32}... | collective-permute-start | bytes 1572872 | tf_op jit(solution)/shard_map/ppermute | solution.py:86
  29.0 5.1 %collective-permute-done = f32[8,16,8,128]{3,2,1,0:T(8,128)S(1)} collective-permute-done((f32[8,16,8,128]{3,2,1,0:T(8,128)}, f32[8,16,8,128]{3,2,1,0:T(8,128)S(1)}, u32[]{:S(2)}, u32[]{:S(2)}) %collective-permute-start) | collective-permute-done | bytes 524320 | tf_op jit(solution)/shard_map/ppermute | solution.py:85
  34.2 1.9 %collective-permute-done.1 = f32[8,16,8,128]{3,2,1,0:T(8,128)S(1)} collective-permute-done((f32[8,16,8,128]{3,2,1,0:T(8,128)}, f32[8,16,8,128]{3,2,1,0:T(8,128)S(1)}, u32[]{:S(2)}, u32[]{:S(2)}) %collective-permute-start.1) | collective-permute-done | bytes 524320 | tf_op jit(solution)/shard_map/ppermute | solution.py:86
  36.0 1.4 %maximum_add_fusion = f32[8,32,8,128]{3,2,1,0:T(8,128)S(1)} fusion(f32[8,32,8,128]{3,2,1,0:T(8,128)} %get-tuple-element.8, f32[8,16,8,128]{3,2,1,0:T(8,128)S(1)} %collective-permute-done.1, f32[8,16,8,128]{3,2,1,0:T(8,128)S(1)} %collective-permute-done), kind=kLoop, calls=%fused_computation.1 | loop fusion | flops 524288 | bytes 3145728 | tf_op jit(solution)/shard_map/add | solution.py:89
  37.4 0.5 copy.16
  38.0 15.2 %all_to_all.5 = f32[4,8,2,32,128]{4,2,3,1,0:T(2,128)S(1)} all-to-all(f32[4,8,2,32,128]{4,2,3,1,0:T(2,128)S(1)} %bitcast.11), channel_id=1, replica_groups=mesh['tile'=128,'epoch'=4] {'epoch'}, dimensions={0} | all-to-all | bytes 2097152 | tf_op jit(solution)/shard_map/all_to_all | solution.py:91
  53.1 0.6 %reduce_sum.9 = f32[8,2,32,128]{3,1,2,0:T(2,128)S(1)} reduce(f32[4,8,2,32,128]{4,2,3,1,0:T(2,128)S(1)} %all_to_all.5, f32[]{:T(128)} %constant.0.clone.1), dimensions={0}, to_apply=%region_0.0 | reduce | flops 196608 | bytes 1310724 | tf_op jit(solution)/shard_map/reduce_sum | solution.py:91
  53.8 0.8 %fusion.1 = f32[32,128]{1,0:T(8,128)} fusion(f32[8,2,32,128]{3,1,2,0:T(2,128)S(1)} %reduce_sum.9), kind=kLoop, calls=%fused_computation.5 | loop fusion | flops 61440 | bytes 278528 | tf_op jit(solution)/shard_map/reduce_max | solution.py:93
Async XLA Ops:
  0.0 3.0 %copy-start = (f32[12,32,512]{2,1,0:T(8,128)S(1)}, f32[12,32,512]{2,1,0:T(8,128)}, u32[]{:S(2)}) copy-start(f32[12,32,512]{2,1,0:T(8,128)} %param.4) | copy-start | bytes 2359300
  16.0 18.2 %collective-permute-start = (f32[8,16,8,128]{3,2,1,0:T(8,128)}, f32[8,16,8,128]{3,2,1,0:T(8,128)S(1)}, u32[]{:S(2)}, u32[]{:S(2)}) collective-permute-start(f32[8,16,8,128]{3,2,1,0:T(8,128)} %get-tuple-element.9), channel_id=1, source_target_pairs={{0,4},{4,8},{8,12},{12,16},{16,20},{20,24},{24,28},{28,32},{32,36}... | collective-permute-start | bytes 1572872 | tf_op jit(solution)/shard_map/ppermute | solution.py:85
  17.9 18.1 %collective-permute-start.1 = (f32[8,16,8,128]{3,2,1,0:T(8,128)}, f32[8,16,8,128]{3,2,1,0:T(8,128)S(1)}, u32[]{:S(2)}, u32[]{:S(2)}) collective-permute-start(f32[8,16,8,128]{3,2,1,0:T(8,128)} %get-tuple-element.10), channel_id=1, source_target_pairs={{4,0},{8,4},{12,8},{16,12},{20,16},{24,20},{28,24},{32,28},{36,32}... | collective-permute-start | bytes 1572872 | tf_op jit(solution)/shard_map/ppermute | solution.py:86

commit v10 on v8

--- a/solution.py
+++ b/solution.py
@@ -14,6 +14,7 @@
     epochs, rows, slots, lanes = x_ref.shape
     blocks = slots // 2
     vels = acc_ref.shape[0]
+    total = sh_ref.shape[0] // (2 * vels)
     first = lax.axis_index("epoch") * epochs
 
     acc_ref[...] = jnp.zeros(acc_ref.shape, jnp.float32)
@@ -21,8 +22,9 @@
     block = lax.broadcasted_iota(jnp.int32, (slots, lanes), 0) % blocks
 
     def add_epoch(v, e):
-        s_r = sh_ref[v, first + e, 0]
-        s_c = sh_ref[v, first + e, 1]
+        at = (v * total + first + e) * 2
+        s_r = sh_ref[at]
+        s_c = sh_ref[at + 1]
         amount = lax.rem(lanes - s_c, lanes)
         moved = lane + s_c
         inside = (moved >= 0) & (moved < lanes)
@@ -65,7 +67,7 @@
             bytes_accessed=4 * (epochs * rows + vels * (rows + 2 * HALO)) * slots * lanes,
             transcendentals=0,
         ),
-    )(shifts, x)
+    )(shifts.reshape(-1), x)
 
 
 def per_device(psi, phi, shifts):

time: 53.2 us -> 50.8 us (0.955)
  Pallas kernels: 9.53 us -> 7.06 us
    pallas_call x1, Pallas kernels: 9.53 us -> 7.06 us  [partial_stacks(): pl.pallas_call(stack_kernel, out_shape=(jax.ShapeDtypeStruct((vels, rows,...]
    reshape x0 -> x1, local copies, waits for them, and re-layouts: none -> 0.74 us  [partial_stacks(): shifts.reshape(-1)]
    unnamed x3, local copies, waits for them, and re-layouts: 1.6 us -> 0.9 us
where the time goes in v10:
time: 50.8 us; the launch traced here: 50.5 us
  blocking collectives  15.2 us (30%)
  starting transfers between devices  13 us (26%)
  Pallas kernels  7.06 us (14%)
  waiting for transfers between devices  6.99 us (14%)
  other arithmetic  4.37 us (9%)
  local copies, waits for them, and re-layouts  3.84 us (8%)
    all_to_all x1, blocking collectives, per_device(): summed = jnp.sum(lax.all_to_all(part, 'epoch', 0, 0, tiled=True), axis=0)  15.2 us
    ppermute x1, starting transfers between devices, per_device(): from_below = lax.ppermute(top, 'tile', backward)  11.1 us
    pallas_call x1, Pallas kernels, partial_stacks(): pl.pallas_call(stack_kernel, out_shape=(jax.ShapeDtypeStruct((vels, rows,...  7.06 us
    ppermute x1, waiting for transfers between devices, per_device(): from_above = lax.ppermute(bottom, 'tile', forward)  5.13 us
    ppermute x1, starting transfers between devices, per_device(): from_above = lax.ppermute(bottom, 'tile', forward)  1.91 us
    ppermute x1, waiting for transfers between devices, per_device(): from_below = lax.ppermute(top, 'tile', backward)  1.86 us
    another operation x2, local copies, waits for them, and re-layouts, per_device(): stacked = jnp.stack([psi, phi]).reshape(2, epochs, rows, blocks, LANES)  1.66 us
    another operation x1, other arithmetic, per_device(): stacked = jnp.stack([psi, phi]).reshape(2, epochs, rows, blocks, LANES)  1.52 us
  transfers between devices with their start and end apart: 2, of which 2 were waited for; matrix products, arithmetic and copies ran while one was open for 0% of the time, Pallas kernels for 0%

profile of v10, /device:TPU:6, one launch (start us, length us, event | category | flops | bytes accessed | tf_op | source)
XLA Modules:
  0.0 50.5 jit_solution(5603318136443899025)
XLA Ops:
  0.0 0.0 copy-start
  0.0 0.9 %copy.9 = s32[8,48,2]{2,1,0:T(8,128)S(1)} copy(s32[8,48,2]{1,2,0:T(2,128)} %param.5) | data formatting | bytes 6144 | tf_op args[2]
  0.9 0.7 %reshape.16.sh_ref = s32[768]{0:T(1024)} reshape(s32[8,48,2]{2,1,0:T(8,128)S(1)} %copy.9) | data formatting | bytes 6144 | tf_op jit(solution)/shard_map/reshape | solution.py:70
  1.6 1.4 %stack.9 = f32[1,12,32,4,128]{4,3,2,1,0:T(4,128)S(1)} reshape(f32[12,32,512]{2,1,0:T(8,128)} %param.3) | data formatting | bytes 1572864 | tf_op jit(solution)/shard_map/stack | solution.py:76
  3.0 0.0 copy-done
  3.0 0.3 stack.10
  3.3 1.5 %pad_maximum_fusion = f32[2,12,32,4,128]{4,3,0,2,1:T(4,128)} fusion(f32[1,12,32,4,128]{4,3,0,2,1:T(4,128)S(1)} %bitcast.13, f32[1,12,32,4,128]{4,3,0,2,1:T(4,128)S(1)} %bitcast.12), kind=kLoop, calls=%fused_computation | loop fusion | flops 393216 | bytes 3145728 | tf_op jit(solution)/shard_map/stack | solution.py:76
  4.9 7.1 %shard_map.37 = (f32[8,32,8,128]{3,2,1,0:T(8,128)}, f32[8,16,8,128]{3,2,1,0:T(8,128)}, f32[8,16,8,128]{3,2,1,0:T(8,128)}) custom-call(s32[768]{0:T(1024)} %reshape.16.sh_ref, f32[12,32,8,128]{3,2,1,0:T(8,128)} %bitcast.9), custom_call_target="tpu_custom_call" | custom-call | flops 6291456 | bytes 3670016 | tf_op jit(solution)/shard_map/pallas_call | solution.py:59
  11.9 1.9 %collective-permute-start = (f32[8,16,8,128]{3,2,1,0:T(8,128)}, f32[8,16,8,128]{3,2,1,0:T(8,128)S(1)}, u32[]{:S(2)}, u32[]{:S(2)}) collective-permute-start(f32[8,16,8,128]{3,2,1,0:T(8,128)} %get-tuple-element.9), channel_id=1, source_target_pairs={{0,4},{4,8},{8,12},{12,16},{16,20},{20,24},{24,28},{28,32},{32,36}... | collective-permute-start | bytes 1572872 | tf_op jit(solution)/shard_map/ppermute | solution.py:82
  13.8 11.1 %collective-permute-start.1 = (f32[8,16,8,128]{3,2,1,0:T(8,128)}, f32[8,16,8,128]{3,2,1,0:T(8,128)S(1)}, u32[]{:S(2)}, u32[]{:S(2)}) collective-permute-start(f32[8,16,8,128]{3,2,1,0:T(8,128)} %get-tuple-element.10), channel_id=1, source_target_pairs={{4,0},{8,4},{12,8},{16,12},{20,16},{24,20},{28,24},{32,28},{36,32}... | collective-permute-start | bytes 1572872 | tf_op jit(solution)/shard_map/ppermute | solution.py:83
  24.9 5.1 %collective-permute-done = f32[8,16,8,128]{3,2,1,0:T(8,128)S(1)} collective-permute-done((f32[8,16,8,128]{3,2,1,0:T(8,128)}, f32[8,16,8,128]{3,2,1,0:T(8,128)S(1)}, u32[]{:S(2)}, u32[]{:S(2)}) %collective-permute-start) | collective-permute-done | bytes 524320 | tf_op jit(solution)/shard_map/ppermute | solution.py:82
  30.1 1.9 %collective-permute-done.1 = f32[8,16,8,128]{3,2,1,0:T(8,128)S(1)} collective-permute-done((f32[8,16,8,128]{3,2,1,0:T(8,128)}, f32[8,16,8,128]{3,2,1,0:T(8,128)S(1)}, u32[]{:S(2)}, u32[]{:S(2)}) %collective-permute-start.1) | collective-permute-done | bytes 524320 | tf_op jit(solution)/shard_map/ppermute | solution.py:83
  31.9 1.4 %maximum_add_fusion = f32[8,32,8,128]{3,2,1,0:T(8,128)S(1)} fusion(f32[8,32,8,128]{3,2,1,0:T(8,128)} %get-tuple-element.8, f32[8,16,8,128]{3,2,1,0:T(8,128)S(1)} %collective-permute-done.1, f32[8,16,8,128]{3,2,1,0:T(8,128)S(1)} %collective-permute-done), kind=kLoop, calls=%fused_computation.1 | loop fusion | flops 524288 | bytes 3145728 | tf_op jit(solution)/shard_map/add | solution.py:86
  33.3 0.5 %copy.18 = f32[8,32,2,4,128]{4,2,1,0,3:T(2,128)S(1)} copy(f32[8,32,2,4,128]{4,3,2,1,0:T(4,128)S(1)} %bitcast.10) | data formatting | bytes 2097152 | tf_op jit(solution)/shard_map/reshape | solution.py:87
  33.9 15.2 %all_to_all.5 = f32[4,8,2,32,128]{4,2,3,1,0:T(2,128)S(1)} all-to-all(f32[4,8,2,32,128]{4,2,3,1,0:T(2,128)S(1)} %bitcast.11), channel_id=1, replica_groups=mesh['tile'=128,'epoch'=4] {'epoch'}, dimensions={0} | all-to-all | bytes 2097152 | tf_op jit(solution)/shard_map/all_to_all | solution.py:88
  49.0 0.6 %reduce_sum.9 = f32[8,2,32,128]{3,1,2,0:T(2,128)S(1)} reduce(f32[4,8,2,32,128]{4,2,3,1,0:T(2,128)S(1)} %all_to_all.5, f32[]{:T(128)} %constant.0.clone.1), dimensions={0}, to_apply=%region_0.0 | reduce | flops 196608 | bytes 1310724 | tf_op jit(solution)/shard_map/reduce_sum | solution.py:88
  49.7 0.8 %fusion.1 = f32[32,128]{1,0:T(8,128)} fusion(f32[8,2,32,128]{3,1,2,0:T(2,128)S(1)} %reduce_sum.9), kind=kLoop, calls=%fused_computation.5 | loop fusion | flops 61440 | bytes 278528 | tf_op jit(solution)/shard_map/reduce_max | solution.py:90
Async XLA Ops:
  0.0 3.0 %copy-start = (f32[12,32,512]{2,1,0:T(8,128)S(1)}, f32[12,32,512]{2,1,0:T(8,128)}, u32[]{:S(2)}) copy-start(f32[12,32,512]{2,1,0:T(8,128)} %param.4) | copy-start | bytes 2359300
  11.9 18.2 %collective-permute-start = (f32[8,16,8,128]{3,2,1,0:T(8,128)}, f32[8,16,8,128]{3,2,1,0:T(8,128)S(1)}, u32[]{:S(2)}, u32[]{:S(2)}) collective-permute-start(f32[8,16,8,128]{3,2,1,0:T(8,128)} %get-tuple-element.9), channel_id=1, source_target_pairs={{0,4},{4,8},{8,12},{12,16},{16,20},{20,24},{24,28},{28,32},{32,36}... | collective-permute-start | bytes 1572872 | tf_op jit(solution)/shard_map/ppermute | solution.py:82
  13.8 18.1 %collective-permute-start.1 = (f32[8,16,8,128]{3,2,1,0:T(8,128)}, f32[8,16,8,128]{3,2,1,0:T(8,128)S(1)}, u32[]{:S(2)}, u32[]{:S(2)}) collective-permute-start(f32[8,16,8,128]{3,2,1,0:T(8,128)} %get-tuple-element.10), channel_id=1, source_target_pairs={{4,0},{8,4},{12,8},{16,12},{20,16},{24,20},{28,24},{32,28},{36,32}... | collective-permute-start | bytes 1572872 | tf_op jit(solution)/shard_map/ppermute | solution.py:83

commit v11 on v10

--- a/solution.py
+++ b/solution.py
@@ -44,7 +44,7 @@
             add_epoch(v, e)
         return carry
 
-    lax.fori_loop(0, epochs, body, 0)
+    lax.fori_loop(0, epochs, body, 0, unroll=2)
     for v in range(vels):
         top_ref[v] = acc_ref[v, :HALO]
         own_ref[v] = acc_ref[v, HALO : HALO + rows]
@@ -85,9 +85,17 @@
     middle = jnp.zeros((vels, rows - 2 * HALO) + own.shape[2:], jnp.float32)
     part = own + jnp.concatenate([from_above, middle, from_below], axis=1)
     part = part.reshape(vels, rows, 2, blocks, LANES).transpose(3, 0, 2, 1, 4)
-    summed = jnp.sum(lax.all_to_all(part, "epoch", 0, 0, tiled=True), axis=0)
-    ratio = summed[:, 0] / jnp.sqrt(summed[:, 1])
-    return jnp.max(ratio, axis=0)
+    gathered = lax.all_to_all(part, "epoch", 0, 0, tiled=True)
+    best = None
+    for v in range(vels):
+        psi_sum = gathered[0, v, 0]
+        phi_sum = gathered[0, v, 1]
+        for source in range(1, gathered.shape[0]):
+            psi_sum = psi_sum + gathered[source, v, 0]
+            phi_sum = phi_sum + gathered[source, v, 1]
+        ratio = psi_sum / jnp.sqrt(phi_sum)
+        best = ratio if best is None else jnp.maximum(best, ratio)
+    return best
 
 
 def solution(mesh):

time: 50.8 us -> 49.2 us (0.969)
  other arithmetic: 4.37 us -> 3.62 us
    reduce_max x1 -> x0, other arithmetic: 0.84 us -> none  [per_device(): return jnp.max(ratio, axis=0)]
    max x0 -> x1, other arithmetic: none -> 0.69 us  [per_device(): best = ratio if best is None else jnp.maximum(best, ratio)]
    reduce_sum x1 -> x0, other arithmetic: 0.62 us -> none  [per_device(): summed = jnp.sum(lax.all_to_all(part, 'epoch', 0, 0, tiled=True), axis=0)]
where the time goes in v11:
time: 49.2 us; the launch traced here: 49 us
  blocking collectives  15.2 us (31%)
  starting transfers between devices  13 us (26%)
  waiting for transfers between devices  6.99 us (14%)
  Pallas kernels  6.61 us (13%)
  other arithmetic  3.62 us (7%)
  local copies, waits for them, and re-layouts  3.5 us (7%)
    all_to_all x1, blocking collectives, per_device(): gathered = lax.all_to_all(part, 'epoch', 0, 0, tiled=True)  15.2 us
    ppermute x1, starting transfers between devices, per_device(): from_below = lax.ppermute(top, 'tile', backward)  11.1 us
    pallas_call x1, Pallas kernels, partial_stacks(): pl.pallas_call(stack_kernel, out_shape=(jax.ShapeDtypeStruct((vels, rows,...  6.61 us
    ppermute x1, waiting for transfers between devices, per_device(): from_above = lax.ppermute(bottom, 'tile', forward)  5.13 us
    ppermute x1, starting transfers between devices, per_device(): from_above = lax.ppermute(bottom, 'tile', forward)  1.91 us
    ppermute x1, waiting for transfers between devices, per_device(): from_below = lax.ppermute(top, 'tile', backward)  1.86 us
    another operation x2, local copies, waits for them, and re-layouts, per_device(): stacked = jnp.stack([psi, phi]).reshape(2, epochs, rows, blocks, LANES)  1.66 us
    another operation x1, other arithmetic, per_device(): stacked = jnp.stack([psi, phi]).reshape(2, epochs, rows, blocks, LANES)  1.54 us
  transfers between devices with their start and end apart: 2, of which 2 were waited for; matrix products, arithmetic and copies ran while one was open for 0% of the time, Pallas kernels for 0%

profile of v11, /device:TPU:6, one launch (start us, length us, event | category | flops | bytes accessed | tf_op | source)
XLA Modules:
  0.0 49.0 jit_solution(2647655693208274595)
XLA Ops:
  0.0 0.0 copy-start
  0.0 0.9 %copy.7 = s32[8,48,2]{2,1,0:T(8,128)S(1)} copy(s32[8,48,2]{1,2,0:T(2,128)} %param.5) | data formatting | bytes 6144 | tf_op args[2]
  0.9 0.7 %reshape.70.sh_ref = s32[768]{0:T(1024)} reshape(s32[8,48,2]{2,1,0:T(8,128)S(1)} %copy.7) | data formatting | bytes 6144 | tf_op jit(solution)/shard_map/reshape | solution.py:70
  1.6 1.4 %stack.9 = f32[1,12,32,4,128]{4,3,2,1,0:T(4,128)S(1)} reshape(f32[12,32,512]{2,1,0:T(8,128)} %param.3) | data formatting | bytes 1572864 | tf_op jit(solution)/shard_map/stack | solution.py:76
  3.0 0.0 copy-done
  3.0 0.3 stack.10
  3.3 1.5 %pad_maximum_fusion = f32[2,12,32,4,128]{4,3,0,2,1:T(4,128)} fusion(f32[1,12,32,4,128]{4,3,0,2,1:T(4,128)S(1)} %bitcast.15, f32[1,12,32,4,128]{4,3,0,2,1:T(4,128)S(1)} %bitcast.14), kind=kLoop, calls=%fused_computation | loop fusion | flops 393216 | bytes 3145728 | tf_op jit(solution)/shard_map/stack | solution.py:76
  4.9 6.6 %shard_map.37 = (f32[8,32,8,128]{3,2,1,0:T(8,128)}, f32[8,16,8,128]{3,2,1,0:T(8,128)}, f32[8,16,8,128]{3,2,1,0:T(8,128)}) custom-call(s32[768]{0:T(1024)} %reshape.70.sh_ref, f32[12,32,8,128]{3,2,1,0:T(8,128)} %bitcast.11), custom_call_target="tpu_custom_call" | custom-call | flops 6291456 | bytes 3670016 | tf_op jit(solution)/shard_map/pallas_call | solution.py:59
  11.5 1.9 %collective-permute-start = (f32[8,16,8,128]{3,2,1,0:T(8,128)}, f32[8,16,8,128]{3,2,1,0:T(8,128)S(1)}, u32[]{:S(2)}, u32[]{:S(2)}) collective-permute-start(f32[8,16,8,128]{3,2,1,0:T(8,128)} %get-tuple-element.9), channel_id=1, source_target_pairs={{0,4},{4,8},{8,12},{12,16},{16,20},{20,24},{24,28},{28,32},{32,36}... | collective-permute-start | bytes 1572872 | tf_op jit(solution)/shard_map/ppermute | solution.py:82
  13.4 11.1 %collective-permute-start.1 = (f32[8,16,8,128]{3,2,1,0:T(8,128)}, f32[8,16,8,128]{3,2,1,0:T(8,128)S(1)}, u32[]{:S(2)}, u32[]{:S(2)}) collective-permute-start(f32[8,16,8,128]{3,2,1,0:T(8,128)} %get-tuple-element.10), channel_id=1, source_target_pairs={{4,0},{8,4},{12,8},{16,12},{20,16},{24,20},{28,24},{32,28},{36,32}... | collective-permute-start | bytes 1572872 | tf_op jit(solution)/shard_map/ppermute | solution.py:83
  24.5 5.1 %collective-permute-done = f32[8,16,8,128]{3,2,1,0:T(8,128)S(1)} collective-permute-done((f32[8,16,8,128]{3,2,1,0:T(8,128)}, f32[8,16,8,128]{3,2,1,0:T(8,128)S(1)}, u32[]{:S(2)}, u32[]{:S(2)}) %collective-permute-start) | collective-permute-done | bytes 524320 | tf_op jit(solution)/shard_map/ppermute | solution.py:82
  29.6 1.9 %collective-permute-done.1 = f32[8,16,8,128]{3,2,1,0:T(8,128)S(1)} collective-permute-done((f32[8,16,8,128]{3,2,1,0:T(8,128)}, f32[8,16,8,128]{3,2,1,0:T(8,128)S(1)}, u32[]{:S(2)}, u32[]{:S(2)}) %collective-permute-start.1) | collective-permute-done | bytes 524320 | tf_op jit(solution)/shard_map/ppermute | solution.py:83
  31.5 1.4 %maximum_add_fusion = f32[8,32,8,128]{3,2,1,0:T(8,128)S(1)} fusion(f32[8,32,8,128]{3,2,1,0:T(8,128)} %get-tuple-element.8, f32[8,16,8,128]{3,2,1,0:T(8,128)S(1)} %collective-permute-done.1, f32[8,16,8,128]{3,2,1,0:T(8,128)S(1)} %collective-permute-done), kind=kLoop, calls=%fused_computation.1 | loop fusion | flops 524288 | bytes 3145728 | tf_op jit(solution)/shard_map/add | solution.py:86
  32.9 0.2 copy.12
  33.1 15.2 %all_to_all.5 = f32[4,8,2,32,128]{4,3,2,1,0:T(8,128)S(1)} all-to-all(f32[4,8,2,32,128]{4,3,2,1,0:T(8,128)S(1)} %bitcast.13), channel_id=1, replica_groups=mesh['tile'=128,'epoch'=4] {'epoch'}, dimensions={0} | all-to-all | bytes 2097152 | tf_op jit(solution)/shard_map/all_to_all | solution.py:88
  48.3 0.7 %fusion.3 = f32[32,128]{1,0:T(8,128)} fusion(f32[4,8,2,32,128]{4,3,2,1,0:T(8,128)S(1)} %all_to_all.5), kind=kLoop, calls=%fused_computation.7 | loop fusion | flops 258048 | bytes 1064960 | tf_op jit(solution)/shard_map/max | solution.py:97
Async XLA Ops:
  0.0 3.0 %copy-start = (f32[12,32,512]{2,1,0:T(8,128)S(1)}, f32[12,32,512]{2,1,0:T(8,128)}, u32[]{:S(2)}) copy-start(f32[12,32,512]{2,1,0:T(8,128)} %param.4) | copy-start | bytes 2359300
  11.5 18.2 %collective-permute-start = (f32[8,16,8,128]{3,2,1,0:T(8,128)}, f32[8,16,8,128]{3,2,1,0:T(8,128)S(1)}, u32[]{:S(2)}, u32[]{:S(2)}) collective-permute-start(f32[8,16,8,128]{3,2,1,0:T(8,128)} %get-tuple-element.9), channel_id=1, source_target_pairs={{0,4},{4,8},{8,12},{12,16},{16,20},{20,24},{24,28},{28,32},{32,36}... | collective-permute-start | bytes 1572872 | tf_op jit(solution)/shard_map/ppermute | solution.py:82
  13.4 18.1 %collective-permute-start.1 = (f32[8,16,8,128]{3,2,1,0:T(8,128)}, f32[8,16,8,128]{3,2,1,0:T(8,128)S(1)}, u32[]{:S(2)}, u32[]{:S(2)}) collective-permute-start(f32[8,16,8,128]{3,2,1,0:T(8,128)} %get-tuple-element.10), channel_id=1, source_target_pairs={{4,0},{8,4},{12,8},{16,12},{20,16},{24,20},{28,24},{32,28},{36,32}... | collective-permute-start | bytes 1572872 | tf_op jit(solution)/shard_map/ppermute | solution.py:83

commit v12 on v11

--- a/solution.py
+++ b/solution.py
@@ -22,9 +22,9 @@
     block = lax.broadcasted_iota(jnp.int32, (slots, lanes), 0) % blocks
 
     def add_epoch(v, e):
-        at = (v * total + first + e) * 2
+        at = v * 2 * total + first + e
         s_r = sh_ref[at]
-        s_c = sh_ref[at + 1]
+        s_c = sh_ref[at + total]
         amount = lax.rem(lanes - s_c, lanes)
         moved = lane + s_c
         inside = (moved >= 0) & (moved < lanes)
@@ -67,7 +67,7 @@
             bytes_accessed=4 * (epochs * rows + vels * (rows + 2 * HALO)) * slots * lanes,
             transcendentals=0,
         ),
-    )(shifts.reshape(-1), x)
+    )(jnp.swapaxes(shifts, 1, 2).reshape(-1), x)
 
 
 def per_device(psi, phi, shifts):

time: 49.2 us -> 49 us (level)
    unnamed x3 -> x2, local copies, waits for them, and re-layouts: 0.9 us -> 0.01 us
    reshape x1, local copies, waits for them, and re-layouts: 0.74 us -> 1.44 us  [partial_stacks(): jnp.swapaxes(shifts, 1, 2).reshape(-1)]
where the time goes in v12:
time: 49 us; the launch traced here: 48.8 us
  blocking collectives  15.2 us (31%)
  starting transfers between devices  13 us (27%)
  waiting for transfers between devices  6.99 us (14%)
  Pallas kernels  6.61 us (13%)
  other arithmetic  3.62 us (7%)
  local copies, waits for them, and re-layouts  3.31 us (7%)
    all_to_all x1, blocking collectives, per_device(): gathered = lax.all_to_all(part, 'epoch', 0, 0, tiled=True)  15.2 us
    ppermute x1, starting transfers between devices, per_device(): from_below = lax.ppermute(top, 'tile', backward)  11.1 us
    pallas_call x1, Pallas kernels, partial_stacks(): pl.pallas_call(stack_kernel, out_shape=(jax.ShapeDtypeStruct((vels, rows,...  6.61 us
    ppermute x1, waiting for transfers between devices, per_device(): from_above = lax.ppermute(bottom, 'tile', forward)  5.13 us
    ppermute x1, starting transfers between devices, per_device(): from_above = lax.ppermute(bottom, 'tile', forward)  1.91 us
    ppermute x1, waiting for transfers between devices, per_device(): from_below = lax.ppermute(top, 'tile', backward)  1.86 us
    another operation x2, local copies, waits for them, and re-layouts, per_device(): stacked = jnp.stack([psi, phi]).reshape(2, epochs, rows, blocks, LANES)  1.66 us
    another operation x1, other arithmetic, per_device(): stacked = jnp.stack([psi, phi]).reshape(2, epochs, rows, blocks, LANES)  1.54 us
  transfers between devices with their start and end apart: 2, of which 2 were waited for; matrix products, arithmetic and copies ran while one was open for 0% of the time, Pallas kernels for 0%

profile of v12, /device:TPU:6, one launch (start us, length us, event | category | flops | bytes accessed | tf_op | source)
XLA Modules:
  0.0 48.8 jit_solution(3967650760578374200)
XLA Ops:
  0.0 0.0 copy-start
  0.0 1.4 %reshape.70.sh_ref = s32[768]{0:T(1024)} reshape(s32[8,2,48]{2,1,0:T(2,128)} %bitcast.17) | data formatting | bytes 6144 | tf_op jit(solution)/shard_map/reshape | solution.py:70
  1.4 1.4 %stack.9 = f32[1,12,32,4,128]{4,3,2,1,0:T(4,128)S(1)} reshape(f32[12,32,512]{2,1,0:T(8,128)} %param.3) | data formatting | bytes 1572864 | tf_op jit(solution)/shard_map/stack | solution.py:76
  2.8 0.0 copy-done
  2.8 0.3 stack.10
  3.1 1.5 %pad_maximum_fusion = f32[2,12,32,4,128]{4,3,0,2,1:T(4,128)} fusion(f32[1,12,32,4,128]{4,3,0,2,1:T(4,128)S(1)} %bitcast.16, f32[1,12,32,4,128]{4,3,0,2,1:T(4,128)S(1)} %bitcast.15), kind=kLoop, calls=%fused_computation | loop fusion | flops 393216 | bytes 3145728 | tf_op jit(solution)/shard_map/stack | solution.py:76
  4.7 6.6 %shard_map.37 = (f32[8,32,8,128]{3,2,1,0:T(8,128)}, f32[8,16,8,128]{3,2,1,0:T(8,128)}, f32[8,16,8,128]{3,2,1,0:T(8,128)}) custom-call(s32[768]{0:T(1024)} %reshape.70.sh_ref, f32[12,32,8,128]{3,2,1,0:T(8,128)} %bitcast.12), custom_call_target="tpu_custom_call" | custom-call | flops 6291456 | bytes 3670016 | tf_op jit(solution)/shard_map/pallas_call | solution.py:59
  11.3 1.9 %collective-permute-start = (f32[8,16,8,128]{3,2,1,0:T(8,128)}, f32[8,16,8,128]{3,2,1,0:T(8,128)S(1)}, u32[]{:S(2)}, u32[]{:S(2)}) collective-permute-start(f32[8,16,8,128]{3,2,1,0:T(8,128)} %get-tuple-element.9), channel_id=1, source_target_pairs={{0,4},{4,8},{8,12},{12,16},{16,20},{20,24},{24,28},{28,32},{32,36}... | collective-permute-start | bytes 1572872 | tf_op jit(solution)/shard_map/ppermute | solution.py:82
  13.2 11.1 %collective-permute-start.1 = (f32[8,16,8,128]{3,2,1,0:T(8,128)}, f32[8,16,8,128]{3,2,1,0:T(8,128)S(1)}, u32[]{:S(2)}, u32[]{:S(2)}) collective-permute-start(f32[8,16,8,128]{3,2,1,0:T(8,128)} %get-tuple-element.10), channel_id=1, source_target_pairs={{4,0},{8,4},{12,8},{16,12},{20,16},{24,20},{28,24},{32,28},{36,32}... | collective-permute-start | bytes 1572872 | tf_op jit(solution)/shard_map/ppermute | solution.py:83
  24.3 5.1 %collective-permute-done = f32[8,16,8,128]{3,2,1,0:T(8,128)S(1)} collective-permute-done((f32[8,16,8,128]{3,2,1,0:T(8,128)}, f32[8,16,8,128]{3,2,1,0:T(8,128)S(1)}, u32[]{:S(2)}, u32[]{:S(2)}) %collective-permute-start) | collective-permute-done | bytes 524320 | tf_op jit(solution)/shard_map/ppermute | solution.py:82
  29.4 1.9 %collective-permute-done.1 = f32[8,16,8,128]{3,2,1,0:T(8,128)S(1)} collective-permute-done((f32[8,16,8,128]{3,2,1,0:T(8,128)}, f32[8,16,8,128]{3,2,1,0:T(8,128)S(1)}, u32[]{:S(2)}, u32[]{:S(2)}) %collective-permute-start.1) | collective-permute-done | bytes 524320 | tf_op jit(solution)/shard_map/ppermute | solution.py:83
  31.3 1.4 %maximum_add_fusion = f32[8,32,8,128]{3,2,1,0:T(8,128)S(1)} fusion(f32[8,32,8,128]{3,2,1,0:T(8,128)} %get-tuple-element.8, f32[8,16,8,128]{3,2,1,0:T(8,128)S(1)} %collective-permute-done.1, f32[8,16,8,128]{3,2,1,0:T(8,128)S(1)} %collective-permute-done), kind=kLoop, calls=%fused_computation.1 | loop fusion | flops 524288 | bytes 3145728 | tf_op jit(solution)/shard_map/add | solution.py:86
  32.7 0.2 copy.8
  32.9 15.2 %all_to_all.5 = f32[4,8,2,32,128]{4,3,2,1,0:T(8,128)S(1)} all-to-all(f32[4,8,2,32,128]{4,3,2,1,0:T(8,128)S(1)} %bitcast.14), channel_id=1, replica_groups=mesh['tile'=128,'epoch'=4] {'epoch'}, dimensions={0} | all-to-all | bytes 2097152 | tf_op jit(solution)/shard_map/all_to_all | solution.py:88
  48.1 0.7 %fusion.3 = f32[32,128]{1,0:T(8,128)} fusion(f32[4,8,2,32,128]{4,3,2,1,0:T(8,128)S(1)} %all_to_all.5), kind=kLoop, calls=%fused_computation.7 | loop fusion | flops 258048 | bytes 1064960 | tf_op jit(solution)/shard_map/max | solution.py:97
Async XLA Ops:
  0.0 2.8 %copy-start = (f32[12,32,512]{2,1,0:T(8,128)S(1)}, f32[12,32,512]{2,1,0:T(8,128)}, u32[]{:S(2)}) copy-start(f32[12,32,512]{2,1,0:T(8,128)} %param.4) | copy-start | bytes 2359300
  11.3 18.2 %collective-permute-start = (f32[8,16,8,128]{3,2,1,0:T(8,128)}, f32[8,16,8,128]{3,2,1,0:T(8,128)S(1)}, u32[]{:S(2)}, u32[]{:S(2)}) collective-permute-start(f32[8,16,8,128]{3,2,1,0:T(8,128)} %get-tuple-element.9), channel_id=1, source_target_pairs={{0,4},{4,8},{8,12},{12,16},{16,20},{20,24},{24,28},{28,32},{32,36}... | collective-permute-start | bytes 1572872 | tf_op jit(solution)/shard_map/ppermute | solution.py:82
  13.2 18.1 %collective-permute-start.1 = (f32[8,16,8,128]{3,2,1,0:T(8,128)}, f32[8,16,8,128]{3,2,1,0:T(8,128)S(1)}, u32[]{:S(2)}, u32[]{:S(2)}) collective-permute-start(f32[8,16,8,128]{3,2,1,0:T(8,128)} %get-tuple-element.10), channel_id=1, source_target_pairs={{4,0},{8,4},{12,8},{16,12},{20,16},{24,20},{28,24},{32,28},{36,32}... | collective-permute-start | bytes 1572872 | tf_op jit(solution)/shard_map/ppermute | solution.py:83

commit v13 on v12

--- a/solution.py
+++ b/solution.py
@@ -10,9 +10,22 @@
 CHUNK = 8
 
 
-def stack_kernel(sh_ref, x_ref, own_ref, top_ref, bottom_ref, acc_ref):
+def stack_kernel(sh_ref, psi_ref, phi_ref, own_ref, top_ref, bottom_ref, acc_ref, x_ref):
     epochs, rows, slots, lanes = x_ref.shape
     blocks = slots // 2
+
+    def pack(e, carry):
+        for a in range(rows // CHUNK):
+            here = slice(a * CHUNK, (a + 1) * CHUNK)
+            pieces = [
+                src[e, here, j * lanes : (j + 1) * lanes]
+                for src in (psi_ref, phi_ref)
+                for j in range(blocks)
+            ]
+            x_ref[e, here] = jnp.swapaxes(jnp.stack(pieces, axis=0), 0, 1)
+        return carry
+
+    lax.fori_loop(0, epochs, pack, 0)
     vels = acc_ref.shape[0]
     total = sh_ref.shape[0] // (2 * vels)
     first = lax.axis_index("epoch") * epochs
@@ -51,31 +64,33 @@
         bottom_ref[v] = acc_ref[v, HALO + rows :]
 
 
-def partial_stacks(shifts, x):
-    epochs, rows, slots, lanes = x.shape
+def partial_stacks(shifts, psi, phi):
+    epochs, rows, cols = psi.shape
+    slots, lanes = 2 * (cols // LANES), LANES
     vels = shifts.shape[0]
     vmem = pl.BlockSpec(memory_space=pltpu.VMEM)
     spill = jax.ShapeDtypeStruct((vels, HALO, slots, lanes), jnp.float32)
     return pl.pallas_call(
         stack_kernel,
         out_shape=(jax.ShapeDtypeStruct((vels, rows, slots, lanes), jnp.float32), spill, spill),
-        in_specs=[pl.BlockSpec(memory_space=pltpu.SMEM), vmem],
+        in_specs=[pl.BlockSpec(memory_space=pltpu.SMEM), vmem, vmem],
         out_specs=(vmem, vmem, vmem),
-        scratch_shapes=[pltpu.VMEM((vels, rows + 2 * HALO, slots, lanes), jnp.float32)],
+        scratch_shapes=[
+            pltpu.VMEM((vels, rows + 2 * HALO, slots, lanes), jnp.float32),
+            pltpu.VMEM((epochs, rows, slots, lanes), jnp.float32),
+        ],
         cost_estimate=pl.CostEstimate(
             flops=2 * vels * epochs * rows * slots * lanes,
             bytes_accessed=4 * (epochs * rows + vels * (rows + 2 * HALO)) * slots * lanes,
             transcendentals=0,
         ),
-    )(jnp.swapaxes(shifts, 1, 2).reshape(-1), x)
+    )(jnp.swapaxes(shifts, 1, 2).reshape(-1), psi, phi)
 
 
 def per_device(psi, phi, shifts):
     epochs, rows, cols = psi.shape
     blocks = cols // LANES
-    stacked = jnp.stack([psi, phi]).reshape(2, epochs, rows, blocks, LANES)
-    x = stacked.transpose(1, 2, 0, 3, 4).reshape(epochs, rows, 2 * blocks, LANES)
-    own, top, bottom = partial_stacks(shifts, x)
+    own, top, bottom = partial_stacks(shifts, psi, phi)
     count = lax.axis_size("tile")
     forward = [(i, i + 1) for i in range(count - 1)]
     backward = [(i + 1, i) for i in range(count - 1)]

time: 49 us -> 46 us (0.939)
  local copies, waits for them, and re-layouts: 3.31 us -> 1.57 us
  other arithmetic: 3.62 us -> 2.08 us
    another operation x2 -> x0, local copies, waits for them, and re-layouts: 1.66 us -> none  [per_device(): stacked = jnp.stack([psi, phi]).reshape(2, epochs, rows, blocks, LANES)]
    another operation x1 -> x0, other arithmetic: 1.54 us -> none  [per_device(): stacked = jnp.stack([psi, phi]).reshape(2, epochs, rows, blocks, LANES)]
where the time goes in v13:
time: 46 us; the launch traced here: 45.7 us
  blocking collectives  15.2 us (33%)
  starting transfers between devices  13 us (28%)
  waiting for transfers between devices  6.99 us (15%)
  Pallas kernels  6.88 us (15%)
  other arithmetic  2.08 us (5%)
  local copies, waits for them, and re-layouts  1.57 us (3%)
    all_to_all x1, blocking collectives, per_device(): gathered = lax.all_to_all(part, 'epoch', 0, 0, tiled=True)  15.2 us
    ppermute x1, starting transfers between devices, per_device(): from_below = lax.ppermute(top, 'tile', backward)  11.1 us
    pallas_call x1, Pallas kernels, partial_stacks(): pl.pallas_call(stack_kernel, out_shape=(jax.ShapeDtypeStruct((vels, rows,...  6.88 us
    ppermute x1, waiting for transfers between devices, per_device(): from_above = lax.ppermute(bottom, 'tile', forward)  5.13 us
    ppermute x1, starting transfers between devices, per_device(): from_above = lax.ppermute(bottom, 'tile', forward)  1.91 us
    ppermute x1, waiting for transfers between devices, per_device(): from_below = lax.ppermute(top, 'tile', backward)  1.86 us
    add x1, other arithmetic, per_device(): part = own + jnp.concatenate([from_above, middle, from_below], axis=1)  1.39 us
    reshape x1, local copies, waits for them, and re-layouts, partial_stacks(): jnp.swapaxes(shifts, 1, 2).reshape(-1)  1.37 us
  transfers between devices with their start and end apart: 2, of which 2 were waited for; matrix products, arithmetic and copies ran while one was open for 0% of the time, Pallas kernels for 0%

profile of v13, /device:TPU:6, one launch (start us, length us, event | category | flops | bytes accessed | tf_op | source)
XLA Modules:
  0.0 45.7 jit_solution(775820021478794213)
XLA Ops:
  0.0 1.4 %reshape.62.sh_ref = s32[768]{0:T(1024)} reshape(s32[8,2,48]{2,1,0:T(2,128)} %bitcast.9) | data formatting | bytes 6144 | tf_op jit(solution)/shard_map/reshape | solution.py:87
  1.4 6.9 %shard_map.37 = (f32[8,32,8,128]{3,2,1,0:T(8,128)}, f32[8,16,8,128]{3,2,1,0:T(8,128)}, f32[8,16,8,128]{3,2,1,0:T(8,128)}) custom-call(s32[768]{0:T(1024)} %reshape.62.sh_ref, f32[12,32,512]{2,1,0:T(8,128)} %psi_ref.1, f32[12,32,512]{2,1,0:T(8,128)} %phi_ref.1), custom_call_target="tpu_custom_call" | custom-call | flops 6291456 | bytes 3670016 | tf_op jit(solution)/shard_map/pallas_call | solution.py:73
  8.3 1.9 %collective-permute-start = (f32[8,16,8,128]{3,2,1,0:T(8,128)}, f32[8,16,8,128]{3,2,1,0:T(8,128)S(1)}, u32[]{:S(2)}, u32[]{:S(2)}) collective-permute-start(f32[8,16,8,128]{3,2,1,0:T(8,128)} %get-tuple-element.9), channel_id=1, source_target_pairs={{0,4},{4,8},{8,12},{12,16},{16,20},{20,24},{24,28},{28,32},{32,36}... | collective-permute-start | bytes 1572872 | tf_op jit(solution)/shard_map/ppermute | solution.py:97
  10.2 11.1 %collective-permute-start.1 = (f32[8,16,8,128]{3,2,1,0:T(8,128)}, f32[8,16,8,128]{3,2,1,0:T(8,128)S(1)}, u32[]{:S(2)}, u32[]{:S(2)}) collective-permute-start(f32[8,16,8,128]{3,2,1,0:T(8,128)} %get-tuple-element.10), channel_id=1, source_target_pairs={{4,0},{8,4},{12,8},{16,12},{20,16},{24,20},{28,24},{32,28},{36,32}... | collective-permute-start | bytes 1572872 | tf_op jit(solution)/shard_map/ppermute | solution.py:98
  21.3 5.1 %collective-permute-done = f32[8,16,8,128]{3,2,1,0:T(8,128)S(1)} collective-permute-done((f32[8,16,8,128]{3,2,1,0:T(8,128)}, f32[8,16,8,128]{3,2,1,0:T(8,128)S(1)}, u32[]{:S(2)}, u32[]{:S(2)}) %collective-permute-start) | collective-permute-done | bytes 524320 | tf_op jit(solution)/shard_map/ppermute | solution.py:97
  26.4 1.9 %collective-permute-done.1 = f32[8,16,8,128]{3,2,1,0:T(8,128)S(1)} collective-permute-done((f32[8,16,8,128]{3,2,1,0:T(8,128)}, f32[8,16,8,128]{3,2,1,0:T(8,128)S(1)}, u32[]{:S(2)}, u32[]{:S(2)}) %collective-permute-start.1) | collective-permute-done | bytes 524320 | tf_op jit(solution)/shard_map/ppermute | solution.py:98
  28.3 1.4 %maximum_add_fusion = f32[8,32,8,128]{3,2,1,0:T(8,128)S(1)} fusion(f32[8,32,8,128]{3,2,1,0:T(8,128)} %get-tuple-element.8, f32[8,16,8,128]{3,2,1,0:T(8,128)S(1)} %collective-permute-done.1, f32[8,16,8,128]{3,2,1,0:T(8,128)S(1)} %collective-permute-done), kind=kLoop, calls=%fused_computation | loop fusion | flops 524288 | bytes 3145728 | tf_op jit(solution)/shard_map/add | solution.py:101
  29.7 0.2 copy.6
  29.9 15.2 %all_to_all.5 = f32[4,8,2,32,128]{4,3,2,1,0:T(8,128)S(1)} all-to-all(f32[4,8,2,32,128]{4,3,2,1,0:T(8,128)S(1)} %bitcast.8), channel_id=1, replica_groups=mesh['tile'=128,'epoch'=4] {'epoch'}, dimensions={0} | all-to-all | bytes 2097152 | tf_op jit(solution)/shard_map/all_to_all | solution.py:103
  45.0 0.7 %fusion.3 = f32[32,128]{1,0:T(8,128)} fusion(f32[4,8,2,32,128]{4,3,2,1,0:T(8,128)S(1)} %all_to_all.5), kind=kLoop, calls=%fused_computation.6 | loop fusion | flops 258048 | bytes 1064960 | tf_op jit(solution)/shard_map/max | solution.py:112
Async XLA Ops:
  8.3 18.2 %collective-permute-start = (f32[8,16,8,128]{3,2,1,0:T(8,128)}, f32[8,16,8,128]{3,2,1,0:T(8,128)S(1)}, u32[]{:S(2)}, u32[]{:S(2)}) collective-permute-start(f32[8,16,8,128]{3,2,1,0:T(8,128)} %get-tuple-element.9), channel_id=1, source_target_pairs={{0,4},{4,8},{8,12},{12,16},{16,20},{20,24},{24,28},{28,32},{32,36}... | collective-permute-start | bytes 1572872 | tf_op jit(solution)/shard_map/ppermute | solution.py:97
  10.2 18.1 %collective-permute-start.1 = (f32[8,16,8,128]{3,2,1,0:T(8,128)}, f32[8,16,8,128]{3,2,1,0:T(8,128)S(1)}, u32[]{:S(2)}, u32[]{:S(2)}) collective-permute-start(f32[8,16,8,128]{3,2,1,0:T(8,128)} %get-tuple-element.10), channel_id=1, source_target_pairs={{4,0},{8,4},{12,8},{16,12},{20,16},{24,20},{28,24},{32,28},{36,32}... | collective-permute-start | bytes 1572872 | tf_op jit(solution)/shard_map/ppermute | solution.py:98

commit v14 on v13

--- a/solution.py
+++ b/solution.py
@@ -57,7 +57,7 @@
             add_epoch(v, e)
         return carry
 
-    lax.fori_loop(0, epochs, body, 0, unroll=2)
+    lax.fori_loop(0, epochs, body, 0, unroll=4)
     for v in range(vels):
         top_ref[v] = acc_ref[v, :HALO]
         own_ref[v] = acc_ref[v, HALO : HALO + rows]

time: 46 us -> 45.8 us (level)
  no operation moved by 1% of the time
where the time goes in v14:
time: 45.8 us; the launch traced here: 45.5 us
  blocking collectives  15.2 us (33%)
  starting transfers between devices  13 us (28%)
  waiting for transfers between devices  6.99 us (15%)
  Pallas kernels  6.64 us (14%)
  other arithmetic  2.08 us (5%)
  local copies, waits for them, and re-layouts  1.57 us (3%)
    all_to_all x1, blocking collectives, per_device(): gathered = lax.all_to_all(part, 'epoch', 0, 0, tiled=True)  15.2 us
    ppermute x1, starting transfers between devices, per_device(): from_below = lax.ppermute(top, 'tile', backward)  11.1 us
    pallas_call x1, Pallas kernels, partial_stacks(): pl.pallas_call(stack_kernel, out_shape=(jax.ShapeDtypeStruct((vels, rows,...  6.64 us
    ppermute x1, waiting for transfers between devices, per_device(): from_above = lax.ppermute(bottom, 'tile', forward)  5.13 us
    ppermute x1, starting transfers between devices, per_device(): from_above = lax.ppermute(bottom, 'tile', forward)  1.91 us
    ppermute x1, waiting for transfers between devices, per_device(): from_below = lax.ppermute(top, 'tile', backward)  1.86 us
    add x1, other arithmetic, per_device(): part = own + jnp.concatenate([from_above, middle, from_below], axis=1)  1.39 us
    reshape x1, local copies, waits for them, and re-layouts, partial_stacks(): jnp.swapaxes(shifts, 1, 2).reshape(-1)  1.37 us
  transfers between devices with their start and end apart: 2, of which 2 were waited for; matrix products, arithmetic and copies ran while one was open for 0% of the time, Pallas kernels for 0%

profile of v14, /device:TPU:6, one launch (start us, length us, event | category | flops | bytes accessed | tf_op | source)
XLA Modules:
  0.0 45.5 jit_solution(11860164752670503447)
XLA Ops:
  0.0 1.4 %reshape.62.sh_ref = s32[768]{0:T(1024)} reshape(s32[8,2,48]{2,1,0:T(2,128)} %bitcast.9) | data formatting | bytes 6144 | tf_op jit(solution)/shard_map/reshape | solution.py:87
  1.4 6.6 %shard_map.37 = (f32[8,32,8,128]{3,2,1,0:T(8,128)}, f32[8,16,8,128]{3,2,1,0:T(8,128)}, f32[8,16,8,128]{3,2,1,0:T(8,128)}) custom-call(s32[768]{0:T(1024)} %reshape.62.sh_ref, f32[12,32,512]{2,1,0:T(8,128)} %psi_ref.1, f32[12,32,512]{2,1,0:T(8,128)} %phi_ref.1), custom_call_target="tpu_custom_call" | custom-call | flops 6291456 | bytes 3670016 | tf_op jit(solution)/shard_map/pallas_call | solution.py:73
  8.0 1.9 %collective-permute-start = (f32[8,16,8,128]{3,2,1,0:T(8,128)}, f32[8,16,8,128]{3,2,1,0:T(8,128)S(1)}, u32[]{:S(2)}, u32[]{:S(2)}) collective-permute-start(f32[8,16,8,128]{3,2,1,0:T(8,128)} %get-tuple-element.9), channel_id=1, source_target_pairs={{0,4},{4,8},{8,12},{12,16},{16,20},{20,24},{24,28},{28,32},{32,36}... | collective-permute-start | bytes 1572872 | tf_op jit(solution)/shard_map/ppermute | solution.py:97
  9.9 11.1 %collective-permute-start.1 = (f32[8,16,8,128]{3,2,1,0:T(8,128)}, f32[8,16,8,128]{3,2,1,0:T(8,128)S(1)}, u32[]{:S(2)}, u32[]{:S(2)}) collective-permute-start(f32[8,16,8,128]{3,2,1,0:T(8,128)} %get-tuple-element.10), channel_id=1, source_target_pairs={{4,0},{8,4},{12,8},{16,12},{20,16},{24,20},{28,24},{32,28},{36,32}... | collective-permute-start | bytes 1572872 | tf_op jit(solution)/shard_map/ppermute | solution.py:98
  21.0 5.1 %collective-permute-done = f32[8,16,8,128]{3,2,1,0:T(8,128)S(1)} collective-permute-done((f32[8,16,8,128]{3,2,1,0:T(8,128)}, f32[8,16,8,128]{3,2,1,0:T(8,128)S(1)}, u32[]{:S(2)}, u32[]{:S(2)}) %collective-permute-start) | collective-permute-done | bytes 524320 | tf_op jit(solution)/shard_map/ppermute | solution.py:97
  26.2 1.9 %collective-permute-done.1 = f32[8,16,8,128]{3,2,1,0:T(8,128)S(1)} collective-permute-done((f32[8,16,8,128]{3,2,1,0:T(8,128)}, f32[8,16,8,128]{3,2,1,0:T(8,128)S(1)}, u32[]{:S(2)}, u32[]{:S(2)}) %collective-permute-start.1) | collective-permute-done | bytes 524320 | tf_op jit(solution)/shard_map/ppermute | solution.py:98
  28.0 1.4 %maximum_add_fusion = f32[8,32,8,128]{3,2,1,0:T(8,128)S(1)} fusion(f32[8,32,8,128]{3,2,1,0:T(8,128)} %get-tuple-element.8, f32[8,16,8,128]{3,2,1,0:T(8,128)S(1)} %collective-permute-done.1, f32[8,16,8,128]{3,2,1,0:T(8,128)S(1)} %collective-permute-done), kind=kLoop, calls=%fused_computation | loop fusion | flops 524288 | bytes 3145728 | tf_op jit(solution)/shard_map/add | solution.py:101
  29.4 0.2 copy.6
  29.6 15.2 %all_to_all.5 = f32[4,8,2,32,128]{4,3,2,1,0:T(8,128)S(1)} all-to-all(f32[4,8,2,32,128]{4,3,2,1,0:T(8,128)S(1)} %bitcast.8), channel_id=1, replica_groups=mesh['tile'=128,'epoch'=4] {'epoch'}, dimensions={0} | all-to-all | bytes 2097152 | tf_op jit(solution)/shard_map/all_to_all | solution.py:103
  44.8 0.7 %fusion.3 = f32[32,128]{1,0:T(8,128)} fusion(f32[4,8,2,32,128]{4,3,2,1,0:T(8,128)S(1)} %all_to_all.5), kind=kLoop, calls=%fused_computation.6 | loop fusion | flops 258048 | bytes 1064960 | tf_op jit(solution)/shard_map/max | solution.py:112
Async XLA Ops:
  8.0 18.2 %collective-permute-start = (f32[8,16,8,128]{3,2,1,0:T(8,128)}, f32[8,16,8,128]{3,2,1,0:T(8,128)S(1)}, u32[]{:S(2)}, u32[]{:S(2)}) collective-permute-start(f32[8,16,8,128]{3,2,1,0:T(8,128)} %get-tuple-element.9), channel_id=1, source_target_pairs={{0,4},{4,8},{8,12},{12,16},{16,20},{20,24},{24,28},{28,32},{32,36}... | collective-permute-start | bytes 1572872 | tf_op jit(solution)/shard_map/ppermute | solution.py:97
  9.9 18.1 %collective-permute-start.1 = (f32[8,16,8,128]{3,2,1,0:T(8,128)}, f32[8,16,8,128]{3,2,1,0:T(8,128)S(1)}, u32[]{:S(2)}, u32[]{:S(2)}) collective-permute-start(f32[8,16,8,128]{3,2,1,0:T(8,128)} %get-tuple-element.10), channel_id=1, source_target_pairs={{4,0},{8,4},{12,8},{16,12},{20,16},{24,20},{28,24},{32,28},{36,32}... | collective-permute-start | bytes 1572872 | tf_op jit(solution)/shard_map/ppermute | solution.py:98

commit v15 on v14

--- a/solution.py
+++ b/solution.py
@@ -97,8 +97,7 @@
     from_above = lax.ppermute(bottom, "tile", forward)
     from_below = lax.ppermute(top, "tile", backward)
     vels = own.shape[0]
-    middle = jnp.zeros((vels, rows - 2 * HALO) + own.shape[2:], jnp.float32)
-    part = own + jnp.concatenate([from_above, middle, from_below], axis=1)
+    part = own.at[:, :HALO].add(from_above).at[:, rows - HALO :].add(from_below)
     part = part.reshape(vels, rows, 2, blocks, LANES).transpose(3, 0, 2, 1, 4)
     gathered = lax.all_to_all(part, "epoch", 0, 0, tiled=True)
     best = None

time: 45.8 us -> 47.7 us (1.041)
  other arithmetic: 2.08 us -> 4.56 us
  waiting for transfers between devices: 6.99 us -> 5.14 us
  local copies, waits for them, and re-layouts: 1.57 us -> 2.8 us
    scatter-add x0 -> x2, other arithmetic: none -> 3.86 us  [per_device(): part = own.at[:, :HALO].add(from_above).at[:, rows - HALO:].add(from_below)]
    ppermute x1, waiting for transfers between devices: 1.86 us -> 0.01 us  [per_device(): from_below = lax.ppermute(top, 'tile', backward)]
    add x1 -> x0, other arithmetic: 1.39 us -> none  [per_device(): part = own + jnp.concatenate([from_above, middle, from_below], axis=1)]
    reshape x1, local copies, waits for them, and re-layouts: 0.2 us -> 1.43 us  [per_device(): part = part.reshape(vels, rows, 2, blocks, LANES).transpose(3, 0, 2, 1, 4)]
  transfers between devices with their start and end apart: 2 -> 2, of which waited for: 2 -> 1; matrix products, arithmetic and copies ran while one was open for 0% -> 4% of each run, Pallas kernels for 0% -> 0%
where the time goes in v15:
time: 47.7 us; the launch traced here: 47.3 us
  blocking collectives  15.2 us (32%)
  starting transfers between devices  13 us (27%)
  Pallas kernels  6.65 us (14%)
  waiting for transfers between devices  5.14 us (11%)
  other arithmetic  4.56 us (10%)
  local copies, waits for them, and re-layouts  2.8 us (6%)
    all_to_all x1, blocking collectives, per_device(): gathered = lax.all_to_all(part, 'epoch', 0, 0, tiled=True)  15.2 us
    ppermute x1, starting transfers between devices, per_device(): from_below = lax.ppermute(top, 'tile', backward)  11.1 us
    pallas_call x1, Pallas kernels, partial_stacks(): pl.pallas_call(stack_kernel, out_shape=(jax.ShapeDtypeStruct((vels, rows,...  6.65 us
    ppermute x1, waiting for transfers between devices, per_device(): from_above = lax.ppermute(bottom, 'tile', forward)  5.13 us
    scatter-add x2, other arithmetic, per_device(): part = own.at[:, :HALO].add(from_above).at[:, rows - HALO:].add(from_below)  3.86 us
    ppermute x1, starting transfers between devices, per_device(): from_above = lax.ppermute(bottom, 'tile', forward)  1.91 us
    reshape x1, local copies, waits for them, and re-layouts, per_device(): part = part.reshape(vels, rows, 2, blocks, LANES).transpose(3, 0, 2, 1, 4)  1.43 us
    reshape x1, local copies, waits for them, and re-layouts, partial_stacks(): jnp.swapaxes(shifts, 1, 2).reshape(-1)  1.37 us
  transfers between devices with their start and end apart: 2, of which 1 were waited for; matrix products, arithmetic and copies ran while one was open for 4% of the time, Pallas kernels for 0%

profile of v15, /device:TPU:6, one launch (start us, length us, event | category | flops | bytes accessed | tf_op | source)
XLA Modules:
  0.0 47.3 jit_solution(2053531741223626157)
XLA Ops:
  0.0 1.4 %reshape.132.sh_ref = s32[768]{0:T(1024)} reshape(s32[8,2,48]{2,1,0:T(2,128)} %bitcast.9) | data formatting | bytes 6144 | tf_op jit(solution)/shard_map/reshape | solution.py:87
  1.4 6.7 %shard_map.37 = (f32[8,32,8,128]{3,2,1,0:T(8,128)}, f32[8,16,8,128]{3,2,1,0:T(8,128)}, f32[8,16,8,128]{3,2,1,0:T(8,128)}) custom-call(s32[768]{0:T(1024)} %reshape.132.sh_ref, f32[12,32,512]{2,1,0:T(8,128)} %psi_ref.1, f32[12,32,512]{2,1,0:T(8,128)} %phi_ref.1), custom_call_target="tpu_custom_call" | custom-call | flops 6291456 | bytes 3670016 | tf_op jit(solution)/shard_map/pallas_call | solution.py:73
  8.0 1.9 %collective-permute-start = (f32[8,16,8,128]{3,2,1,0:T(8,128)}, f32[8,16,8,128]{3,2,1,0:T(8,128)S(1)}, u32[]{:S(2)}, u32[]{:S(2)}) collective-permute-start(f32[8,16,8,128]{3,2,1,0:T(8,128)} %get-tuple-element.33), channel_id=1, source_target_pairs={{0,4},{4,8},{8,12},{12,16},{16,20},{20,24},{24,28},{28,32},{32,36}... | collective-permute-start | bytes 1572872 | tf_op jit(solution)/shard_map/ppermute | solution.py:97
  9.9 11.1 %collective-permute-start.1 = (f32[8,16,8,128]{3,2,1,0:T(8,128)}, f32[8,16,8,128]{3,2,1,0:T(8,128)S(1)}, u32[]{:S(2)}, u32[]{:S(2)}) collective-permute-start(f32[8,16,8,128]{3,2,1,0:T(8,128)} %get-tuple-element.34), channel_id=1, source_target_pairs={{4,0},{8,4},{12,8},{16,12},{20,16},{24,20},{28,24},{32,28},{36,32}... | collective-permute-start | bytes 1572872 | tf_op jit(solution)/shard_map/ppermute | solution.py:98
  21.1 5.1 %collective-permute-done = f32[8,16,8,128]{3,2,1,0:T(8,128)S(1)} collective-permute-done((f32[8,16,8,128]{3,2,1,0:T(8,128)}, f32[8,16,8,128]{3,2,1,0:T(8,128)S(1)}, u32[]{:S(2)}, u32[]{:S(2)}) %collective-permute-start) | collective-permute-done | bytes 524320 | tf_op jit(solution)/shard_map/ppermute | solution.py:97
  26.2 1.9 %add_dynamic-update-slice_fusion = f32[8,32,8,128]{3,2,1,0:T(8,128)} fusion(f32[8,32,8,128]{3,2,1,0:T(8,128)} %get-tuple-element.32, f32[8,16,8,128]{3,2,1,0:T(8,128)S(1)} %collective-permute-done), kind=kLoop, calls=%fused_computation.3 | loop fusion | flops 131072 | bytes 1572864 | tf_op jit(solution)/shard_map/scatter-add | solution.py:100
  28.1 0.0 collective-permute-done.1
  28.1 1.9 %fusion = f32[8,32,8,128]{3,2,1,0:T(8,128)} fusion(f32[8,32,8,128]{3,2,1,0:T(8,128)} %add_dynamic-update-slice_fusion, f32[8,16,8,128]{3,2,1,0:T(8,128)S(1)} %collective-permute-done.1), kind=kLoop, calls=%fused_computation.2 | loop fusion | flops 131072 | bytes 1572864 | tf_op jit(solution)/shard_map/scatter-add | solution.py:100
  30.1 1.4 %copy.6 = f32[8,32,2,4,128]{4,1,2,0,3:T(8,128)S(1)} copy(f32[8,32,2,4,128]{4,3,2,1,0:T(4,128)} %bitcast.7) | data formatting | bytes 2097152 | tf_op jit(solution)/shard_map/reshape | solution.py:101
  31.5 15.2 %all_to_all.5 = f32[4,8,2,32,128]{4,3,2,1,0:T(8,128)S(1)} all-to-all(f32[4,8,2,32,128]{4,3,2,1,0:T(8,128)S(1)} %bitcast.8), channel_id=1, replica_groups=mesh['tile'=128,'epoch'=4] {'epoch'}, dimensions={0} | all-to-all | bytes 2097152 | tf_op jit(solution)/shard_map/all_to_all | solution.py:102
  46.7 0.7 %fusion.4 = f32[32,128]{1,0:T(8,128)} fusion(f32[4,8,2,32,128]{4,3,2,1,0:T(8,128)S(1)} %all_to_all.5), kind=kLoop, calls=%fused_computation.8 | loop fusion | flops 258048 | bytes 1064960 | tf_op jit(solution)/shard_map/max | solution.py:111
Async XLA Ops:
  8.0 18.2 %collective-permute-start = (f32[8,16,8,128]{3,2,1,0:T(8,128)}, f32[8,16,8,128]{3,2,1,0:T(8,128)S(1)}, u32[]{:S(2)}, u32[]{:S(2)}) collective-permute-start(f32[8,16,8,128]{3,2,1,0:T(8,128)} %get-tuple-element.33), channel_id=1, source_target_pairs={{0,4},{4,8},{8,12},{12,16},{16,20},{20,24},{24,28},{28,32},{32,36}... | collective-permute-start | bytes 1572872 | tf_op jit(solution)/shard_map/ppermute | solution.py:97
  9.9 18.2 %collective-permute-start.1 = (f32[8,16,8,128]{3,2,1,0:T(8,128)}, f32[8,16,8,128]{3,2,1,0:T(8,128)S(1)}, u32[]{:S(2)}, u32[]{:S(2)}) collective-permute-start(f32[8,16,8,128]{3,2,1,0:T(8,128)} %get-tuple-element.34), channel_id=1, source_target_pairs={{4,0},{8,4},{12,8},{16,12},{20,16},{24,20},{28,24},{32,28},{36,32}... | collective-permute-start | bytes 1572872 | tf_op jit(solution)/shard_map/ppermute | solution.py:98

commit v16 on v14

--- a/solution.py
+++ b/solution.py
@@ -7,7 +7,7 @@
 
 HALO = 16
 LANES = 128
-CHUNK = 8
+CHUNK = 16
 
 
 def stack_kernel(sh_ref, psi_ref, phi_ref, own_ref, top_ref, bottom_ref, acc_ref, x_ref):

time: 45.8 us -> 45.8 us (level)
  no operation moved by 1% of the time
where the time goes in v16:
time: 45.8 us; the launch traced here: 45.5 us
  blocking collectives  15.2 us (33%)
  starting transfers between devices  13 us (28%)
  waiting for transfers between devices  6.99 us (15%)
  Pallas kernels  6.66 us (15%)
  other arithmetic  2.08 us (5%)
  local copies, waits for them, and re-layouts  1.57 us (3%)
    all_to_all x1, blocking collectives, per_device(): gathered = lax.all_to_all(part, 'epoch', 0, 0, tiled=True)  15.2 us
    ppermute x1, starting transfers between devices, per_device(): from_below = lax.ppermute(top, 'tile', backward)  11.1 us
    pallas_call x1, Pallas kernels, partial_stacks(): pl.pallas_call(stack_kernel, out_shape=(jax.ShapeDtypeStruct((vels, rows,...  6.66 us
    ppermute x1, waiting for transfers between devices, per_device(): from_above = lax.ppermute(bottom, 'tile', forward)  5.13 us
    ppermute x1, starting transfers between devices, per_device(): from_above = lax.ppermute(bottom, 'tile', forward)  1.91 us
    ppermute x1, waiting for transfers between devices, per_device(): from_below = lax.ppermute(top, 'tile', backward)  1.86 us
    add x1, other arithmetic, per_device(): part = own + jnp.concatenate([from_above, middle, from_below], axis=1)  1.39 us
    reshape x1, local copies, waits for them, and re-layouts, partial_stacks(): jnp.swapaxes(shifts, 1, 2).reshape(-1)  1.37 us
  transfers between devices with their start and end apart: 2, of which 2 were waited for; matrix products, arithmetic and copies ran while one was open for 0% of the time, Pallas kernels for 0%

profile of v16, /device:TPU:6, one launch (start us, length us, event | category | flops | bytes accessed | tf_op | source)
XLA Modules:
  0.0 45.5 jit_solution(4883593159332571985)
XLA Ops:
  0.0 1.4 %reshape.62.sh_ref = s32[768]{0:T(1024)} reshape(s32[8,2,48]{2,1,0:T(2,128)} %bitcast.9) | data formatting | bytes 6144 | tf_op jit(solution)/shard_map/reshape | solution.py:87
  1.4 6.7 %shard_map.37 = (f32[8,32,8,128]{3,2,1,0:T(8,128)}, f32[8,16,8,128]{3,2,1,0:T(8,128)}, f32[8,16,8,128]{3,2,1,0:T(8,128)}) custom-call(s32[768]{0:T(1024)} %reshape.62.sh_ref, f32[12,32,512]{2,1,0:T(8,128)} %psi_ref.1, f32[12,32,512]{2,1,0:T(8,128)} %phi_ref.1), custom_call_target="tpu_custom_call" | custom-call | flops 6291456 | bytes 3670016 | tf_op jit(solution)/shard_map/pallas_call | solution.py:73
  8.0 1.9 %collective-permute-start = (f32[8,16,8,128]{3,2,1,0:T(8,128)}, f32[8,16,8,128]{3,2,1,0:T(8,128)S(1)}, u32[]{:S(2)}, u32[]{:S(2)}) collective-permute-start(f32[8,16,8,128]{3,2,1,0:T(8,128)} %get-tuple-element.9), channel_id=1, source_target_pairs={{0,4},{4,8},{8,12},{12,16},{16,20},{20,24},{24,28},{28,32},{32,36}... | collective-permute-start | bytes 1572872 | tf_op jit(solution)/shard_map/ppermute | solution.py:97
  9.9 11.1 %collective-permute-start.1 = (f32[8,16,8,128]{3,2,1,0:T(8,128)}, f32[8,16,8,128]{3,2,1,0:T(8,128)S(1)}, u32[]{:S(2)}, u32[]{:S(2)}) collective-permute-start(f32[8,16,8,128]{3,2,1,0:T(8,128)} %get-tuple-element.10), channel_id=1, source_target_pairs={{4,0},{8,4},{12,8},{16,12},{20,16},{24,20},{28,24},{32,28},{36,32}... | collective-permute-start | bytes 1572872 | tf_op jit(solution)/shard_map/ppermute | solution.py:98
  21.1 5.1 %collective-permute-done = f32[8,16,8,128]{3,2,1,0:T(8,128)S(1)} collective-permute-done((f32[8,16,8,128]{3,2,1,0:T(8,128)}, f32[8,16,8,128]{3,2,1,0:T(8,128)S(1)}, u32[]{:S(2)}, u32[]{:S(2)}) %collective-permute-start) | collective-permute-done | bytes 524320 | tf_op jit(solution)/shard_map/ppermute | solution.py:97
  26.2 1.9 %collective-permute-done.1 = f32[8,16,8,128]{3,2,1,0:T(8,128)S(1)} collective-permute-done((f32[8,16,8,128]{3,2,1,0:T(8,128)}, f32[8,16,8,128]{3,2,1,0:T(8,128)S(1)}, u32[]{:S(2)}, u32[]{:S(2)}) %collective-permute-start.1) | collective-permute-done | bytes 524320 | tf_op jit(solution)/shard_map/ppermute | solution.py:98
  28.1 1.4 %maximum_add_fusion = f32[8,32,8,128]{3,2,1,0:T(8,128)S(1)} fusion(f32[8,32,8,128]{3,2,1,0:T(8,128)} %get-tuple-element.8, f32[8,16,8,128]{3,2,1,0:T(8,128)S(1)} %collective-permute-done.1, f32[8,16,8,128]{3,2,1,0:T(8,128)S(1)} %collective-permute-done), kind=kLoop, calls=%fused_computation | loop fusion | flops 524288 | bytes 3145728 | tf_op jit(solution)/shard_map/add | solution.py:101
  29.4 0.2 copy.6
  29.7 15.2 %all_to_all.5 = f32[4,8,2,32,128]{4,3,2,1,0:T(8,128)S(1)} all-to-all(f32[4,8,2,32,128]{4,3,2,1,0:T(8,128)S(1)} %bitcast.8), channel_id=1, replica_groups=mesh['tile'=128,'epoch'=4] {'epoch'}, dimensions={0} | all-to-all | bytes 2097152 | tf_op jit(solution)/shard_map/all_to_all | solution.py:103
  44.8 0.7 %fusion.3 = f32[32,128]{1,0:T(8,128)} fusion(f32[4,8,2,32,128]{4,3,2,1,0:T(8,128)S(1)} %all_to_all.5), kind=kLoop, calls=%fused_computation.6 | loop fusion | flops 258048 | bytes 1064960 | tf_op jit(solution)/shard_map/max | solution.py:112
Async XLA Ops:
  8.0 18.2 %collective-permute-start = (f32[8,16,8,128]{3,2,1,0:T(8,128)}, f32[8,16,8,128]{3,2,1,0:T(8,128)S(1)}, u32[]{:S(2)}, u32[]{:S(2)}) collective-permute-start(f32[8,16,8,128]{3,2,1,0:T(8,128)} %get-tuple-element.9), channel_id=1, source_target_pairs={{0,4},{4,8},{8,12},{12,16},{16,20},{20,24},{24,28},{28,32},{32,36}... | collective-permute-start | bytes 1572872 | tf_op jit(solution)/shard_map/ppermute | solution.py:97
  9.9 18.1 %collective-permute-start.1 = (f32[8,16,8,128]{3,2,1,0:T(8,128)}, f32[8,16,8,128]{3,2,1,0:T(8,128)S(1)}, u32[]{:S(2)}, u32[]{:S(2)}) collective-permute-start(f32[8,16,8,128]{3,2,1,0:T(8,128)} %get-tuple-element.10), channel_id=1, source_target_pairs={{4,0},{8,4},{12,8},{16,12},{20,16},{24,20},{28,24},{32,28},{36,32}... | collective-permute-start | bytes 1572872 | tf_op jit(solution)/shard_map/ppermute | solution.py:98

commit v17 on v14

--- a/solution.py
+++ b/solution.py
@@ -57,7 +57,7 @@
             add_epoch(v, e)
         return carry
 
-    lax.fori_loop(0, epochs, body, 0, unroll=4)
+    lax.fori_loop(0, epochs, body, 0, unroll=True)
     for v in range(vels):
         top_ref[v] = acc_ref[v, :HALO]
         own_ref[v] = acc_ref[v, HALO : HALO + rows]

time: 45.8 us -> 45.6 us (level)
  no operation moved by 1% of the time
where the time goes in v17:
time: 45.6 us; the launch traced here: 45.3 us
  blocking collectives  15.2 us (33%)
  starting transfers between devices  13 us (29%)
  waiting for transfers between devices  6.99 us (15%)
  Pallas kernels  6.44 us (14%)
  other arithmetic  2.08 us (5%)
  local copies, waits for them, and re-layouts  1.57 us (3%)
    all_to_all x1, blocking collectives, per_device(): gathered = lax.all_to_all(part, 'epoch', 0, 0, tiled=True)  15.2 us
    ppermute x1, starting transfers between devices, per_device(): from_below = lax.ppermute(top, 'tile', backward)  11.1 us
    pallas_call x1, Pallas kernels, partial_stacks(): pl.pallas_call(stack_kernel, out_shape=(jax.ShapeDtypeStruct((vels, rows,...  6.44 us
    ppermute x1, waiting for transfers between devices, per_device(): from_above = lax.ppermute(bottom, 'tile', forward)  5.13 us
    ppermute x1, starting transfers between devices, per_device(): from_above = lax.ppermute(bottom, 'tile', forward)  1.91 us
    ppermute x1, waiting for transfers between devices, per_device(): from_below = lax.ppermute(top, 'tile', backward)  1.86 us
    add x1, other arithmetic, per_device(): part = own + jnp.concatenate([from_above, middle, from_below], axis=1)  1.39 us
    reshape x1, local copies, waits for them, and re-layouts, partial_stacks(): jnp.swapaxes(shifts, 1, 2).reshape(-1)  1.37 us
  transfers between devices with their start and end apart: 2, of which 2 were waited for; matrix products, arithmetic and copies ran while one was open for 0% of the time, Pallas kernels for 0%

profile of v17, /device:TPU:6, one launch (start us, length us, event | category | flops | bytes accessed | tf_op | source)
XLA Modules:
  0.0 45.3 jit_solution(13581729241994439610)
XLA Ops:
  0.0 1.4 %reshape.62.sh_ref = s32[768]{0:T(1024)} reshape(s32[8,2,48]{2,1,0:T(2,128)} %bitcast.9) | data formatting | bytes 6144 | tf_op jit(solution)/shard_map/reshape | solution.py:87
  1.4 6.4 %shard_map.37 = (f32[8,32,8,128]{3,2,1,0:T(8,128)}, f32[8,16,8,128]{3,2,1,0:T(8,128)}, f32[8,16,8,128]{3,2,1,0:T(8,128)}) custom-call(s32[768]{0:T(1024)} %reshape.62.sh_ref, f32[12,32,512]{2,1,0:T(8,128)} %psi_ref.1, f32[12,32,512]{2,1,0:T(8,128)} %phi_ref.1), custom_call_target="tpu_custom_call" | custom-call | flops 6291456 | bytes 3670016 | tf_op jit(solution)/shard_map/pallas_call | solution.py:73
  7.8 1.9 %collective-permute-start = (f32[8,16,8,128]{3,2,1,0:T(8,128)}, f32[8,16,8,128]{3,2,1,0:T(8,128)S(1)}, u32[]{:S(2)}, u32[]{:S(2)}) collective-permute-start(f32[8,16,8,128]{3,2,1,0:T(8,128)} %get-tuple-element.9), channel_id=1, source_target_pairs={{0,4},{4,8},{8,12},{12,16},{16,20},{20,24},{24,28},{28,32},{32,36}... | collective-permute-start | bytes 1572872 | tf_op jit(solution)/shard_map/ppermute | solution.py:97
  9.7 11.1 %collective-permute-start.1 = (f32[8,16,8,128]{3,2,1,0:T(8,128)}, f32[8,16,8,128]{3,2,1,0:T(8,128)S(1)}, u32[]{:S(2)}, u32[]{:S(2)}) collective-permute-start(f32[8,16,8,128]{3,2,1,0:T(8,128)} %get-tuple-element.10), channel_id=1, source_target_pairs={{4,0},{8,4},{12,8},{16,12},{20,16},{24,20},{28,24},{32,28},{36,32}... | collective-permute-start | bytes 1572872 | tf_op jit(solution)/shard_map/ppermute | solution.py:98
  20.8 5.1 %collective-permute-done = f32[8,16,8,128]{3,2,1,0:T(8,128)S(1)} collective-permute-done((f32[8,16,8,128]{3,2,1,0:T(8,128)}, f32[8,16,8,128]{3,2,1,0:T(8,128)S(1)}, u32[]{:S(2)}, u32[]{:S(2)}) %collective-permute-start) | collective-permute-done | bytes 524320 | tf_op jit(solution)/shard_map/ppermute | solution.py:97
  26.0 1.9 %collective-permute-done.1 = f32[8,16,8,128]{3,2,1,0:T(8,128)S(1)} collective-permute-done((f32[8,16,8,128]{3,2,1,0:T(8,128)}, f32[8,16,8,128]{3,2,1,0:T(8,128)S(1)}, u32[]{:S(2)}, u32[]{:S(2)}) %collective-permute-start.1) | collective-permute-done | bytes 524320 | tf_op jit(solution)/shard_map/ppermute | solution.py:98
  27.8 1.4 %maximum_add_fusion = f32[8,32,8,128]{3,2,1,0:T(8,128)S(1)} fusion(f32[8,32,8,128]{3,2,1,0:T(8,128)} %get-tuple-element.8, f32[8,16,8,128]{3,2,1,0:T(8,128)S(1)} %collective-permute-done.1, f32[8,16,8,128]{3,2,1,0:T(8,128)S(1)} %collective-permute-done), kind=kLoop, calls=%fused_computation | loop fusion | flops 524288 | bytes 3145728 | tf_op jit(solution)/shard_map/add | solution.py:101
  29.2 0.2 copy.6
  29.4 15.2 %all_to_all.5 = f32[4,8,2,32,128]{4,3,2,1,0:T(8,128)S(1)} all-to-all(f32[4,8,2,32,128]{4,3,2,1,0:T(8,128)S(1)} %bitcast.8), channel_id=1, replica_groups=mesh['tile'=128,'epoch'=4] {'epoch'}, dimensions={0} | all-to-all | bytes 2097152 | tf_op jit(solution)/shard_map/all_to_all | solution.py:103
  44.6 0.7 %fusion.3 = f32[32,128]{1,0:T(8,128)} fusion(f32[4,8,2,32,128]{4,3,2,1,0:T(8,128)S(1)} %all_to_all.5), kind=kLoop, calls=%fused_computation.6 | loop fusion | flops 258048 | bytes 1064960 | tf_op jit(solution)/shard_map/max | solution.py:112
Async XLA Ops:
  7.8 18.2 %collective-permute-start = (f32[8,16,8,128]{3,2,1,0:T(8,128)}, f32[8,16,8,128]{3,2,1,0:T(8,128)S(1)}, u32[]{:S(2)}, u32[]{:S(2)}) collective-permute-start(f32[8,16,8,128]{3,2,1,0:T(8,128)} %get-tuple-element.9), channel_id=1, source_target_pairs={{0,4},{4,8},{8,12},{12,16},{16,20},{20,24},{24,28},{28,32},{32,36}... | collective-permute-start | bytes 1572872 | tf_op jit(solution)/shard_map/ppermute | solution.py:97
  9.7 18.1 %collective-permute-start.1 = (f32[8,16,8,128]{3,2,1,0:T(8,128)}, f32[8,16,8,128]{3,2,1,0:T(8,128)S(1)}, u32[]{:S(2)}, u32[]{:S(2)}) collective-permute-start(f32[8,16,8,128]{3,2,1,0:T(8,128)} %get-tuple-element.10), channel_id=1, source_target_pairs={{4,0},{8,4},{12,8},{16,12},{20,16},{24,20},{28,24},{32,28},{36,32}... | collective-permute-start | bytes 1572872 | tf_op jit(solution)/shard_map/ppermute | solution.py:98

commit v18 on v17

--- a/solution.py
+++ b/solution.py
@@ -25,7 +25,7 @@
             x_ref[e, here] = jnp.swapaxes(jnp.stack(pieces, axis=0), 0, 1)
         return carry
 
-    lax.fori_loop(0, epochs, pack, 0)
+    lax.fori_loop(0, epochs, pack, 0, unroll=True)
     vels = acc_ref.shape[0]
     total = sh_ref.shape[0] // (2 * vels)
     first = lax.axis_index("epoch") * epochs

time: 45.6 us -> 45.3 us (level)
  no operation moved by 1% of the time
where the time goes in v18:
time: 45.3 us; the launch traced here: 45 us
  blocking collectives  15.2 us (34%)
  starting transfers between devices  13 us (29%)
  waiting for transfers between devices  6.99 us (15%)
  Pallas kernels  6.17 us (14%)
  other arithmetic  2.08 us (5%)
  local copies, waits for them, and re-layouts  1.57 us (3%)
    all_to_all x1, blocking collectives, per_device(): gathered = lax.all_to_all(part, 'epoch', 0, 0, tiled=True)  15.2 us
    ppermute x1, starting transfers between devices, per_device(): from_below = lax.ppermute(top, 'tile', backward)  11.1 us
    pallas_call x1, Pallas kernels, partial_stacks(): pl.pallas_call(stack_kernel, out_shape=(jax.ShapeDtypeStruct((vels, rows,...  6.17 us
    ppermute x1, waiting for transfers between devices, per_device(): from_above = lax.ppermute(bottom, 'tile', forward)  5.13 us
    ppermute x1, starting transfers between devices, per_device(): from_above = lax.ppermute(bottom, 'tile', forward)  1.91 us
    ppermute x1, waiting for transfers between devices, per_device(): from_below = lax.ppermute(top, 'tile', backward)  1.86 us
    add x1, other arithmetic, per_device(): part = own + jnp.concatenate([from_above, middle, from_below], axis=1)  1.39 us
    reshape x1, local copies, waits for them, and re-layouts, partial_stacks(): jnp.swapaxes(shifts, 1, 2).reshape(-1)  1.37 us
  transfers between devices with their start and end apart: 2, of which 2 were waited for; matrix products, arithmetic and copies ran while one was open for 0% of the time, Pallas kernels for 0%

profile of v18, /device:TPU:6, one launch (start us, length us, event | category | flops | bytes accessed | tf_op | source)
XLA Modules:
  0.0 45.0 jit_solution(92137519849789745)
XLA Ops:
  0.0 1.4 %reshape.62.sh_ref = s32[768]{0:T(1024)} reshape(s32[8,2,48]{2,1,0:T(2,128)} %bitcast.9) | data formatting | bytes 6144 | tf_op jit(solution)/shard_map/reshape | solution.py:87
  1.4 6.2 %shard_map.37 = (f32[8,32,8,128]{3,2,1,0:T(8,128)}, f32[8,16,8,128]{3,2,1,0:T(8,128)}, f32[8,16,8,128]{3,2,1,0:T(8,128)}) custom-call(s32[768]{0:T(1024)} %reshape.62.sh_ref, f32[12,32,512]{2,1,0:T(8,128)} %psi_ref.1, f32[12,32,512]{2,1,0:T(8,128)} %phi_ref.1), custom_call_target="tpu_custom_call" | custom-call | flops 6291456 | bytes 3670016 | tf_op jit(solution)/shard_map/pallas_call | solution.py:73
  7.5 1.9 %collective-permute-start = (f32[8,16,8,128]{3,2,1,0:T(8,128)}, f32[8,16,8,128]{3,2,1,0:T(8,128)S(1)}, u32[]{:S(2)}, u32[]{:S(2)}) collective-permute-start(f32[8,16,8,128]{3,2,1,0:T(8,128)} %get-tuple-element.9), channel_id=1, source_target_pairs={{0,4},{4,8},{8,12},{12,16},{16,20},{20,24},{24,28},{28,32},{32,36}... | collective-permute-start | bytes 1572872 | tf_op jit(solution)/shard_map/ppermute | solution.py:97
  9.5 11.1 %collective-permute-start.1 = (f32[8,16,8,128]{3,2,1,0:T(8,128)}, f32[8,16,8,128]{3,2,1,0:T(8,128)S(1)}, u32[]{:S(2)}, u32[]{:S(2)}) collective-permute-start(f32[8,16,8,128]{3,2,1,0:T(8,128)} %get-tuple-element.10), channel_id=1, source_target_pairs={{4,0},{8,4},{12,8},{16,12},{20,16},{24,20},{28,24},{32,28},{36,32}... | collective-permute-start | bytes 1572872 | tf_op jit(solution)/shard_map/ppermute | solution.py:98
  20.6 5.1 %collective-permute-done = f32[8,16,8,128]{3,2,1,0:T(8,128)S(1)} collective-permute-done((f32[8,16,8,128]{3,2,1,0:T(8,128)}, f32[8,16,8,128]{3,2,1,0:T(8,128)S(1)}, u32[]{:S(2)}, u32[]{:S(2)}) %collective-permute-start) | collective-permute-done | bytes 524320 | tf_op jit(solution)/shard_map/ppermute | solution.py:97
  25.7 1.9 %collective-permute-done.1 = f32[8,16,8,128]{3,2,1,0:T(8,128)S(1)} collective-permute-done((f32[8,16,8,128]{3,2,1,0:T(8,128)}, f32[8,16,8,128]{3,2,1,0:T(8,128)S(1)}, u32[]{:S(2)}, u32[]{:S(2)}) %collective-permute-start.1) | collective-permute-done | bytes 524320 | tf_op jit(solution)/shard_map/ppermute | solution.py:98
  27.6 1.4 %maximum_add_fusion = f32[8,32,8,128]{3,2,1,0:T(8,128)S(1)} fusion(f32[8,32,8,128]{3,2,1,0:T(8,128)} %get-tuple-element.8, f32[8,16,8,128]{3,2,1,0:T(8,128)S(1)} %collective-permute-done.1, f32[8,16,8,128]{3,2,1,0:T(8,128)S(1)} %collective-permute-done), kind=kLoop, calls=%fused_computation | loop fusion | flops 524288 | bytes 3145728 | tf_op jit(solution)/shard_map/add | solution.py:101
  29.0 0.2 copy.6
  29.2 15.2 %all_to_all.5 = f32[4,8,2,32,128]{4,3,2,1,0:T(8,128)S(1)} all-to-all(f32[4,8,2,32,128]{4,3,2,1,0:T(8,128)S(1)} %bitcast.8), channel_id=1, replica_groups=mesh['tile'=128,'epoch'=4] {'epoch'}, dimensions={0} | all-to-all | bytes 2097152 | tf_op jit(solution)/shard_map/all_to_all | solution.py:103
  44.3 0.7 %fusion.3 = f32[32,128]{1,0:T(8,128)} fusion(f32[4,8,2,32,128]{4,3,2,1,0:T(8,128)S(1)} %all_to_all.5), kind=kLoop, calls=%fused_computation.6 | loop fusion | flops 258048 | bytes 1064960 | tf_op jit(solution)/shard_map/max | solution.py:112
Async XLA Ops:
  7.5 18.2 %collective-permute-start = (f32[8,16,8,128]{3,2,1,0:T(8,128)}, f32[8,16,8,128]{3,2,1,0:T(8,128)S(1)}, u32[]{:S(2)}, u32[]{:S(2)}) collective-permute-start(f32[8,16,8,128]{3,2,1,0:T(8,128)} %get-tuple-element.9), channel_id=1, source_target_pairs={{0,4},{4,8},{8,12},{12,16},{16,20},{20,24},{24,28},{28,32},{32,36}... | collective-permute-start | bytes 1572872 | tf_op jit(solution)/shard_map/ppermute | solution.py:97
  9.5 18.1 %collective-permute-start.1 = (f32[8,16,8,128]{3,2,1,0:T(8,128)}, f32[8,16,8,128]{3,2,1,0:T(8,128)S(1)}, u32[]{:S(2)}, u32[]{:S(2)}) collective-permute-start(f32[8,16,8,128]{3,2,1,0:T(8,128)} %get-tuple-element.10), channel_id=1, source_target_pairs={{4,0},{8,4},{12,8},{16,12},{20,16},{24,20},{28,24},{32,28},{36,32}... | collective-permute-start | bytes 1572872 | tf_op jit(solution)/shard_map/ppermute | solution.py:98
